TPU v7x, 256 devices: a whole 4x4x8 slice. The times are simulated.
256 devices in a mesh: blk: 64 (over z, x, core), lane: 4 (over y).
Axes of the slice: x: 4, y: 4, z: 8, core: 2. Of those that a mesh axis runs over, the one named last changes fastest.
Arguments:
- tangent_blocks: bfloat16 [8192, 64, 512], P('blk', None, 'lane'), may hold values from -0.75 to 0.75
- tangent_columns: int32 [8192, 8], P('blk', 'lane'), may hold values from 0 to 8191, as said below
- prolong_blocks: bfloat16 [8192, 24, 512], P('blk'), may hold values from -0.375 to 0.375
- prolong_columns: int32 [8192, 8], P('blk'), may hold values from 0 to 255, as said below
Outputs:
- coarse_band: float32 [256, 24, 672], P(('blk', 'lane'))
Inputs may be any that keep to these rules, and one draw needn't show every extreme that they name: tangent_columns[i, 0] = i; every entry of row i is a fine block row of the slab i // 128 or one of the 32 rows on either side of that slab, counted cyclically over the 8192 rows. The 8 entries of a row are distinct; prolong_columns[i, 0] = (i // 128) * 4 + ((i mod 128) * 4) // 128; every entry c of row i has c // 4 equal to i // 128, one more or one less, cyclically over 64 slabs.
All inputs are finite; a program needn't handle non-finite values.
Results may differ from a plain program's by a relative error of at most 0.0029.
Values may be sent and summed in bfloat16 or wider, within the bound.
No kernel may reach another device: no remote copies, remote signals or barrier semaphores. Data moves between devices by JAX's collectives and lax.ppermute only.
A program may use at most 128 MiB of HBM per device.

v0:
```python
import functools

import jax
import jax.numpy as jnp
from jax import lax
from jax.experimental import pallas as pl
from jax.experimental.pallas import tpu as pltpu
from jax.sharding import PartitionSpec as P

B = 64
CB = 24
KP = 8
NCD = 4
GROUP = 8


def shifted(value, axis, steps):
    count = lax.axis_size(axis)
    pairs = [(source, (source + steps) % count) for source in range(count)]
    return lax.ppermute(value, axis, pairs)


def widen(values, left_pad, right_pad):
    return jnp.pad(values, ((0, 0),) * (values.ndim - 1) + ((left_pad, right_pad),))


def slab_kernel(halo_rows, row_count, local_k, wpos_ref, jloc_ref, pb_ref, tb_ref, gt_ref,
                s_ref, xs_ref, w_ref):
    window_slots = 5 * NCD
    row_slots = 3 * NCD
    f32 = jnp.float32
    bf16 = jnp.bfloat16
    upper24 = lax.broadcasted_iota(jnp.int32, (CB, 128), 1) >= B
    upper64 = lax.broadcasted_iota(jnp.int32, (B, 128), 1) >= B
    gt_ref[...] = jnp.zeros(gt_ref.shape, f32)
    w_ref[...] = jnp.zeros(w_ref.shape, bf16)

    def place(dst, slot, lane_group, upper, r, p):
        src = pb_ref[r, :, (p // 2) * 128:(p // 2) * 128 + 128].astype(f32)
        if (p % 2 == 1) != upper:
            src = pltpu.roll(src, B, 1)
        keep = upper24 if upper else jnp.logical_not(upper24)
        rows = pl.ds(pl.multiple_of(slot * CB, 8), CB)
        lanes = slice(lane_group * 128, lane_group * 128 + 128)
        dst[rows, lanes] = dst[rows, lanes] + jnp.where(keep, src, 0.0)

    def group(g, carry):
        base = g * GROUP
        xs_ref[...] = jnp.zeros(xs_ref.shape, f32)
        for m in range(GROUP):
            r = base + m + halo_rows
            for p in range(KP):
                w = wpos_ref[r * KP + p]
                slot = jnp.clip(w - NCD, 0, row_slots - 1)
                place(xs_ref, slot, m // 2, m % 2 == 1, r, p)
        xsb = xs_ref[...].astype(bf16)
        for k in range(local_k):
            s_ref[...] = jnp.zeros(s_ref.shape, f32)
            for m in range(GROUP):
                r = jloc_ref[(base + m) * local_k + k]
                for p in range(KP):
                    w = wpos_ref[r * KP + p]
                    slot = jnp.clip(w, 0, window_slots - 1)
                    place(s_ref, slot, m // 2, m % 2 == 1, r, p)
            parts = []
            for c in range(GROUP // 4):
                for mm in range(4):
                    t = tb_ref[base + 4 * c + mm].astype(f32)
                    if (k % 2 == 1) != (mm % 2 == 1):
                        t = pltpu.roll(t, B, 1)
                    keep = upper64 if mm % 2 == 1 else jnp.logical_not(upper64)
                    w_ref[mm * B:(mm + 1) * B, (mm // 2) * 128:(mm // 2) * 128 + 128] = jnp.where(
                        keep, t, 0.0
                    ).astype(bf16)
                window = s_ref[:, c * 256:(c + 1) * 256].astype(bf16)
                q = lax.dot_general(
                    window, w_ref[...], (((1,), (1,)), ((), ())), preferred_element_type=f32
                )
                parts.append(q.astype(bf16))
            qt = jnp.concatenate(parts, axis=1)
            gt_ref[...] += lax.dot_general(
                qt, xsb, (((1,), (1,)), ((), ())), preferred_element_type=f32
            )
        return carry

    lax.fori_loop(0, row_count // GROUP, group, 0)


def slab_terms_t(wpos, jloc, pb, tb, halo_rows, row_count):
    local_k = tb.shape[2] // B
    window_width = 5 * NCD * CB
    row_width = 3 * NCD * CB
    kernel = functools.partial(slab_kernel, halo_rows, row_count, local_k)
    flops = 2 * row_count * local_k * (window_width * 256 * B + window_width * row_width * B)
    return pl.pallas_call(
        kernel,
        out_shape=jax.ShapeDtypeStruct((window_width, row_width), jnp.float32),
        in_specs=[
            pl.BlockSpec(memory_space=pltpu.SMEM),
            pl.BlockSpec(memory_space=pltpu.SMEM),
            pl.BlockSpec(memory_space=pltpu.VMEM),
            pl.BlockSpec(memory_space=pltpu.VMEM),
        ],
        out_specs=pl.BlockSpec(memory_space=pltpu.VMEM),
        scratch_shapes=[
            pltpu.VMEM((window_width, GROUP * B), jnp.float32),
            pltpu.VMEM((row_width, GROUP * B), jnp.float32),
            pltpu.VMEM((256, 256), jnp.bfloat16),
        ],
        compiler_params=pltpu.CompilerParams(vmem_limit_bytes=48 * 1024 * 1024),
        cost_estimate=pl.CostEstimate(
            flops=flops,
            bytes_accessed=pb.size * 2 + tb.size * 2 + window_width * row_width * 4,
            transcendentals=0,
        ),
    )(wpos, jloc, pb, tb)


def on_device(tangent_blocks, tangent_columns, prolong_blocks, prolong_columns):
    slab_count = lax.axis_size("blk")
    slab_index = lax.axis_index("blk")
    lane_count = lax.axis_size("lane")
    lane_index = lax.axis_index("lane")
    row_count = prolong_blocks.shape[0]
    halo_rows = row_count // 4
    coarse_width = NCD * CB
    fine_count = row_count * slab_count

    lower_blocks = shifted(prolong_blocks[row_count - halo_rows:], "blk", 1)
    upper_blocks = shifted(prolong_blocks[:halo_rows], "blk", -1)
    lower_columns = shifted(prolong_columns[row_count - halo_rows:], "blk", 1)
    upper_columns = shifted(prolong_columns[:halo_rows], "blk", -1)
    near_blocks = jnp.concatenate([lower_blocks, prolong_blocks, upper_blocks], axis=0)
    near_columns = jnp.concatenate([lower_columns, prolong_columns, upper_columns], axis=0)
    wpos = ((near_columns // NCD - slab_index + 2) % slab_count) * NCD + near_columns % NCD
    wpos = wpos.astype(jnp.int32).reshape(-1)
    jloc = (tangent_columns - slab_index * row_count + halo_rows) % fine_count
    jloc = jnp.clip(jloc, 0, row_count + 2 * halo_rows - 1).astype(jnp.int32).reshape(-1)

    gt = slab_terms_t(wpos, jloc, near_blocks, tangent_blocks, halo_rows, row_count)
    terms = gt.T.reshape(3, NCD, CB, 5 * coarse_width)

    shares = lax.dynamic_index_in_dim(terms, lane_index, axis=1, keepdims=False)
    for step in range(1, lane_count):
        piece = lax.dynamic_index_in_dim(
            terms, (lane_index + step) % lane_count, axis=1, keepdims=False
        )
        shares = shares + shifted(piece, "lane", step)
    from_lower = shifted(shares[2], "blk", 1)
    from_upper = shifted(shares[0], "blk", -1)
    coarse_band = (
        widen(shares[1], coarse_width, coarse_width)
        + widen(from_lower, 0, 2 * coarse_width)
        + widen(from_upper, 2 * coarse_width, 0)
    )
    return coarse_band[None]


def solution(mesh):
    return jax.shard_map(
        on_device,
        mesh=mesh,
        in_specs=(P("blk", None, "lane"), P("blk", "lane"), P("blk", None, None), P("blk", None)),
        out_specs=P(("blk", "lane"), None, None),
        check_vma=False,
    )
```

profile of v0, /device:TPU:0, one launch (start us, length us, event | category | flops | bytes accessed | tf_op | source)
XLA Modules:
  0.0 77.9 jit_solution(8691131455066164591)
XLA Ops:
  0.0 0.0 copy-start.1
  0.0 2.8 %fusion.10 = (bf16[32,24,512]{2,1,0:T(8,128)(2,1)}, bf16[32,24,512]{2,1,0:T(8,128)(2,1)}) fusion(bf16[128,24,512]{2,1,0:T(8,128)(2,1)} %param.6), kind=kLoop, calls=%fused_computation.32 | loop fusion | bytes 3145728 | tf_op jit(solution)/shard_map/slice | solution.py:129
  2.8 5.8 %collective-permute-start.3 = (bf16[32,24,512]{2,1,0:T(8,128)(2,1)}, bf16[32,24,512]{2,1,0:T(8,128)(2,1)}, u32[]{:S(2)}, u32[]{:S(2)}) collective-permute-start(bf16[32,24,512]{2,1,0:T(8,128)(2,1)} %get-tuple-element.6), channel_id=1, source_target_pairs={{0,252},{4,0},{8,4},{12,8},{16,12},{20,16},{24,20},{28,24},{32,28}... | collective-permute-start | bytes 2359304 | tf_op jit(solution)/shard_map/ppermute | solution.py:20
  8.6 0.0 collective-permute-start.2
  8.6 0.8 %fusion.11 = (s32[32,8]{0,1:T(8,128)S(1)}, s32[32,8]{0,1:T(8,128)S(1)}) fusion(s32[128,8]{0,1:T(8,128)} %param.7), kind=kLoop, calls=%fused_computation.33 | loop fusion | bytes 4096 | tf_op jit(solution)/shard_map/slice | solution.py:131
  9.4 5.1 %collective-permute-start.1 = (s32[32,8]{0,1:T(8,128)S(1)}, s32[32,8]{0,1:T(8,128)S(1)}, u32[]{:S(2)}, u32[]{:S(2)}) collective-permute-start(s32[32,8]{0,1:T(8,128)S(1)} %get-tuple-element.14), channel_id=1, source_target_pairs={{0,252},{4,0},{8,4},{12,8},{16,12},{20,16},{24,20},{28,24},{32,28}... | collective-permute-start | bytes 3080 | tf_op jit(solution)/shard_map/ppermute | solution.py:20
  14.5 0.0 collective-permute-start
  14.5 0.7 fusion.8
  15.2 0.1 copy.10
  15.3 0.1 reshape.8.jloc_ref
  15.4 3.0 %collective-permute-done.1 = s32[32,8]{0,1:T(8,128)S(1)} collective-permute-done((s32[32,8]{0,1:T(8,128)S(1)}, s32[32,8]{0,1:T(8,128)S(1)}, u32[]{:S(2)}, u32[]{:S(2)}) %collective-permute-start.1) | collective-permute-done | bytes 1056 | tf_op jit(solution)/shard_map/ppermute | solution.py:20
  18.4 5.2 %collective-permute-done = s32[32,8]{0,1:T(8,128)S(1)} collective-permute-done((s32[32,8]{0,1:T(8,128)S(1)}, s32[32,8]{0,1:T(8,128)S(1)}, u32[]{:S(2)}, u32[]{:S(2)}) %collective-permute-start) | collective-permute-done | bytes 1056 | tf_op jit(solution)/shard_map/ppermute | solution.py:20
  23.6 0.8 pad_add_fusion
  24.4 0.1 copy.9
  24.5 0.1 concatenate.9
  24.6 0.0 copy-start
  24.6 0.0 collective-permute-done.3
  24.7 0.0 collective-permute-done.2
  24.7 0.0 copy-done.1
  24.7 3.7 %pad_maximum_fusion.pb_ref = bf16[192,24,512]{2,1,0:T(8,128)(2,1)} fusion(bf16[32,24,512]{2,1,0:T(8,128)(2,1)} %collective-permute-done.3, bf16[128,24,512]{2,1,0:T(8,128)(2,1)S(1)} %copy-done.1, bf16[32,24,512]{2,1,0:T(8,128)(2,1)} %collective-permute-done.2), kind=kLoop, calls=%fused_computation | loop fusion | flops 4718592 | bytes 9437184 | tf_op jit(solution)/shard_map/concatenate | solution.py:133
  28.4 0.0 copy-done
  28.4 29.9 %shard_map.46 = f32[480,288]{1,0:T(8,128)S(1)} custom-call(s32[1536]{0:T(1024)S(1)} %fusion.6.wpos_ref, s32[256]{0:T(256)S(1)} %reshape.8.jloc_ref, bf16[192,24,512]{2,1,0:T(8,128)(2,1)} %pad_maximum_fusion.pb_ref, bf16[128,64,128]{2,1,0:T(8,128)(2,1)S(1)} %copy-done), custom_call_target="tpu_custom_call" | custom-call | flops 8556380160 | bytes 7368704 | tf_op jit(solution)/shard_map/pallas_call | solution.py:95
  58.3 0.2 copy.11
  58.6 3.1 %collective-permute-start.6 = (f32[3,24,480]{2,1,0:T(8,128)S(1)}, f32[3,24,480]{2,1,0:T(8,128)S(1)}, u32[]{:S(2)}, u32[]{:S(2)}) collective-permute-start(f32[3,24,480]{2,1,0:T(8,128)S(1)} %get-tuple-element.8), channel_id=1, source_target_pairs={{0,3},{1,0},{2,1},{3,2},{4,7},{5,4},{6,5},{7,6},{8,11},{9,8},{10,9... | collective-permute-start | bytes 414728 | tf_op jit(solution)/shard_map/ppermute | solution.py:20
  61.7 0.6 collective-permute-start.5
  62.3 1.0 %collective-permute-start.4 = (f32[3,24,480]{2,1,0:T(8,128)S(1)}, f32[3,24,480]{2,1,0:T(8,128)S(1)}, u32[]{:S(2)}, u32[]{:S(2)}) collective-permute-start(f32[3,24,480]{2,1,0:T(8,128)S(1)} %get-tuple-element.7), channel_id=1, source_target_pairs={{0,1},{1,2},{2,3},{3,0},{4,5},{5,6},{6,7},{7,4},{8,9},{9,10},{10,1... | collective-permute-start | bytes 414728 | tf_op jit(solution)/shard_map/ppermute | solution.py:20
  63.3 2.7 %collective-permute-done.6 = f32[3,24,480]{2,1,0:T(8,128)S(1)} collective-permute-done((f32[3,24,480]{2,1,0:T(8,128)S(1)}, f32[3,24,480]{2,1,0:T(8,128)S(1)}, u32[]{:S(2)}, u32[]{:S(2)}) %collective-permute-start.6) | collective-permute-done | bytes 138272 | tf_op jit(solution)/shard_map/ppermute | solution.py:20
  66.0 2.5 %collective-permute-done.5 = f32[3,24,480]{2,1,0:T(8,128)S(1)} collective-permute-done((f32[3,24,480]{2,1,0:T(8,128)S(1)}, f32[3,24,480]{2,1,0:T(8,128)S(1)}, u32[]{:S(2)}, u32[]{:S(2)}) %collective-permute-start.5) | collective-permute-done | bytes 138272 | tf_op jit(solution)/shard_map/ppermute | solution.py:20
  68.5 1.5 %collective-permute-done.4 = f32[3,24,480]{2,1,0:T(8,128)S(1)} collective-permute-done((f32[3,24,480]{2,1,0:T(8,128)S(1)}, f32[3,24,480]{2,1,0:T(8,128)S(1)}, u32[]{:S(2)}, u32[]{:S(2)}) %collective-permute-start.4) | collective-permute-done | bytes 138272 | tf_op jit(solution)/shard_map/ppermute | solution.py:20
  69.9 0.1 fusion.1
  70.0 0.3 collective-permute-start.8
  70.3 0.3 collective-permute-start.7
  70.6 1.5 %collective-permute-done.8 = f32[24,480]{1,0:T(8,128)S(1)} collective-permute-done((f32[24,480]{1,0:T(8,128)S(1)}, f32[24,480]{1,0:T(8,128)S(1)}, u32[]{:S(2)}, u32[]{:S(2)}) %collective-permute-start.8) | collective-permute-done | bytes 46112 | tf_op jit(solution)/shard_map/ppermute | solution.py:20
  72.1 5.1 %collective-permute-done.7 = f32[24,480]{1,0:T(8,128)S(1)} collective-permute-done((f32[24,480]{1,0:T(8,128)S(1)}, f32[24,480]{1,0:T(8,128)S(1)}, u32[]{:S(2)}, u32[]{:S(2)}) %collective-permute-start.7) | collective-permute-done | bytes 46112 | tf_op jit(solution)/shard_map/ppermute | solution.py:20
  77.2 0.7 add_bitcast_fusion
  (3 shorter events, 0.1 us)
Async XLA Ops:
  0.0 24.7 %copy-start.1 = (bf16[128,24,512]{2,1,0:T(8,128)(2,1)S(1)}, bf16[128,24,512]{2,1,0:T(8,128)(2,1)}, u32[]{:S(2)}) copy-start(bf16[128,24,512]{2,1,0:T(8,128)(2,1)} %param.6) | copy-start | bytes 9437188
  2.8 21.8 %collective-permute-start.3 = (bf16[32,24,512]{2,1,0:T(8,128)(2,1)}, bf16[32,24,512]{2,1,0:T(8,128)(2,1)}, u32[]{:S(2)}, u32[]{:S(2)}) collective-permute-start(bf16[32,24,512]{2,1,0:T(8,128)(2,1)} %get-tuple-element.6), channel_id=1, source_target_pairs={{0,252},{4,0},{8,4},{12,8},{16,12},{20,16},{24,20},{28,24},{32,28}... | collective-permute-start | bytes 2359304 | tf_op jit(solution)/shard_map/ppermute | solution.py:20
  8.6 16.1 %collective-permute-start.2 = (bf16[32,24,512]{2,1,0:T(8,128)(2,1)}, bf16[32,24,512]{2,1,0:T(8,128)(2,1)}, u32[]{:S(2)}, u32[]{:S(2)}) collective-permute-start(bf16[32,24,512]{2,1,0:T(8,128)(2,1)} %get-tuple-element.5), channel_id=1, source_target_pairs={{0,4},{4,8},{8,12},{12,16},{16,20},{20,24},{24,28},{28,32},{32,36}... | collective-permute-start | bytes 2359304 | tf_op jit(solution)/shard_map/ppermute | solution.py:20
  9.4 9.0 %collective-permute-start.1 = (s32[32,8]{0,1:T(8,128)S(1)}, s32[32,8]{0,1:T(8,128)S(1)}, u32[]{:S(2)}, u32[]{:S(2)}) collective-permute-start(s32[32,8]{0,1:T(8,128)S(1)} %get-tuple-element.14), channel_id=1, source_target_pairs={{0,252},{4,0},{8,4},{12,8},{16,12},{20,16},{24,20},{28,24},{32,28}... | collective-permute-start | bytes 3080 | tf_op jit(solution)/shard_map/ppermute | solution.py:20
  14.5 9.2 %collective-permute-start = (s32[32,8]{0,1:T(8,128)S(1)}, s32[32,8]{0,1:T(8,128)S(1)}, u32[]{:S(2)}, u32[]{:S(2)}) collective-permute-start(s32[32,8]{0,1:T(8,128)S(1)} %get-tuple-element.13), channel_id=1, source_target_pairs={{0,4},{4,8},{8,12},{12,16},{16,20},{20,24},{24,28},{28,32},{32,36}... | collective-permute-start | bytes 3080 | tf_op jit(solution)/shard_map/ppermute | solution.py:20
  24.6 3.8 %copy-start = (bf16[128,64,128]{2,1,0:T(8,128)(2,1)S(1)}, bf16[128,64,128]{2,1,0:T(8,128)(2,1)}, u32[]{:S(2)}) copy-start(bf16[128,64,128]{2,1,0:T(8,128)(2,1)} %tb_ref.1) | copy-start | bytes 6291460
  58.6 7.4 %collective-permute-start.6 = (f32[3,24,480]{2,1,0:T(8,128)S(1)}, f32[3,24,480]{2,1,0:T(8,128)S(1)}, u32[]{:S(2)}, u32[]{:S(2)}) collective-permute-start(f32[3,24,480]{2,1,0:T(8,128)S(1)} %get-tuple-element.8), channel_id=1, source_target_pairs={{0,3},{1,0},{2,1},{3,2},{4,7},{5,4},{6,5},{7,6},{8,11},{9,8},{10,9... | collective-permute-start | bytes 414728 | tf_op jit(solution)/shard_map/ppermute | solution.py:20
  61.7 6.8 %collective-permute-start.5 = (f32[3,24,480]{2,1,0:T(8,128)S(1)}, f32[3,24,480]{2,1,0:T(8,128)S(1)}, u32[]{:S(2)}, u32[]{:S(2)}) collective-permute-start(f32[3,24,480]{2,1,0:T(8,128)S(1)} %get-tuple-element.9), channel_id=1, source_target_pairs={{0,2},{1,3},{2,0},{3,1},{4,6},{5,7},{6,4},{7,5},{8,10},{9,11},{10,... | collective-permute-start | bytes 414728 | tf_op jit(solution)/shard_map/ppermute | solution.py:20
  62.3 7.6 %collective-permute-start.4 = (f32[3,24,480]{2,1,0:T(8,128)S(1)}, f32[3,24,480]{2,1,0:T(8,128)S(1)}, u32[]{:S(2)}, u32[]{:S(2)}) collective-permute-start(f32[3,24,480]{2,1,0:T(8,128)S(1)} %get-tuple-element.7), channel_id=1, source_target_pairs={{0,1},{1,2},{2,3},{3,0},{4,5},{5,6},{6,7},{7,4},{8,9},{9,10},{10,1... | collective-permute-start | bytes 414728 | tf_op jit(solution)/shard_map/ppermute | solution.py:20
  70.0 2.1 %collective-permute-start.8 = (f32[24,480]{1,0:T(8,128)S(1)}, f32[24,480]{1,0:T(8,128)S(1)}, u32[]{:S(2)}, u32[]{:S(2)}) collective-permute-start(f32[24,480]{1,0:T(8,128)S(1)} %get-tuple-element.11), channel_id=1, source_target_pairs={{0,252},{4,0},{8,4},{12,8},{16,12},{20,16},{24,20},{28,24},{32,28}... | collective-permute-start | bytes 138248 | tf_op jit(solution)/shard_map/ppermute | solution.py:20
  70.3 6.8 %collective-permute-start.7 = (f32[24,480]{1,0:T(8,128)S(1)}, f32[24,480]{1,0:T(8,128)S(1)}, u32[]{:S(2)}, u32[]{:S(2)}) collective-permute-start(f32[24,480]{1,0:T(8,128)S(1)} %get-tuple-element.12), channel_id=1, source_target_pairs={{0,4},{4,8},{8,12},{12,16},{16,20},{20,24},{24,28},{28,32},{32,36}... | collective-permute-start | bytes 138248 | tf_op jit(solution)/shard_map/ppermute | solution.py:20
where the time goes:
time: 78.1 us; the launch traced here: 77.9 us
  Pallas kernels  29.9 us (38%)
  waiting for transfers between devices  21.4 us (27%)
  starting transfers between devices  16.1 us (21%)
  other arithmetic  5.98 us (8%)
  local copies, waits for them, and re-layouts  4.4 us (6%)
    pallas_call x1, Pallas kernels, slab_terms_t(): pl.pallas_call(kernel, out_shape=jax.ShapeDtypeStruct((window_width, row_...  29.9 us
    ppermute x9, waiting for transfers between devices, shifted(): return lax.ppermute(value, axis, pairs)  21.4 us
    ppermute x9, starting transfers between devices, shifted(): return lax.ppermute(value, axis, pairs)  16.1 us
    concatenate x1, other arithmetic, on_device(): jnp.concatenate([lower_blocks, prolong_blocks, upper_blocks], axis=0)  3.72 us
    slice x1, local copies, waits for them, and re-layouts, on_device(): lower_blocks = shifted(prolong_blocks[row_count - halo_rows:], 'blk', 1)  2.8 us
  transfers between devices with their start and end apart: 9, of which 7 were waited for; matrix products, arithmetic and copies ran while one was open for 4% of the time, Pallas kernels for 0%

commit v1 on v0

--- a/solution.py
+++ b/solution.py
@@ -140,16 +140,27 @@
     gt = slab_terms_t(wpos, jloc, near_blocks, tangent_blocks, halo_rows, row_count)
     terms = gt.T.reshape(3, NCD, CB, 5 * coarse_width)
 
-    shares = lax.dynamic_index_in_dim(terms, lane_index, axis=1, keepdims=False)
-    for step in range(1, lane_count):
-        piece = lax.dynamic_index_in_dim(
-            terms, (lane_index + step) % lane_count, axis=1, keepdims=False
-        )
-        shares = shares + shifted(piece, "lane", step)
-    from_lower = shifted(shares[2], "blk", 1)
-    from_upper = shifted(shares[0], "blk", -1)
+    combined = ("blk", "lane")
+    device_count = slab_count * lane_count
+    bands = []
+    for slab_step in (1, 0, -1):
+        total = None
+        for lane_step in range(lane_count):
+            piece = lax.dynamic_index_in_dim(
+                terms[1 + slab_step], (lane_index + lane_step) % lane_count, axis=0, keepdims=False
+            )
+            if slab_step != 0 or lane_step != 0:
+                pairs = []
+                for source in range(device_count):
+                    s_src, l_src = divmod(source, lane_count)
+                    target = ((s_src + slab_step) % slab_count) * lane_count + (l_src + lane_step) % lane_count
+                    pairs.append((source, target))
+                piece = lax.ppermute(piece, combined, pairs)
+            total = piece if total is None else total + piece
+        bands.append(total)
+    from_lower, own, from_upper = bands
     coarse_band = (
-        widen(shares[1], coarse_width, coarse_width)
+        widen(own, coarse_width, coarse_width)
         + widen(from_lower, 0, 2 * coarse_width)
         + widen(from_upper, 2 * coarse_width, 0)
     )

time: 78.1 us -> 84.4 us (1.081)
  starting transfers between devices: 16.1 us -> 22.9 us
  waiting for transfers between devices: 21.4 us -> 20.5 us
    ppermute x9 -> x4, waiting for transfers between devices: 21.4 us -> 8.18 us  [shifted(): return lax.ppermute(value, axis, pairs)]
    ppermute x0 -> x11, waiting for transfers between devices: none -> 12.3 us  [on_device(): piece = lax.ppermute(piece, combined, pairs)]
    ppermute x0 -> x11, starting transfers between devices: none -> 12 us  [on_device(): piece = lax.ppermute(piece, combined, pairs)]
    ppermute x9 -> x4, starting transfers between devices: 16.1 us -> 10.8 us  [shifted(): return lax.ppermute(value, axis, pairs)]
  transfers between devices with their start and end apart: 9 -> 15, of which waited for: 7 -> 7; matrix products, arithmetic and copies ran while one was open for 4% -> 4% of each run, Pallas kernels for 0% -> 0%
where the time goes in v1:
time: 84.4 us; the launch traced here: 84.2 us
  Pallas kernels  29.9 us (35%)
  starting transfers between devices  22.9 us (27%)
  waiting for transfers between devices  20.5 us (24%)
  other arithmetic  5.97 us (7%)
  local copies, waits for them, and re-layouts  4.74 us (6%)
    pallas_call x1, Pallas kernels, slab_terms_t(): pl.pallas_call(kernel, out_shape=jax.ShapeDtypeStruct((window_width, row_...  29.9 us
    ppermute x11, waiting for transfers between devices, on_device(): piece = lax.ppermute(piece, combined, pairs)  12.3 us
    ppermute x11, starting transfers between devices, on_device(): piece = lax.ppermute(piece, combined, pairs)  12 us
    ppermute x4, starting transfers between devices, shifted(): return lax.ppermute(value, axis, pairs)  10.8 us
    ppermute x4, waiting for transfers between devices, shifted(): return lax.ppermute(value, axis, pairs)  8.18 us
    concatenate x1, other arithmetic, on_device(): jnp.concatenate([lower_blocks, prolong_blocks, upper_blocks], axis=0)  3.71 us
    slice x1, local copies, waits for them, and re-layouts, on_device(): lower_blocks = shifted(prolong_blocks[row_count - halo_rows:], 'blk', 1)  2.8 us
  transfers between devices with their start and end apart: 15, of which 7 were waited for; matrix products, arithmetic and copies ran while one was open for 4% of the time, Pallas kernels for 0%

profile of v1, /device:TPU:0, one launch (start us, length us, event | category | flops | bytes accessed | tf_op | source)
XLA Modules:
  0.0 84.2 jit_solution(6615877090622444314)
XLA Ops:
  0.0 0.0 copy-start.1
  0.0 2.8 %fusion.10 = (bf16[32,24,512]{2,1,0:T(8,128)(2,1)}, bf16[32,24,512]{2,1,0:T(8,128)(2,1)}) fusion(bf16[128,24,512]{2,1,0:T(8,128)(2,1)} %param.6), kind=kLoop, calls=%fused_computation.39 | loop fusion | bytes 3145728 | tf_op jit(solution)/shard_map/slice | solution.py:129
  2.8 5.8 %collective-permute-start.3 = (bf16[32,24,512]{2,1,0:T(8,128)(2,1)}, bf16[32,24,512]{2,1,0:T(8,128)(2,1)}, u32[]{:S(2)}, u32[]{:S(2)}) collective-permute-start(bf16[32,24,512]{2,1,0:T(8,128)(2,1)} %get-tuple-element.6), channel_id=1, source_target_pairs={{0,252},{4,0},{8,4},{12,8},{16,12},{20,16},{24,20},{28,24},{32,28}... | collective-permute-start | bytes 2359304 | tf_op jit(solution)/shard_map/ppermute | solution.py:20
  8.6 0.0 collective-permute-start.2
  8.6 0.8 fusion.12
  9.4 5.1 %collective-permute-start.1 = (s32[32,8]{0,1:T(8,128)S(1)}, s32[32,8]{0,1:T(8,128)S(1)}, u32[]{:S(2)}, u32[]{:S(2)}) collective-permute-start(s32[32,8]{0,1:T(8,128)S(1)} %get-tuple-element.22), channel_id=1, source_target_pairs={{0,252},{4,0},{8,4},{12,8},{16,12},{20,16},{24,20},{28,24},{32,28}... | collective-permute-start | bytes 3080 | tf_op jit(solution)/shard_map/ppermute | solution.py:20
  14.5 0.0 collective-permute-start
  14.5 0.7 fusion.8
  15.2 0.1 copy.18
  15.3 0.1 reshape.12.jloc_ref
  15.4 3.0 %collective-permute-done.1 = s32[32,8]{0,1:T(8,128)S(1)} collective-permute-done((s32[32,8]{0,1:T(8,128)S(1)}, s32[32,8]{0,1:T(8,128)S(1)}, u32[]{:S(2)}, u32[]{:S(2)}) %collective-permute-start.1) | collective-permute-done | bytes 1056 | tf_op jit(solution)/shard_map/ppermute | solution.py:20
  18.4 5.2 %collective-permute-done = s32[32,8]{0,1:T(8,128)S(1)} collective-permute-done((s32[32,8]{0,1:T(8,128)S(1)}, s32[32,8]{0,1:T(8,128)S(1)}, u32[]{:S(2)}, u32[]{:S(2)}) %collective-permute-start) | collective-permute-done | bytes 1056 | tf_op jit(solution)/shard_map/ppermute | solution.py:20
  23.6 0.8 pad_add_fusion
  24.4 0.1 copy.17
  24.5 0.1 concatenate.9
  24.6 0.0 copy-start
  24.6 0.0 collective-permute-done.3
  24.7 0.0 collective-permute-done.2
  24.7 0.0 copy-done.1
  24.7 3.7 %pad_maximum_fusion.pb_ref = bf16[192,24,512]{2,1,0:T(8,128)(2,1)} fusion(bf16[32,24,512]{2,1,0:T(8,128)(2,1)} %collective-permute-done.3, bf16[128,24,512]{2,1,0:T(8,128)(2,1)S(1)} %copy-done.1, bf16[32,24,512]{2,1,0:T(8,128)(2,1)} %collective-permute-done.2), kind=kLoop, calls=%fused_computation | loop fusion | flops 4718592 | bytes 9437184 | tf_op jit(solution)/shard_map/concatenate | solution.py:133
  28.4 0.0 copy-done
  28.4 29.9 %shard_map.46 = f32[480,288]{1,0:T(8,128)S(1)} custom-call(s32[1536]{0:T(1024)S(1)} %fusion.6.wpos_ref, s32[256]{0:T(256)S(1)} %reshape.12.jloc_ref, bf16[192,24,512]{2,1,0:T(8,128)(2,1)} %pad_maximum_fusion.pb_ref, bf16[128,64,128]{2,1,0:T(8,128)(2,1)S(1)} %copy-done), custom_call_target="tpu_custom_call" | custom-call | flops 8556380160 | bytes 7368704 | tf_op jit(solution)/shard_map/pallas_call | solution.py:95
  58.3 0.2 fusion.11
  58.5 0.1 copy.21
  58.7 2.5 %collective-permute-start.14 = (f32[24,480]{1,0:T(8,128)S(1)}, f32[24,480]{1,0:T(8,128)S(1)}, u32[]{:S(2)}, u32[]{:S(2)}) collective-permute-start(f32[24,480]{1,0:T(8,128)S(1)} %get-tuple-element.18), channel_id=1, source_target_pairs={{0,255},{1,252},{2,253},{3,254},{4,3},{5,0},{6,1},{7,2},{8,7},{9,4... | collective-permute-start | bytes 138248 | tf_op jit(solution)/shard_map/ppermute | solution.py:158
  61.2 0.3 collective-permute-start.13
  61.5 0.0 collective-permute-start.11
  61.5 0.0 collective-permute-start.12
  61.5 0.1 copy.20
  61.6 3.0 %collective-permute-start.10 = (f32[24,480]{1,0:T(8,128)S(1)}, f32[24,480]{1,0:T(8,128)S(1)}, u32[]{:S(2)}, u32[]{:S(2)}) collective-permute-start(f32[24,480]{1,0:T(8,128)S(1)} %get-tuple-element.14), channel_id=1, source_target_pairs={{0,7},{1,4},{2,5},{3,6},{4,11},{5,8},{6,9},{7,10},{8,15},{9,12},{1... | collective-permute-start | bytes 138248 | tf_op jit(solution)/shard_map/ppermute | solution.py:158
  64.7 0.1 copy.19
  64.8 0.0 collective-permute-done.14
  64.8 2.8 %collective-permute-start.9 = (f32[24,480]{1,0:T(8,128)S(1)}, f32[24,480]{1,0:T(8,128)S(1)}, u32[]{:S(2)}, u32[]{:S(2)}) collective-permute-start(f32[24,480]{1,0:T(8,128)S(1)} %get-tuple-element.15), channel_id=1, source_target_pairs={{0,6},{1,7},{2,4},{3,5},{4,10},{5,11},{6,8},{7,9},{8,14},{9,15},{1... | collective-permute-start | bytes 138248 | tf_op jit(solution)/shard_map/ppermute | solution.py:158
  67.6 0.0 collective-permute-done.13
  67.6 0.7 collective-permute-start.6
  68.3 0.0 collective-permute-done.11
  68.3 1.4 %collective-permute-start.5 = (f32[24,480]{1,0:T(8,128)S(1)}, f32[24,480]{1,0:T(8,128)S(1)}, u32[]{:S(2)}, u32[]{:S(2)}) collective-permute-start(f32[24,480]{1,0:T(8,128)S(1)} %get-tuple-element.12), channel_id=1, source_target_pairs={{0,2},{1,3},{2,0},{3,1},{4,6},{5,7},{6,4},{7,5},{8,10},{9,11},{10,... | collective-permute-start | bytes 138248 | tf_op jit(solution)/shard_map/ppermute | solution.py:158
  69.7 0.0 collective-permute-done.12
  69.7 1.3 %collective-permute-start.4 = (f32[24,480]{1,0:T(8,128)S(1)}, f32[24,480]{1,0:T(8,128)S(1)}, u32[]{:S(2)}, u32[]{:S(2)}) collective-permute-start(f32[24,480]{1,0:T(8,128)S(1)} %get-tuple-element.10), channel_id=1, source_target_pairs={{0,1},{1,2},{2,3},{3,0},{4,5},{5,6},{6,7},{7,4},{8,9},{9,10},{10,1... | collective-permute-start | bytes 138248 | tf_op jit(solution)/shard_map/ppermute | solution.py:158
  71.1 0.9 %collective-permute-done.6 = f32[24,480]{1,0:T(8,128)S(1)} collective-permute-done((f32[24,480]{1,0:T(8,128)S(1)}, f32[24,480]{1,0:T(8,128)S(1)}, u32[]{:S(2)}, u32[]{:S(2)}) %collective-permute-start.6) | collective-permute-done | bytes 46112 | tf_op jit(solution)/shard_map/ppermute | solution.py:158
  71.9 0.0 collective-permute-start.7
  71.9 2.6 %collective-permute-done.5 = f32[24,480]{1,0:T(8,128)S(1)} collective-permute-done((f32[24,480]{1,0:T(8,128)S(1)}, f32[24,480]{1,0:T(8,128)S(1)}, u32[]{:S(2)}, u32[]{:S(2)}) %collective-permute-start.5) | collective-permute-done | bytes 46112 | tf_op jit(solution)/shard_map/ppermute | solution.py:158
  74.5 0.0 collective-permute-start.8
  74.5 1.0 %collective-permute-done.4 = f32[24,480]{1,0:T(8,128)S(1)} collective-permute-done((f32[24,480]{1,0:T(8,128)S(1)}, f32[24,480]{1,0:T(8,128)S(1)}, u32[]{:S(2)}, u32[]{:S(2)}) %collective-permute-start.4) | collective-permute-done | bytes 46112 | tf_op jit(solution)/shard_map/ppermute | solution.py:158
  75.5 0.0 collective-permute-done.10
  75.5 0.0 collective-permute-done.9
  75.5 3.2 %collective-permute-done.7 = f32[24,480]{1,0:T(8,128)S(1)} collective-permute-done((f32[24,480]{1,0:T(8,128)S(1)}, f32[24,480]{1,0:T(8,128)S(1)}, u32[]{:S(2)}, u32[]{:S(2)}) %collective-permute-start.7) | collective-permute-done | bytes 46112 | tf_op jit(solution)/shard_map/ppermute | solution.py:158
  78.8 4.7 %collective-permute-done.8 = f32[24,480]{1,0:T(8,128)S(1)} collective-permute-done((f32[24,480]{1,0:T(8,128)S(1)}, f32[24,480]{1,0:T(8,128)S(1)}, u32[]{:S(2)}, u32[]{:S(2)}) %collective-permute-start.8) | collective-permute-done | bytes 46112 | tf_op jit(solution)/shard_map/ppermute | solution.py:158
  83.5 0.7 add_bitcast_fusion
  (7 shorter events, 0.2 us)
Async XLA Ops:
  0.0 24.7 %copy-start.1 = (bf16[128,24,512]{2,1,0:T(8,128)(2,1)S(1)}, bf16[128,24,512]{2,1,0:T(8,128)(2,1)}, u32[]{:S(2)}) copy-start(bf16[128,24,512]{2,1,0:T(8,128)(2,1)} %param.6) | copy-start | bytes 9437188
  2.8 21.8 %collective-permute-start.3 = (bf16[32,24,512]{2,1,0:T(8,128)(2,1)}, bf16[32,24,512]{2,1,0:T(8,128)(2,1)}, u32[]{:S(2)}, u32[]{:S(2)}) collective-permute-start(bf16[32,24,512]{2,1,0:T(8,128)(2,1)} %get-tuple-element.6), channel_id=1, source_target_pairs={{0,252},{4,0},{8,4},{12,8},{16,12},{20,16},{24,20},{28,24},{32,28}... | collective-permute-start | bytes 2359304 | tf_op jit(solution)/shard_map/ppermute | solution.py:20
  8.6 16.1 %collective-permute-start.2 = (bf16[32,24,512]{2,1,0:T(8,128)(2,1)}, bf16[32,24,512]{2,1,0:T(8,128)(2,1)}, u32[]{:S(2)}, u32[]{:S(2)}) collective-permute-start(bf16[32,24,512]{2,1,0:T(8,128)(2,1)} %get-tuple-element.5), channel_id=1, source_target_pairs={{0,4},{4,8},{8,12},{12,16},{16,20},{20,24},{24,28},{28,32},{32,36}... | collective-permute-start | bytes 2359304 | tf_op jit(solution)/shard_map/ppermute | solution.py:20
  9.4 9.0 %collective-permute-start.1 = (s32[32,8]{0,1:T(8,128)S(1)}, s32[32,8]{0,1:T(8,128)S(1)}, u32[]{:S(2)}, u32[]{:S(2)}) collective-permute-start(s32[32,8]{0,1:T(8,128)S(1)} %get-tuple-element.22), channel_id=1, source_target_pairs={{0,252},{4,0},{8,4},{12,8},{16,12},{20,16},{24,20},{28,24},{32,28}... | collective-permute-start | bytes 3080 | tf_op jit(solution)/shard_map/ppermute | solution.py:20
  14.5 9.2 %collective-permute-start = (s32[32,8]{0,1:T(8,128)S(1)}, s32[32,8]{0,1:T(8,128)S(1)}, u32[]{:S(2)}, u32[]{:S(2)}) collective-permute-start(s32[32,8]{0,1:T(8,128)S(1)} %get-tuple-element.21), channel_id=1, source_target_pairs={{0,4},{4,8},{8,12},{12,16},{16,20},{20,24},{24,28},{28,32},{32,36}... | collective-permute-start | bytes 3080 | tf_op jit(solution)/shard_map/ppermute | solution.py:20
  24.6 3.8 %copy-start = (bf16[128,64,128]{2,1,0:T(8,128)(2,1)S(1)}, bf16[128,64,128]{2,1,0:T(8,128)(2,1)}, u32[]{:S(2)}) copy-start(bf16[128,64,128]{2,1,0:T(8,128)(2,1)} %tb_ref.1) | copy-start | bytes 6291460
  58.7 6.1 %collective-permute-start.14 = (f32[24,480]{1,0:T(8,128)S(1)}, f32[24,480]{1,0:T(8,128)S(1)}, u32[]{:S(2)}, u32[]{:S(2)}) collective-permute-start(f32[24,480]{1,0:T(8,128)S(1)} %get-tuple-element.18), channel_id=1, source_target_pairs={{0,255},{1,252},{2,253},{3,254},{4,3},{5,0},{6,1},{7,2},{8,7},{9,4... | collective-permute-start | bytes 138248 | tf_op jit(solution)/shard_map/ppermute | solution.py:158
  61.2 6.4 %collective-permute-start.13 = (f32[24,480]{1,0:T(8,128)S(1)}, f32[24,480]{1,0:T(8,128)S(1)}, u32[]{:S(2)}, u32[]{:S(2)}) collective-permute-start(f32[24,480]{1,0:T(8,128)S(1)} %get-tuple-element.19), channel_id=1, source_target_pairs={{0,254},{1,255},{2,252},{3,253},{4,2},{5,3},{6,0},{7,1},{8,6},{9,7... | collective-permute-start | bytes 138248 | tf_op jit(solution)/shard_map/ppermute | solution.py:158
  61.5 6.9 %collective-permute-start.11 = (f32[24,480]{1,0:T(8,128)S(1)}, f32[24,480]{1,0:T(8,128)S(1)}, u32[]{:S(2)}, u32[]{:S(2)}) collective-permute-start(f32[24,480]{1,0:T(8,128)S(1)} %get-tuple-element.20), channel_id=1, source_target_pairs={{0,252},{1,253},{2,254},{3,255},{4,0},{5,1},{6,2},{7,3},{8,4},{9,5... | collective-permute-start | bytes 138248 | tf_op jit(solution)/shard_map/ppermute | solution.py:158
  61.5 8.3 %collective-permute-start.12 = (f32[24,480]{1,0:T(8,128)S(1)}, f32[24,480]{1,0:T(8,128)S(1)}, u32[]{:S(2)}, u32[]{:S(2)}) collective-permute-start(f32[24,480]{1,0:T(8,128)S(1)} %get-tuple-element.17), channel_id=1, source_target_pairs={{0,253},{1,254},{2,255},{3,252},{4,1},{5,2},{6,3},{7,0},{8,5},{9,6... | collective-permute-start | bytes 138248 | tf_op jit(solution)/shard_map/ppermute | solution.py:158
  61.6 13.9 %collective-permute-start.10 = (f32[24,480]{1,0:T(8,128)S(1)}, f32[24,480]{1,0:T(8,128)S(1)}, u32[]{:S(2)}, u32[]{:S(2)}) collective-permute-start(f32[24,480]{1,0:T(8,128)S(1)} %get-tuple-element.14), channel_id=1, source_target_pairs={{0,7},{1,4},{2,5},{3,6},{4,11},{5,8},{6,9},{7,10},{8,15},{9,12},{1... | collective-permute-start | bytes 138248 | tf_op jit(solution)/shard_map/ppermute | solution.py:158
  64.8 10.7 %collective-permute-start.9 = (f32[24,480]{1,0:T(8,128)S(1)}, f32[24,480]{1,0:T(8,128)S(1)}, u32[]{:S(2)}, u32[]{:S(2)}) collective-permute-start(f32[24,480]{1,0:T(8,128)S(1)} %get-tuple-element.15), channel_id=1, source_target_pairs={{0,6},{1,7},{2,4},{3,5},{4,10},{5,11},{6,8},{7,9},{8,14},{9,15},{1... | collective-permute-start | bytes 138248 | tf_op jit(solution)/shard_map/ppermute | solution.py:158
  67.6 4.4 %collective-permute-start.6 = (f32[24,480]{1,0:T(8,128)S(1)}, f32[24,480]{1,0:T(8,128)S(1)}, u32[]{:S(2)}, u32[]{:S(2)}) collective-permute-start(f32[24,480]{1,0:T(8,128)S(1)} %get-tuple-element.11), channel_id=1, source_target_pairs={{0,3},{1,0},{2,1},{3,2},{4,7},{5,4},{6,5},{7,6},{8,11},{9,8},{10,9... | collective-permute-start | bytes 138248 | tf_op jit(solution)/shard_map/ppermute | solution.py:158
  68.3 6.2 %collective-permute-start.5 = (f32[24,480]{1,0:T(8,128)S(1)}, f32[24,480]{1,0:T(8,128)S(1)}, u32[]{:S(2)}, u32[]{:S(2)}) collective-permute-start(f32[24,480]{1,0:T(8,128)S(1)} %get-tuple-element.12), channel_id=1, source_target_pairs={{0,2},{1,3},{2,0},{3,1},{4,6},{5,7},{6,4},{7,5},{8,10},{9,11},{10,... | collective-permute-start | bytes 138248 | tf_op jit(solution)/shard_map/ppermute | solution.py:158
  69.7 5.8 %collective-permute-start.4 = (f32[24,480]{1,0:T(8,128)S(1)}, f32[24,480]{1,0:T(8,128)S(1)}, u32[]{:S(2)}, u32[]{:S(2)}) collective-permute-start(f32[24,480]{1,0:T(8,128)S(1)} %get-tuple-element.10), channel_id=1, source_target_pairs={{0,1},{1,2},{2,3},{3,0},{4,5},{5,6},{6,7},{7,4},{8,9},{9,10},{10,1... | collective-permute-start | bytes 138248 | tf_op jit(solution)/shard_map/ppermute | solution.py:158
  71.9 6.8 %collective-permute-start.7 = (f32[24,480]{1,0:T(8,128)S(1)}, f32[24,480]{1,0:T(8,128)S(1)}, u32[]{:S(2)}, u32[]{:S(2)}) collective-permute-start(f32[24,480]{1,0:T(8,128)S(1)} %get-tuple-element.16), channel_id=1, source_target_pairs={{0,4},{1,5},{2,6},{3,7},{4,8},{5,9},{6,10},{7,11},{8,12},{9,13},{1... | collective-permute-start | bytes 138248 | tf_op jit(solution)/shard_map/ppermute | solution.py:158
  74.5 8.9 %collective-permute-start.8 = (f32[24,480]{1,0:T(8,128)S(1)}, f32[24,480]{1,0:T(8,128)S(1)}, u32[]{:S(2)}, u32[]{:S(2)}) collective-permute-start(f32[24,480]{1,0:T(8,128)S(1)} %get-tuple-element.13), channel_id=1, source_target_pairs={{0,5},{1,6},{2,7},{3,4},{4,9},{5,10},{6,11},{7,8},{8,13},{9,14},{1... | collective-permute-start | bytes 138248 | tf_op jit(solution)/shard_map/ppermute | solution.py:158

commit v2 on v0

--- a/solution.py
+++ b/solution.py
@@ -126,12 +126,23 @@
     coarse_width = NCD * CB
     fine_count = row_count * slab_count
 
-    lower_blocks = shifted(prolong_blocks[row_count - halo_rows:], "blk", 1)
-    upper_blocks = shifted(prolong_blocks[:halo_rows], "blk", -1)
-    lower_columns = shifted(prolong_columns[row_count - halo_rows:], "blk", 1)
-    upper_columns = shifted(prolong_columns[:halo_rows], "blk", -1)
-    near_blocks = jnp.concatenate([lower_blocks, prolong_blocks, upper_blocks], axis=0)
-    near_columns = jnp.concatenate([lower_columns, prolong_columns, upper_columns], axis=0)
+    def with_columns(rows):
+        blocks = prolong_blocks[rows]
+        columns = prolong_columns[rows].astype(jnp.bfloat16)
+        columns = jnp.pad(columns, ((0, 0), (0, blocks.shape[2] - KP)))[:, None, :]
+        return jnp.concatenate([blocks, columns], axis=1)
+
+    lower = shifted(with_columns(slice(row_count - halo_rows, row_count)), "blk", 1)
+    upper = shifted(with_columns(slice(0, halo_rows)), "blk", -1)
+    near_blocks = jnp.concatenate([lower[:, :CB], prolong_blocks, upper[:, :CB]], axis=0)
+    near_columns = jnp.concatenate(
+        [
+            lower[:, CB, :KP].astype(jnp.int32),
+            prolong_columns,
+            upper[:, CB, :KP].astype(jnp.int32),
+        ],
+        axis=0,
+    )
     wpos = ((near_columns // NCD - slab_index + 2) % slab_count) * NCD + near_columns % NCD
     wpos = wpos.astype(jnp.int32).reshape(-1)
     jloc = (tangent_columns - slab_index * row_count + halo_rows) % fine_count

time: 78.1 us -> 82.8 us (1.060)
  waiting for transfers between devices: 21.4 us -> 27.6 us
  starting transfers between devices: 16.1 us -> 11.1 us
  local copies, waits for them, and re-layouts: 4.4 us -> 6.95 us
    ppermute x9 -> x7, waiting for transfers between devices: 21.4 us -> 27.6 us  [shifted(): return lax.ppermute(value, axis, pairs)]
    ppermute x9 -> x7, starting transfers between devices: 16.1 us -> 11.1 us  [shifted(): return lax.ppermute(value, axis, pairs)]
    unnamed x4 -> x13, local copies, waits for them, and re-layouts: 0.01 us -> 2.15 us
    convert_element_type x0 -> x2, other arithmetic: none -> 1.4 us  [the longest x1 0.7 us: on_device(): lower[:, CB, :KP].astype(jnp.int32)]
    slice x2 -> x4, local copies, waits for them, and re-layouts: 3.64 us -> 3.89 us  [the longest x1 1.48 us: with_columns(): blocks = prolong_blocks[rows]]
    concatenate x2 -> x4, other arithmetic: 4.48 us -> 4.53 us  [the longest x1 2.48 us: on_device(): jnp.concatenate([lower[:, :CB], prolong_blocks, upper[:, :CB]], axis=0)]
  transfers between devices with their start and end apart: 9 -> 7, of which waited for: 7 -> 7; matrix products, arithmetic and copies ran while one was open for 4% -> 3% of each run, Pallas kernels for 0% -> 0%
where the time goes in v2:
time: 82.8 us; the launch traced here: 82.4 us
  Pallas kernels  29.9 us (36%)
  waiting for transfers between devices  27.6 us (33%)
  starting transfers between devices  11.1 us (13%)
  local copies, waits for them, and re-layouts  6.95 us (8%)
  other arithmetic  6.76 us (8%)
    pallas_call x1, Pallas kernels, slab_terms_t(): pl.pallas_call(kernel, out_shape=jax.ShapeDtypeStruct((window_width, row_...  29.9 us
    ppermute x7, waiting for transfers between devices, shifted(): return lax.ppermute(value, axis, pairs)  27.6 us
    ppermute x7, starting transfers between devices, shifted(): return lax.ppermute(value, axis, pairs)  11.1 us
    concatenate x1, other arithmetic, on_device(): jnp.concatenate([lower[:, :CB], prolong_blocks, upper[:, :CB]], axis=0)  2.48 us
    unnamed x13, local copies, waits for them, and re-layouts  2.15 us
    concatenate x2, other arithmetic, with_columns(): return jnp.concatenate([blocks, columns], axis=1)  1.98 us
  transfers between devices with their start and end apart: 7, of which 7 were waited for; matrix products, arithmetic and copies ran while one was open for 3% of the time, Pallas kernels for 0%

profile of v2, /device:TPU:0, one launch (start us, length us, event | category | flops | bytes accessed | tf_op | source)
XLA Modules:
  0.0 82.4 jit_solution(11410345685971405682)
XLA Ops:
  0.0 0.8 copy.29
  0.8 0.0 copy-start.3
  0.8 0.0 copy-start.2
  0.8 1.5 %fusion.12 = (bf16[32,24,512]{2,1,0:T(8,128)(2,1)S(1)}, bf16[32,24,512]{2,1,0:T(8,128)(2,1)S(1)}) fusion(bf16[128,24,512]{2,1,0:T(8,128)(2,1)} %param.6), kind=kLoop, calls=%fused_computation.40 | loop fusion | bytes 3145728 | tf_op jit(solution)/shard_map/slice | solution.py:130
  2.3 0.2 copy.39
  2.6 1.0 %pad_maximum_fusion.2 = bf16[32,25,512]{2,0,1:T(8,128)(2,1)} fusion(bf16[32,1,512]{2,0,1:T(8,128)(2,1)S(1)} %pad_bitcast_fusion, bf16[32,24,512]{2,0,1:T(8,128)(2,1)S(1)} %copy.39), kind=kLoop, calls=%fused_computation.2 | loop fusion | flops 409600 | bytes 1638400 | tf_op jit(solution)/shard_map/concatenate | solution.py:133
  3.6 5.8 %collective-permute-start.1 = (bf16[32,25,512]{2,0,1:T(8,128)(2,1)}, bf16[32,25,512]{2,0,1:T(8,128)(2,1)}, u32[]{:S(2)}, u32[]{:S(2)}) collective-permute-start(bf16[32,25,512]{2,0,1:T(8,128)(2,1)} %pad_maximum_fusion.2), channel_id=1, source_target_pairs={{0,252},{4,0},{8,4},{12,8},{16,12},{20,16},{24,20},{28,24},{32,28}... | collective-permute-start | bytes 2457608 | tf_op jit(solution)/shard_map/ppermute | solution.py:20
  9.3 0.0 copy-start.1
  9.3 0.2 copy.38
  9.6 1.0 %pad_maximum_fusion.1 = bf16[32,25,512]{2,0,1:T(8,128)(2,1)} fusion(bf16[32,1,512]{2,0,1:T(8,128)(2,1)S(1)} %pad_bitcast_fusion.1, bf16[32,24,512]{2,0,1:T(8,128)(2,1)S(1)} %copy.38), kind=kLoop, calls=%fused_computation.1 | loop fusion | flops 409600 | bytes 1638400 | tf_op jit(solution)/shard_map/concatenate | solution.py:133
  10.6 0.0 collective-permute-start
  10.6 0.0 copy-done.3
  10.6 0.1 copy.34
  10.7 0.1 reshape.12.jloc_ref
  10.9 8.6 %collective-permute-done.1 = bf16[32,25,512]{2,0,1:T(8,128)(2,1)} collective-permute-done((bf16[32,25,512]{2,0,1:T(8,128)(2,1)}, bf16[32,25,512]{2,0,1:T(8,128)(2,1)}, u32[]{:S(2)}, u32[]{:S(2)}) %collective-permute-start.1) | collective-permute-done | bytes 819232 | tf_op jit(solution)/shard_map/ppermute | solution.py:20
  19.5 0.7 fusion.7
  20.2 0.1 copy.32
  20.3 5.7 %collective-permute-done = bf16[32,25,512]{2,0,1:T(8,128)(2,1)} collective-permute-done((bf16[32,25,512]{2,0,1:T(8,128)(2,1)}, bf16[32,25,512]{2,0,1:T(8,128)(2,1)}, u32[]{:S(2)}, u32[]{:S(2)}) %collective-permute-start) | collective-permute-done | bytes 819232 | tf_op jit(solution)/shard_map/ppermute | solution.py:20
  26.0 0.7 fusion.8
  26.7 0.1 copy.31
  26.7 0.0 copy-done.2
  26.7 0.1 pad_add_fusion
  26.8 0.1 copy.33
  26.9 0.1 concatenate.17
  27.1 1.2 %slice.51 = bf16[32,24,512]{2,0,1:T(8,128)(2,1)S(1)} slice(bf16[32,25,512]{2,0,1:T(8,128)(2,1)} %collective-permute-done.1), slice={[0:32], [0:24], [0:512]} | slice | bytes 1572864 | tf_op jit(solution)/shard_map/slice | solution.py:137
  28.3 0.4 copy.41
  28.7 1.2 %slice.50 = bf16[32,24,512]{2,0,1:T(8,128)(2,1)S(1)} slice(bf16[32,25,512]{2,0,1:T(8,128)(2,1)} %collective-permute-done), slice={[0:32], [0:24], [0:512]} | slice | bytes 1572864 | tf_op jit(solution)/shard_map/slice | solution.py:137
  29.9 0.4 copy.40
  30.4 0.0 copy-done.1
  30.4 0.0 copy-start
  30.4 2.5 %pad_maximum_fusion.pb_ref = bf16[192,24,512]{2,1,0:T(8,128)(2,1)} fusion(bf16[32,24,512]{2,1,0:T(8,128)(2,1)S(1)} %copy.41, bf16[128,24,512]{2,1,0:T(8,128)(2,1)S(1)} %copy-done.1, bf16[32,24,512]{2,1,0:T(8,128)(2,1)S(1)} %copy.40), kind=kLoop, calls=%fused_computation | loop fusion | flops 4718592 | bytes 9437184 | tf_op jit(solution)/shard_map/concatenate | solution.py:137
  32.9 0.0 copy-done
  32.9 29.9 %shard_map.46 = f32[480,288]{1,0:T(8,128)S(1)} custom-call(s32[1536]{0:T(1024)S(1)} %fusion.6.wpos_ref, s32[256]{0:T(256)S(1)} %reshape.12.jloc_ref, bf16[192,24,512]{2,1,0:T(8,128)(2,1)} %pad_maximum_fusion.pb_ref, bf16[128,64,128]{2,1,0:T(8,128)(2,1)S(1)} %copy-done), custom_call_target="tpu_custom_call" | custom-call | flops 8556380160 | bytes 7368704 | tf_op jit(solution)/shard_map/pallas_call | solution.py:95
  62.8 0.2 copy.37
  63.1 3.1 %collective-permute-start.4 = (f32[3,24,480]{2,1,0:T(8,128)S(1)}, f32[3,24,480]{2,1,0:T(8,128)S(1)}, u32[]{:S(2)}, u32[]{:S(2)}) collective-permute-start(f32[3,24,480]{2,1,0:T(8,128)S(1)} %get-tuple-element.8), channel_id=1, source_target_pairs={{0,3},{1,0},{2,1},{3,2},{4,7},{5,4},{6,5},{7,6},{8,11},{9,8},{10,9... | collective-permute-start | bytes 414728 | tf_op jit(solution)/shard_map/ppermute | solution.py:20
  66.2 0.6 collective-permute-start.3
  66.8 1.0 %collective-permute-start.2 = (f32[3,24,480]{2,1,0:T(8,128)S(1)}, f32[3,24,480]{2,1,0:T(8,128)S(1)}, u32[]{:S(2)}, u32[]{:S(2)}) collective-permute-start(f32[3,24,480]{2,1,0:T(8,128)S(1)} %get-tuple-element.7), channel_id=1, source_target_pairs={{0,1},{1,2},{2,3},{3,0},{4,5},{5,6},{6,7},{7,4},{8,9},{9,10},{10,1... | collective-permute-start | bytes 414728 | tf_op jit(solution)/shard_map/ppermute | solution.py:20
  67.8 2.7 %collective-permute-done.4 = f32[3,24,480]{2,1,0:T(8,128)S(1)} collective-permute-done((f32[3,24,480]{2,1,0:T(8,128)S(1)}, f32[3,24,480]{2,1,0:T(8,128)S(1)}, u32[]{:S(2)}, u32[]{:S(2)}) %collective-permute-start.4) | collective-permute-done | bytes 138272 | tf_op jit(solution)/shard_map/ppermute | solution.py:20
  70.5 2.5 %collective-permute-done.3 = f32[3,24,480]{2,1,0:T(8,128)S(1)} collective-permute-done((f32[3,24,480]{2,1,0:T(8,128)S(1)}, f32[3,24,480]{2,1,0:T(8,128)S(1)}, u32[]{:S(2)}, u32[]{:S(2)}) %collective-permute-start.3) | collective-permute-done | bytes 138272 | tf_op jit(solution)/shard_map/ppermute | solution.py:20
  72.9 1.5 %collective-permute-done.2 = f32[3,24,480]{2,1,0:T(8,128)S(1)} collective-permute-done((f32[3,24,480]{2,1,0:T(8,128)S(1)}, f32[3,24,480]{2,1,0:T(8,128)S(1)}, u32[]{:S(2)}, u32[]{:S(2)}) %collective-permute-start.2) | collective-permute-done | bytes 138272 | tf_op jit(solution)/shard_map/ppermute | solution.py:20
  74.4 0.1 fusion.1
  74.5 0.3 collective-permute-start.6
  74.8 0.2 collective-permute-start.5
  75.1 1.5 %collective-permute-done.6 = f32[24,480]{1,0:T(8,128)S(1)} collective-permute-done((f32[24,480]{1,0:T(8,128)S(1)}, f32[24,480]{1,0:T(8,128)S(1)}, u32[]{:S(2)}, u32[]{:S(2)}) %collective-permute-start.6) | collective-permute-done | bytes 46112 | tf_op jit(solution)/shard_map/ppermute | solution.py:20
  76.6 5.1 %collective-permute-done.5 = f32[24,480]{1,0:T(8,128)S(1)} collective-permute-done((f32[24,480]{1,0:T(8,128)S(1)}, f32[24,480]{1,0:T(8,128)S(1)}, u32[]{:S(2)}, u32[]{:S(2)}) %collective-permute-start.5) | collective-permute-done | bytes 46112 | tf_op jit(solution)/shard_map/ppermute | solution.py:20
  81.7 0.7 add_bitcast_fusion
  (8 shorter events, 0.1 us)
Async XLA Ops:
  0.8 9.7 %copy-start.3 = (s32[128,2]{0,1:T(2,128)S(1)}, s32[128,2]{0,1:T(2,128)}, u32[]{:S(2)}) copy-start(s32[128,2]{0,1:T(2,128)} %param.5) | copy-start | bytes 3076
  0.8 25.9 %copy-start.2 = (s32[128,8]{0,1:T(8,128)S(1)}, s32[128,8]{0,1:T(8,128)}, u32[]{:S(2)}) copy-start(s32[128,8]{0,1:T(8,128)} %param.7) | copy-start | bytes 12292
  3.6 15.9 %collective-permute-start.1 = (bf16[32,25,512]{2,0,1:T(8,128)(2,1)}, bf16[32,25,512]{2,0,1:T(8,128)(2,1)}, u32[]{:S(2)}, u32[]{:S(2)}) collective-permute-start(bf16[32,25,512]{2,0,1:T(8,128)(2,1)} %pad_maximum_fusion.2), channel_id=1, source_target_pairs={{0,252},{4,0},{8,4},{12,8},{16,12},{20,16},{24,20},{28,24},{32,28}... | collective-permute-start | bytes 2457608 | tf_op jit(solution)/shard_map/ppermute | solution.py:20
  9.3 21.1 %copy-start.1 = (bf16[128,24,512]{2,1,0:T(8,128)(2,1)S(1)}, bf16[128,24,512]{2,1,0:T(8,128)(2,1)}, u32[]{:S(2)}) copy-start(bf16[128,24,512]{2,1,0:T(8,128)(2,1)} %param.6) | copy-start | bytes 9437188
  10.6 15.4 %collective-permute-start = (bf16[32,25,512]{2,0,1:T(8,128)(2,1)}, bf16[32,25,512]{2,0,1:T(8,128)(2,1)}, u32[]{:S(2)}, u32[]{:S(2)}) collective-permute-start(bf16[32,25,512]{2,0,1:T(8,128)(2,1)} %pad_maximum_fusion.1), channel_id=1, source_target_pairs={{0,4},{4,8},{8,12},{12,16},{16,20},{20,24},{24,28},{28,32},{32,36}... | collective-permute-start | bytes 2457608 | tf_op jit(solution)/shard_map/ppermute | solution.py:20
  30.4 2.5 %copy-start = (bf16[128,64,128]{2,1,0:T(8,128)(2,1)S(1)}, bf16[128,64,128]{2,1,0:T(8,128)(2,1)}, u32[]{:S(2)}) copy-start(bf16[128,64,128]{2,1,0:T(8,128)(2,1)} %tb_ref.1) | copy-start | bytes 6291460
  63.1 7.4 %collective-permute-start.4 = (f32[3,24,480]{2,1,0:T(8,128)S(1)}, f32[3,24,480]{2,1,0:T(8,128)S(1)}, u32[]{:S(2)}, u32[]{:S(2)}) collective-permute-start(f32[3,24,480]{2,1,0:T(8,128)S(1)} %get-tuple-element.8), channel_id=1, source_target_pairs={{0,3},{1,0},{2,1},{3,2},{4,7},{5,4},{6,5},{7,6},{8,11},{9,8},{10,9... | collective-permute-start | bytes 414728 | tf_op jit(solution)/shard_map/ppermute | solution.py:20
  66.2 6.8 %collective-permute-start.3 = (f32[3,24,480]{2,1,0:T(8,128)S(1)}, f32[3,24,480]{2,1,0:T(8,128)S(1)}, u32[]{:S(2)}, u32[]{:S(2)}) collective-permute-start(f32[3,24,480]{2,1,0:T(8,128)S(1)} %get-tuple-element.9), channel_id=1, source_target_pairs={{0,2},{1,3},{2,0},{3,1},{4,6},{5,7},{6,4},{7,5},{8,10},{9,11},{10,... | collective-permute-start | bytes 414728 | tf_op jit(solution)/shard_map/ppermute | solution.py:20
  66.8 7.6 %collective-permute-start.2 = (f32[3,24,480]{2,1,0:T(8,128)S(1)}, f32[3,24,480]{2,1,0:T(8,128)S(1)}, u32[]{:S(2)}, u32[]{:S(2)}) collective-permute-start(f32[3,24,480]{2,1,0:T(8,128)S(1)} %get-tuple-element.7), channel_id=1, source_target_pairs={{0,1},{1,2},{2,3},{3,0},{4,5},{5,6},{6,7},{7,4},{8,9},{9,10},{10,1... | collective-permute-start | bytes 414728 | tf_op jit(solution)/shard_map/ppermute | solution.py:20
  74.5 2.1 %collective-permute-start.6 = (f32[24,480]{1,0:T(8,128)S(1)}, f32[24,480]{1,0:T(8,128)S(1)}, u32[]{:S(2)}, u32[]{:S(2)}) collective-permute-start(f32[24,480]{1,0:T(8,128)S(1)} %get-tuple-element.11), channel_id=1, source_target_pairs={{0,252},{4,0},{8,4},{12,8},{16,12},{20,16},{24,20},{28,24},{32,28}... | collective-permute-start | bytes 138248 | tf_op jit(solution)/shard_map/ppermute | solution.py:20
  74.8 6.8 %collective-permute-start.5 = (f32[24,480]{1,0:T(8,128)S(1)}, f32[24,480]{1,0:T(8,128)S(1)}, u32[]{:S(2)}, u32[]{:S(2)}) collective-permute-start(f32[24,480]{1,0:T(8,128)S(1)} %get-tuple-element.12), channel_id=1, source_target_pairs={{0,4},{4,8},{8,12},{12,16},{16,20},{20,24},{24,28},{28,32},{32,36}... | collective-permute-start | bytes 138248 | tf_op jit(solution)/shard_map/ppermute | solution.py:20

commit v3 on v2

v3 whole, which is shorter than its diff:
```python
import functools

import jax
import jax.numpy as jnp
from jax import lax
from jax.experimental import pallas as pl
from jax.experimental.pallas import tpu as pltpu
from jax.sharding import PartitionSpec as P

B = 64
CB = 24
KP = 8
NCD = 4
GROUP = 8


def shifted(value, axis, steps):
    count = lax.axis_size(axis)
    pairs = [(source, (source + steps) % count) for source in range(count)]
    return lax.ppermute(value, axis, pairs)


def widen(values, left_pad, right_pad):
    return jnp.pad(values, ((0, 0),) * (values.ndim - 1) + ((left_pad, right_pad),))


NT = (((1,), (1,)), ((), ()))


def half_masks():
    upper24 = lax.broadcasted_iota(jnp.int32, (CB, 128), 1) >= B
    upper64 = lax.broadcasted_iota(jnp.int32, (B, 128), 1) >= B
    return upper24, upper64


def place(src_ref, r, p, dst, slot, lane_group, upper, upper24):
    src = src_ref[r, 0:CB, (p // 2) * 128:(p // 2) * 128 + 128].astype(jnp.float32)
    if (p % 2 == 1) != upper:
        src = pltpu.roll(src, B, 1)
    keep = upper24 if upper else jnp.logical_not(upper24)
    rows = pl.ds(pl.multiple_of(slot * CB, 8), CB)
    lanes = slice(lane_group * 128, lane_group * 128 + 128)
    dst[rows, lanes] = dst[rows, lanes] + jnp.where(keep, src, 0.0)


def place_row_side(pb_ref, wpos_ref, wbase, i, xs_ref, m, upper24):
    for p in range(KP):
        slot = jnp.clip(wpos_ref[wbase + p] - NCD, 0, 3 * NCD - 1)
        place(pb_ref, i, p, xs_ref, slot, m // 2, m % 2 == 1, upper24)


def place_window(src_ref, r, wpos_ref, wbase, s_ref, m, upper24):
    for p in range(KP):
        slot = jnp.clip(wpos_ref[wbase + p], 0, 5 * NCD - 1)
        place(src_ref, r, p, s_ref, slot, m // 2, m % 2 == 1, upper24)


def chunk_product(s_ref, w_ref, c):
    window = s_ref[:, c * 256:(c + 1) * 256].astype(jnp.bfloat16)
    q = lax.dot_general(window, w_ref[...], NT, preferred_element_type=jnp.float32)
    return q.astype(jnp.bfloat16)


def own_kernel(halo_rows, local_k, wpos_ref, jloc_ref, pb_ref, tb_ref, gt_ref, s_ref, xs_ref, w_ref):
    row_count = pb_ref.shape[0]
    f32 = jnp.float32
    upper24, upper64 = half_masks()
    gt_ref[...] = jnp.zeros(gt_ref.shape, f32)
    w_ref[...] = jnp.zeros(w_ref.shape, jnp.bfloat16)

    def group(g, carry):
        base = g * GROUP
        xs_ref[...] = jnp.zeros(xs_ref.shape, f32)
        for m in range(GROUP):
            place_row_side(pb_ref, wpos_ref, (base + m) * KP, base + m, xs_ref, m, upper24)
        xsb = xs_ref[...].astype(jnp.bfloat16)
        for k in range(local_k):
            s_ref[...] = jnp.zeros(s_ref.shape, f32)
            for m in range(GROUP):
                r = jloc_ref[(base + m) * local_k + k] - halo_rows
                inside = jnp.logical_and(r >= 0, r < row_count)
                rr = jnp.clip(r, 0, row_count - 1)

                @pl.when(inside)
                def _():
                    place_window(pb_ref, rr, wpos_ref, rr * KP, s_ref, m, upper24)

            parts = []
            for c in range(GROUP // 4):
                for mm in range(4):
                    t = tb_ref[base + 4 * c + mm].astype(f32)
                    if (k % 2 == 1) != (mm % 2 == 1):
                        t = pltpu.roll(t, B, 1)
                    keep = upper64 if mm % 2 == 1 else jnp.logical_not(upper64)
                    w_ref[mm * B:(mm + 1) * B, (mm // 2) * 128:(mm // 2) * 128 + 128] = jnp.where(
                        keep, t, 0.0
                    ).astype(jnp.bfloat16)
                parts.append(chunk_product(s_ref, w_ref, c))
            qt = jnp.concatenate(parts, axis=1)
            gt_ref[...] += lax.dot_general(qt, xsb, NT, preferred_element_type=f32)
        return carry

    lax.fori_loop(0, row_count // GROUP, group, 0)


def halo_kernel(halo_rows, local_k, count_ref, list_ref, wpos_ref, jloc_ref, pb_ref, lo_ref, up_ref,
                tb_ref, ga_ref, gt_ref, s_ref, xs_ref, w_ref):
    row_count = pb_ref.shape[0]
    f32 = jnp.float32
    upper24, upper64 = half_masks()
    gt_ref[...] = ga_ref[...]

    def group(g, carry):
        s_ref[...] = jnp.zeros(s_ref.shape, f32)
        xs_ref[...] = jnp.zeros(xs_ref.shape, f32)
        parts = []
        for c in range(GROUP // 4):
            for mm in range(4):
                m = 4 * c + mm
                pair = list_ref[g * GROUP + m]
                valid = pair >= 0
                pc = jnp.maximum(pair, 0)
                i = pc // local_k
                k = pc % local_k
                r = jloc_ref[pc]
                t = tb_ref[i].astype(f32)
                same = (k % 2) == (mm % 2)
                t = jnp.where(same, t, pltpu.roll(t, B, 1))
                keep = upper64 if mm % 2 == 1 else jnp.logical_not(upper64)
                keep = jnp.logical_and(keep, valid)
                w_ref[mm * B:(mm + 1) * B, (mm // 2) * 128:(mm // 2) * 128 + 128] = jnp.where(
                    keep, t, 0.0
                ).astype(jnp.bfloat16)

                @pl.when(valid)
                def _():
                    place_row_side(pb_ref, wpos_ref, (i + halo_rows) * KP, i, xs_ref, m, upper24)

                    @pl.when(r < halo_rows)
                    def _():
                        rl = jnp.clip(r, 0, halo_rows - 1)
                        place_window(lo_ref, rl, wpos_ref, r * KP, s_ref, m, upper24)

                    @pl.when(r >= halo_rows + row_count)
                    def _():
                        ru = jnp.clip(r - halo_rows - row_count, 0, halo_rows - 1)
                        place_window(up_ref, ru, wpos_ref, r * KP, s_ref, m, upper24)

            parts.append(chunk_product(s_ref, w_ref, c))
        qt = jnp.concatenate(parts, axis=1)
        xsb = xs_ref[...].astype(jnp.bfloat16)
        gt_ref[...] += lax.dot_general(qt, xsb, NT, preferred_element_type=f32)
        return carry

    lax.fori_loop(0, count_ref[0], group, 0)


def scratch():
    return [
        pltpu.VMEM((5 * NCD * CB, GROUP * B), jnp.float32),
        pltpu.VMEM((3 * NCD * CB, GROUP * B), jnp.float32),
        pltpu.VMEM((256, 256), jnp.bfloat16),
    ]


def own_terms(wpos_own, jloc, pb, tb, halo_rows):
    local_k = tb.shape[2] // B
    row_count = pb.shape[0]
    shape = (5 * NCD * CB, 3 * NCD * CB)
    flops = 2 * row_count * local_k * shape[0] * (256 + shape[1]) * B
    smem = pl.BlockSpec(memory_space=pltpu.SMEM)
    vmem = pl.BlockSpec(memory_space=pltpu.VMEM)
    return pl.pallas_call(
        functools.partial(own_kernel, halo_rows, local_k),
        out_shape=jax.ShapeDtypeStruct(shape, jnp.float32),
        in_specs=[smem, smem, vmem, vmem],
        out_specs=vmem,
        scratch_shapes=scratch(),
        compiler_params=pltpu.CompilerParams(vmem_limit_bytes=48 * 1024 * 1024),
        cost_estimate=pl.CostEstimate(
            flops=flops, bytes_accessed=pb.size * 2 + tb.size * 2 + shape[0] * shape[1] * 4,
            transcendentals=0,
        ),
    )(wpos_own, jloc, pb, tb)


def halo_terms(count, pair_list, wpos, jloc, pb, lower, upper, tb, own_part, halo_rows):
    local_k = tb.shape[2] // B
    shape = own_part.shape
    smem = pl.BlockSpec(memory_space=pltpu.SMEM)
    vmem = pl.BlockSpec(memory_space=pltpu.VMEM)
    flops = 2 * pair_list.shape[0] // 2 * shape[0] * (256 + shape[1]) * B
    return pl.pallas_call(
        functools.partial(halo_kernel, halo_rows, local_k),
        out_shape=jax.ShapeDtypeStruct(shape, jnp.float32),
        in_specs=[smem, smem, smem, smem, vmem, vmem, vmem, vmem, vmem],
        out_specs=vmem,
        scratch_shapes=scratch(),
        compiler_params=pltpu.CompilerParams(vmem_limit_bytes=48 * 1024 * 1024),
        cost_estimate=pl.CostEstimate(
            flops=flops, bytes_accessed=pb.size * 2 + tb.size * 2 + shape[0] * shape[1] * 8,
            transcendentals=0,
        ),
    )(count, pair_list, wpos, jloc, pb, lower, upper, tb, own_part)


def on_device(tangent_blocks, tangent_columns, prolong_blocks, prolong_columns):
    slab_count = lax.axis_size("blk")
    slab_index = lax.axis_index("blk")
    lane_count = lax.axis_size("lane")
    lane_index = lax.axis_index("lane")
    row_count = prolong_blocks.shape[0]
    halo_rows = row_count // 4
    coarse_width = NCD * CB
    fine_count = row_count * slab_count

    def with_columns(rows):
        blocks = prolong_blocks[rows]
        columns = prolong_columns[rows].astype(jnp.bfloat16)
        columns = jnp.pad(columns, ((0, 0), (0, blocks.shape[2] - KP)))[:, None, :]
        return jnp.concatenate([blocks, columns], axis=1)

    lower = shifted(with_columns(slice(row_count - halo_rows, row_count)), "blk", 1)
    upper = shifted(with_columns(slice(0, halo_rows)), "blk", -1)

    def window_slots(columns):
        slots = ((columns // NCD - slab_index + 2) % slab_count) * NCD + columns % NCD
        return slots.astype(jnp.int32)

    wpos_own = window_slots(prolong_columns)
    jloc = (tangent_columns - slab_index * row_count + halo_rows) % fine_count
    jloc = jnp.clip(jloc, 0, row_count + 2 * halo_rows - 1).astype(jnp.int32).reshape(-1)

    own_part = own_terms(wpos_own.reshape(-1), jloc, prolong_blocks, tangent_blocks, halo_rows)

    pair_count = jloc.shape[0]
    in_halo = jnp.logical_or(jloc < halo_rows, jloc >= halo_rows + row_count)
    order = jnp.cumsum(in_halo.astype(jnp.int32)) - 1
    slots = jnp.arange(pair_count, dtype=jnp.int32)
    match = jnp.logical_and(in_halo[None, :], order[None, :] == slots[:, None])
    pair_list = jnp.where(
        jnp.any(match, axis=1), jnp.sum(jnp.where(match, slots[None, :], 0), axis=1), -1
    ).astype(jnp.int32)
    halo_count = jnp.sum(in_halo.astype(jnp.int32))
    group_count = ((halo_count + GROUP - 1) // GROUP).astype(jnp.int32).reshape(1)

    lower_columns = lower[:, CB, :KP].astype(jnp.int32)
    upper_columns = upper[:, CB, :KP].astype(jnp.int32)
    wpos = jnp.concatenate(
        [window_slots(lower_columns), wpos_own, window_slots(upper_columns)], axis=0
    ).reshape(-1)
    gt = halo_terms(group_count, pair_list, wpos, jloc, prolong_blocks, lower, upper,
                    tangent_blocks, own_part, halo_rows)
    terms = gt.T.reshape(3, NCD, CB, 5 * coarse_width)

    shares = lax.dynamic_index_in_dim(terms, lane_index, axis=1, keepdims=False)
    for step in range(1, lane_count):
        piece = lax.dynamic_index_in_dim(
            terms, (lane_index + step) % lane_count, axis=1, keepdims=False
        )
        shares = shares + shifted(piece, "lane", step)
    from_lower = shifted(shares[2], "blk", 1)
    from_upper = shifted(shares[0], "blk", -1)
    coarse_band = (
        widen(shares[1], coarse_width, coarse_width)
        + widen(from_lower, 0, 2 * coarse_width)
        + widen(from_upper, 2 * coarse_width, 0)
    )
    return coarse_band[None]


def solution(mesh):
    return jax.shard_map(
        on_device,
        mesh=mesh,
        in_specs=(P("blk", None, "lane"), P("blk", "lane"), P("blk", None, None), P("blk", None)),
        out_specs=P(("blk", "lane"), None, None),
        check_vma=False,
    )
```

time: 82.8 us -> 131 us (1.58)
  Pallas kernels: 29.9 us -> 69.2 us
  starting transfers between devices: 11.1 us -> 30.4 us
  waiting for transfers between devices: 27.6 us -> 13.8 us
  local copies, waits for them, and re-layouts: 6.95 us -> 10 us
    pallas_call x1 -> x2, Pallas kernels: 29.9 us -> 69.2 us  [the longest x1 52.5 us: own_terms(): pl.pallas_call(functools.partial(own_kernel, halo_rows, local_k), out_sha...]
    ppermute x7, starting transfers between devices: 11.1 us -> 30.4 us  [shifted(): return lax.ppermute(value, axis, pairs)]
    ppermute x7, waiting for transfers between devices: 27.6 us -> 13.8 us  [shifted(): return lax.ppermute(value, axis, pairs)]
    ppermute x0 -> x2, local copies, waits for them, and re-layouts: none -> 3.29 us  [shifted(): return lax.ppermute(value, axis, pairs)]
    concatenate x2 -> x1, other arithmetic: 2.55 us -> 0.08 us  [on_device(): jnp.concatenate([window_slots(lower_columns), wpos_own, window_slots(uppe...]
    slice x2 -> x1, local copies, waits for them, and re-layouts: 2.4 us -> 0.07 us  [the longest x1 1.2 us: on_device(): lower[:, :CB]]
    add x1 -> x3, other arithmetic: 0.03 us -> 1.64 us  [window_slots(): slots = (columns // NCD - slab_index + 2) % slab_count * NCD + columns % NCD]
    unnamed x13 -> x17, local copies, waits for them, and re-layouts: 2.15 us -> 3.72 us
  transfers between devices with their start and end apart: 7 -> 7, of which waited for: 7 -> 5; matrix products, arithmetic and copies ran while one was open for 3% -> 3% of each run, Pallas kernels for 0% -> 40%
where the time goes in v3:
time: 131 us; the launch traced here: 130 us
  Pallas kernels  69.2 us (53%)
  starting transfers between devices  30.4 us (23%)
  waiting for transfers between devices  13.8 us (11%)
  local copies, waits for them, and re-layouts  10 us (8%)
  other arithmetic  5.78 us (4%)
    pallas_call x1, Pallas kernels, own_terms(): pl.pallas_call(functools.partial(own_kernel, halo_rows, local_k), out_sha...  52.5 us
    ppermute x7, starting transfers between devices, shifted(): return lax.ppermute(value, axis, pairs)  30.4 us
    pallas_call x1, Pallas kernels, halo_terms(): pl.pallas_call(functools.partial(halo_kernel, halo_rows, local_k), out_sh...  16.7 us
    ppermute x7, waiting for transfers between devices, shifted(): return lax.ppermute(value, axis, pairs)  13.8 us
    unnamed x17, local copies, waits for them, and re-layouts  3.72 us
    ppermute x2, local copies, waits for them, and re-layouts, shifted(): return lax.ppermute(value, axis, pairs)  3.29 us
  transfers between devices with their start and end apart: 7, of which 5 were waited for; matrix products, arithmetic and copies ran while one was open for 3% of the time, Pallas kernels for 40%

profile of v3, /device:TPU:0, one launch (start us, length us, event | category | flops | bytes accessed | tf_op | source)
XLA Modules:
  0.0 130.1 jit_solution(5607415733675540678)
XLA Ops:
  0.0 0.8 copy.62
  0.8 1.5 %fusion.32 = (bf16[32,24,512]{2,1,0:T(8,128)(2,1)S(1)}, bf16[32,24,512]{2,1,0:T(8,128)(2,1)S(1)}) fusion(bf16[128,24,512]{2,1,0:T(8,128)(2,1)} %pb_ref.3), kind=kLoop, calls=%fused_computation.87 | loop fusion | bytes 3145728 | tf_op jit(solution)/shard_map/slice | solution.py:218
  2.3 0.0 copy-start.6
  2.3 0.0 copy-start.5
  2.3 0.0 copy-start
  2.3 0.2 copy.72
  2.6 1.0 pad_maximum_fusion.1
  3.6 5.8 %collective-permute-start.1 = (bf16[32,25,512]{2,0,1:T(8,128)(2,1)}, bf16[32,25,512]{2,0,1:T(8,128)(2,1)}, u32[]{:S(2)}, u32[]{:S(2)}) collective-permute-start(bf16[32,25,512]{2,0,1:T(8,128)(2,1)} %pad_maximum_fusion.1), channel_id=1, source_target_pairs={{0,252},{4,0},{8,4},{12,8},{16,12},{20,16},{24,20},{28,24},{32,28}... | collective-permute-start | bytes 2457608 | tf_op jit(solution)/shard_map/ppermute | solution.py:20
  9.3 0.2 copy.71
  9.6 1.0 pad_maximum_fusion
  10.5 0.0 collective-permute-start
  10.5 0.0 copy-done.6
  10.5 0.1 copy.60
  10.7 0.1 reshape.69
  10.8 0.3 reduce-window.9
  11.1 0.1 slice.36
  11.2 0.1 slice_reduce_fusion
  11.3 0.1 add_bitcast_fusion.1
  11.4 0.1 copy.59
  11.5 0.1 reshape.64.jloc_ref
  11.7 0.1 fusion.1
  11.8 0.1 select_reduce_fusion
  11.9 0.0 copy-done.5
  12.0 0.6 fusion.30
  13.3 0.1 copy.67
  13.4 0.1 reshape.67.wpos_ref
  13.6 0.0 copy-done
  13.6 0.0 copy-start.1
  13.6 1.6 %copy-done.1 = bf16[128,64,128]{2,1,0:T(8,128)(2,1)S(1)} copy-done((bf16[128,64,128]{2,1,0:T(8,128)(2,1)S(1)}, bf16[128,64,128]{2,1,0:T(8,128)(2,1)}, u32[]{:S(2)}) %copy-start.1) | copy-done | bytes 2097176
  15.2 52.5 %shard_map.46.ga_ref = f32[480,288]{1,0:T(8,128)S(1)} custom-call(s32[1024]{0:T(1024)S(1)} %reshape.67.wpos_ref, s32[256]{0:T(256)S(1)} %reshape.64.jloc_ref, bf16[128,24,512]{2,1,0:T(8,128)(2,1)S(1)} %copy-done, bf16[128,64,128]{2,1,0:T(8,128)(2,1)S(1)} %copy-done.1), custom_call_target="tpu_custom_call" | custom-call | flops 8556380160 | bytes 5795840 | tf_op jit(solution)/shard_map/pallas_call | solution.py:173
  67.7 0.0 copy-start.3
  67.7 0.9 copy-done.3
  68.6 0.0 copy-start.2
  68.6 0.0 collective-permute-done.1
  68.6 0.9 fusion.17
  69.5 0.1 copy.65
  69.5 0.0 collective-permute-done
  69.5 0.7 fusion.12
  70.3 0.1 copy.64
  70.3 0.1 pad_add_fusion
  70.4 0.1 copy.66
  70.5 0.1 reshape.66.wpos_ref
  70.6 0.0 copy-start.4
  70.7 1.7 %copy.68.lo_ref = bf16[32,25,512]{2,1,0:T(8,128)(2,1)S(1)} copy(bf16[32,25,512]{2,0,1:T(8,128)(2,1)} %collective-permute-done) | data formatting | bytes 1638400 | tf_op jit(solution)/shard_map/ppermute | solution.py:20
  72.3 1.6 %copy.69.up_ref = bf16[32,25,512]{2,1,0:T(8,128)(2,1)S(1)} copy(bf16[32,25,512]{2,0,1:T(8,128)(2,1)} %collective-permute-done.1) | data formatting | bytes 1638400 | tf_op jit(solution)/shard_map/ppermute | solution.py:20
  74.0 0.0 copy-done.2
  74.0 0.0 copy-done.4
  74.0 16.7 %shard_map.47 = f32[480,288]{1,0:T(8,128)S(1)} custom-call(s32[1]{0:T(128)} %bitcast.count_ref, s32[256]{0:T(256)S(1)} %broadcast_select_fusion.list_ref, s32[1536]{0:T(1024)S(1)} %reshape.66.wpos_ref, s32[256]{0:T(256)S(1)} %reshape.64.jloc_ref, bf16[128,24,512]{2,1,0:T(8,128)(2,1)} %pb_ref.3, bf16[32,25,512]{2,1,0:T(8,128)(2,1)S(1)} %copy.68.lo_ref, ...), custom_call_target="tpu_custom_call" | custom-call | flops 4278190080 | bytes 6348800 | tf_op jit(solution)/shard_map/pallas_call | solution.py:193
  90.6 0.2 copy.70
  90.9 21.6 %collective-permute-start.4 = (f32[3,24,480]{2,1,0:T(8,128)S(1)}, f32[3,24,480]{2,1,0:T(8,128)S(1)}, u32[]{:S(2)}, u32[]{:S(2)}) collective-permute-start(f32[3,24,480]{2,1,0:T(8,128)S(1)} %get-tuple-element.10), channel_id=1, source_target_pairs={{0,3},{1,0},{2,1},{3,2},{4,7},{5,4},{6,5},{7,6},{8,11},{9,8},{10,9... | collective-permute-start | bytes 414728 | tf_op jit(solution)/shard_map/ppermute | solution.py:20
  112.6 0.0 collective-permute-start.3
  112.6 1.0 collective-permute-start.2
  113.5 3.3 %collective-permute-done.4 = f32[3,24,480]{2,1,0:T(8,128)S(1)} collective-permute-done((f32[3,24,480]{2,1,0:T(8,128)S(1)}, f32[3,24,480]{2,1,0:T(8,128)S(1)}, u32[]{:S(2)}, u32[]{:S(2)}) %collective-permute-start.4) | collective-permute-done | bytes 138272 | tf_op jit(solution)/shard_map/ppermute | solution.py:20
  116.9 2.5 %collective-permute-done.3 = f32[3,24,480]{2,1,0:T(8,128)S(1)} collective-permute-done((f32[3,24,480]{2,1,0:T(8,128)S(1)}, f32[3,24,480]{2,1,0:T(8,128)S(1)}, u32[]{:S(2)}, u32[]{:S(2)}) %collective-permute-start.3) | collective-permute-done | bytes 138272 | tf_op jit(solution)/shard_map/ppermute | solution.py:20
  119.3 1.2 collective-permute-done.2
  120.6 2.0 %collective-permute-start.6 = (f32[24,480]{1,0:T(8,128)S(1)}, f32[24,480]{1,0:T(8,128)S(1)}, u32[]{:S(2)}, u32[]{:S(2)}) collective-permute-start(f32[24,480]{1,0:T(8,128)S(1)} %get-tuple-element.13), channel_id=1, source_target_pairs={{0,252},{4,0},{8,4},{12,8},{16,12},{20,16},{24,20},{28,24},{32,28}... | collective-permute-start | bytes 138248 | tf_op jit(solution)/shard_map/ppermute | solution.py:20
  122.6 0.0 collective-permute-start.5
  122.6 1.7 %collective-permute-done.6 = f32[24,480]{1,0:T(8,128)S(1)} collective-permute-done((f32[24,480]{1,0:T(8,128)S(1)}, f32[24,480]{1,0:T(8,128)S(1)}, u32[]{:S(2)}, u32[]{:S(2)}) %collective-permute-start.6) | collective-permute-done | bytes 46112 | tf_op jit(solution)/shard_map/ppermute | solution.py:20
  124.3 5.1 %collective-permute-done.5 = f32[24,480]{1,0:T(8,128)S(1)} collective-permute-done((f32[24,480]{1,0:T(8,128)S(1)}, f32[24,480]{1,0:T(8,128)S(1)}, u32[]{:S(2)}, u32[]{:S(2)}) %collective-permute-start.5) | collective-permute-done | bytes 46112 | tf_op jit(solution)/shard_map/ppermute | solution.py:20
  129.4 0.7 add_bitcast_fusion
  (12 shorter events, 0.2 us)
Async XLA Ops:
  2.3 8.2 %copy-start.6 = (s32[128,2]{0,1:T(2,128)S(1)}, s32[128,2]{0,1:T(2,128)}, u32[]{:S(2)}) copy-start(s32[128,2]{0,1:T(2,128)} %param.5) | copy-start | bytes 3076
  2.3 9.6 %copy-start.5 = (s32[128,8]{0,1:T(8,128)S(1)}, s32[128,8]{0,1:T(8,128)}, u32[]{:S(2)}) copy-start(s32[128,8]{0,1:T(8,128)} %param.7) | copy-start | bytes 12292
  2.3 11.2 %copy-start = (bf16[128,24,512]{2,1,0:T(8,128)(2,1)S(1)}, bf16[128,24,512]{2,1,0:T(8,128)(2,1)}, u32[]{:S(2)}) copy-start(bf16[128,24,512]{2,1,0:T(8,128)(2,1)} %pb_ref.3) | copy-start | bytes 9437188
  3.6 65.0 %collective-permute-start.1 = (bf16[32,25,512]{2,0,1:T(8,128)(2,1)}, bf16[32,25,512]{2,0,1:T(8,128)(2,1)}, u32[]{:S(2)}, u32[]{:S(2)}) collective-permute-start(bf16[32,25,512]{2,0,1:T(8,128)(2,1)} %pad_maximum_fusion.1), channel_id=1, source_target_pairs={{0,252},{4,0},{8,4},{12,8},{16,12},{20,16},{24,20},{28,24},{32,28}... | collective-permute-start | bytes 2457608 | tf_op jit(solution)/shard_map/ppermute | solution.py:20
  10.5 59.0 %collective-permute-start = (bf16[32,25,512]{2,0,1:T(8,128)(2,1)}, bf16[32,25,512]{2,0,1:T(8,128)(2,1)}, u32[]{:S(2)}, u32[]{:S(2)}) collective-permute-start(bf16[32,25,512]{2,0,1:T(8,128)(2,1)} %pad_maximum_fusion), channel_id=1, source_target_pairs={{0,4},{4,8},{8,12},{12,16},{16,20},{20,24},{24,28},{28,32},{32,36}... | collective-permute-start | bytes 2457608 | tf_op jit(solution)/shard_map/ppermute | solution.py:20
  13.6 1.6 %copy-start.1 = (bf16[128,64,128]{2,1,0:T(8,128)(2,1)S(1)}, bf16[128,64,128]{2,1,0:T(8,128)(2,1)}, u32[]{:S(2)}) copy-start(bf16[128,64,128]{2,1,0:T(8,128)(2,1)} %tb_ref.3) | copy-start | bytes 6291460
  67.7 0.9 copy-start.3
  68.6 5.4 %copy-start.2 = (bf16[128,64,128]{2,1,0:T(8,128)(2,1)S(1)}, bf16[128,64,128]{2,1,0:T(8,128)(2,1)}, u32[]{:S(2)}) copy-start(bf16[128,64,128]{2,1,0:T(8,128)(2,1)} %tb_ref.3) | copy-start | bytes 6291460
  70.6 3.3 %copy-start.4 = (f32[480,288]{1,0:T(8,128)S(1)}, f32[480,288]{1,0:T(8,128)}, u32[]{:S(2)}) copy-start(f32[480,288]{1,0:T(8,128)} %copy-done.3) | copy-start | bytes 1658884
  90.9 25.9 %collective-permute-start.4 = (f32[3,24,480]{2,1,0:T(8,128)S(1)}, f32[3,24,480]{2,1,0:T(8,128)S(1)}, u32[]{:S(2)}, u32[]{:S(2)}) collective-permute-start(f32[3,24,480]{2,1,0:T(8,128)S(1)} %get-tuple-element.10), channel_id=1, source_target_pairs={{0,3},{1,0},{2,1},{3,2},{4,7},{5,4},{6,5},{7,6},{8,11},{9,8},{10,9... | collective-permute-start | bytes 414728 | tf_op jit(solution)/shard_map/ppermute | solution.py:20
  112.6 6.8 %collective-permute-start.3 = (f32[3,24,480]{2,1,0:T(8,128)S(1)}, f32[3,24,480]{2,1,0:T(8,128)S(1)}, u32[]{:S(2)}, u32[]{:S(2)}) collective-permute-start(f32[3,24,480]{2,1,0:T(8,128)S(1)} %get-tuple-element.11), channel_id=1, source_target_pairs={{0,2},{1,3},{2,0},{3,1},{4,6},{5,7},{6,4},{7,5},{8,10},{9,11},{10,... | collective-permute-start | bytes 414728 | tf_op jit(solution)/shard_map/ppermute | solution.py:20
  112.6 7.9 %collective-permute-start.2 = (f32[3,24,480]{2,1,0:T(8,128)S(1)}, f32[3,24,480]{2,1,0:T(8,128)S(1)}, u32[]{:S(2)}, u32[]{:S(2)}) collective-permute-start(f32[3,24,480]{2,1,0:T(8,128)S(1)} %get-tuple-element.9), channel_id=1, source_target_pairs={{0,1},{1,2},{2,3},{3,0},{4,5},{5,6},{6,7},{7,4},{8,9},{9,10},{10,1... | collective-permute-start | bytes 414728 | tf_op jit(solution)/shard_map/ppermute | solution.py:20
  120.6 3.7 %collective-permute-start.6 = (f32[24,480]{1,0:T(8,128)S(1)}, f32[24,480]{1,0:T(8,128)S(1)}, u32[]{:S(2)}, u32[]{:S(2)}) collective-permute-start(f32[24,480]{1,0:T(8,128)S(1)} %get-tuple-element.13), channel_id=1, source_target_pairs={{0,252},{4,0},{8,4},{12,8},{16,12},{20,16},{24,20},{28,24},{32,28}... | collective-permute-start | bytes 138248 | tf_op jit(solution)/shard_map/ppermute | solution.py:20
  122.6 6.8 %collective-permute-start.5 = (f32[24,480]{1,0:T(8,128)S(1)}, f32[24,480]{1,0:T(8,128)S(1)}, u32[]{:S(2)}, u32[]{:S(2)}) collective-permute-start(f32[24,480]{1,0:T(8,128)S(1)} %get-tuple-element.14), channel_id=1, source_target_pairs={{0,4},{4,8},{8,12},{12,16},{16,20},{20,24},{24,28},{28,32},{32,36}... | collective-permute-start | bytes 138248 | tf_op jit(solution)/shard_map/ppermute | solution.py:20

commit v4 on v0

--- a/solution.py
+++ b/solution.py
@@ -42,7 +42,7 @@
         keep = upper24 if upper else jnp.logical_not(upper24)
         rows = pl.ds(pl.multiple_of(slot * CB, 8), CB)
         lanes = slice(lane_group * 128, lane_group * 128 + 128)
-        dst[rows, lanes] = dst[rows, lanes] + jnp.where(keep, src, 0.0)
+        pltpu.store(dst.at[rows, lanes], src, mask=keep)
 
     def group(g, carry):
         base = g * GROUP

time: 78.1 us -> 76.2 us (0.976)
  Pallas kernels: 29.9 us -> 28 us
    pallas_call x1, Pallas kernels: 29.9 us -> 28 us  [slab_terms_t(): pl.pallas_call(kernel, out_shape=jax.ShapeDtypeStruct((window_width, row_...]
where the time goes in v4:
time: 76.2 us; the launch traced here: 76 us
  Pallas kernels  28 us (37%)
  waiting for transfers between devices  21.4 us (28%)
  starting transfers between devices  16.1 us (21%)
  other arithmetic  5.98 us (8%)
  local copies, waits for them, and re-layouts  4.4 us (6%)
    pallas_call x1, Pallas kernels, slab_terms_t(): pl.pallas_call(kernel, out_shape=jax.ShapeDtypeStruct((window_width, row_...  28 us
    ppermute x9, waiting for transfers between devices, shifted(): return lax.ppermute(value, axis, pairs)  21.4 us
    ppermute x9, starting transfers between devices, shifted(): return lax.ppermute(value, axis, pairs)  16.1 us
    concatenate x1, other arithmetic, on_device(): jnp.concatenate([lower_blocks, prolong_blocks, upper_blocks], axis=0)  3.72 us
    slice x1, local copies, waits for them, and re-layouts, on_device(): lower_blocks = shifted(prolong_blocks[row_count - halo_rows:], 'blk', 1)  2.8 us
  transfers between devices with their start and end apart: 9, of which 7 were waited for; matrix products, arithmetic and copies ran while one was open for 4% of the time, Pallas kernels for 0%

profile of v4, /device:TPU:0, one launch (start us, length us, event | category | flops | bytes accessed | tf_op | source)
XLA Modules:
  0.0 76.0 jit_solution(5067363515385909094)
XLA Ops:
  0.0 0.0 copy-start.1
  0.0 2.8 %fusion.10 = (bf16[32,24,512]{2,1,0:T(8,128)(2,1)}, bf16[32,24,512]{2,1,0:T(8,128)(2,1)}) fusion(bf16[128,24,512]{2,1,0:T(8,128)(2,1)} %param.6), kind=kLoop, calls=%fused_computation.32 | loop fusion | bytes 3145728 | tf_op jit(solution)/shard_map/slice | solution.py:129
  2.8 5.8 %collective-permute-start.3 = (bf16[32,24,512]{2,1,0:T(8,128)(2,1)}, bf16[32,24,512]{2,1,0:T(8,128)(2,1)}, u32[]{:S(2)}, u32[]{:S(2)}) collective-permute-start(bf16[32,24,512]{2,1,0:T(8,128)(2,1)} %get-tuple-element.6), channel_id=1, source_target_pairs={{0,252},{4,0},{8,4},{12,8},{16,12},{20,16},{24,20},{28,24},{32,28}... | collective-permute-start | bytes 2359304 | tf_op jit(solution)/shard_map/ppermute | solution.py:20
  8.6 0.0 collective-permute-start.2
  8.6 0.8 %fusion.11 = (s32[32,8]{0,1:T(8,128)S(1)}, s32[32,8]{0,1:T(8,128)S(1)}) fusion(s32[128,8]{0,1:T(8,128)} %param.7), kind=kLoop, calls=%fused_computation.33 | loop fusion | bytes 4096 | tf_op jit(solution)/shard_map/slice | solution.py:131
  9.4 5.1 %collective-permute-start.1 = (s32[32,8]{0,1:T(8,128)S(1)}, s32[32,8]{0,1:T(8,128)S(1)}, u32[]{:S(2)}, u32[]{:S(2)}) collective-permute-start(s32[32,8]{0,1:T(8,128)S(1)} %get-tuple-element.14), channel_id=1, source_target_pairs={{0,252},{4,0},{8,4},{12,8},{16,12},{20,16},{24,20},{28,24},{32,28}... | collective-permute-start | bytes 3080 | tf_op jit(solution)/shard_map/ppermute | solution.py:20
  14.5 0.0 collective-permute-start
  14.5 0.7 fusion.8
  15.2 0.1 copy.10
  15.3 0.1 reshape.8.jloc_ref
  15.4 3.0 %collective-permute-done.1 = s32[32,8]{0,1:T(8,128)S(1)} collective-permute-done((s32[32,8]{0,1:T(8,128)S(1)}, s32[32,8]{0,1:T(8,128)S(1)}, u32[]{:S(2)}, u32[]{:S(2)}) %collective-permute-start.1) | collective-permute-done | bytes 1056 | tf_op jit(solution)/shard_map/ppermute | solution.py:20
  18.4 5.2 %collective-permute-done = s32[32,8]{0,1:T(8,128)S(1)} collective-permute-done((s32[32,8]{0,1:T(8,128)S(1)}, s32[32,8]{0,1:T(8,128)S(1)}, u32[]{:S(2)}, u32[]{:S(2)}) %collective-permute-start) | collective-permute-done | bytes 1056 | tf_op jit(solution)/shard_map/ppermute | solution.py:20
  23.6 0.8 %pad_add_fusion = s32[192,8]{0,1:T(8,128)S(1)} fusion(s32[32,8]{0,1:T(8,128)S(1)} %collective-permute-done.1, s32[128,8]{0,1:T(8,128)} %param.7, s32[32,8]{0,1:T(8,128)S(1)} %collective-permute-done), kind=kLoop, calls=%fused_computation.24 | loop fusion | flops 3072 | bytes 12288 | tf_op jit(solution)/shard_map/concatenate | solution.py:134
  24.4 0.1 copy.9
  24.5 0.1 concatenate.9
  24.6 0.0 copy-start
  24.6 0.0 collective-permute-done.3
  24.7 0.0 collective-permute-done.2
  24.7 0.0 copy-done.1
  24.7 3.7 %pad_maximum_fusion.pb_ref = bf16[192,24,512]{2,1,0:T(8,128)(2,1)} fusion(bf16[32,24,512]{2,1,0:T(8,128)(2,1)} %collective-permute-done.3, bf16[128,24,512]{2,1,0:T(8,128)(2,1)S(1)} %copy-done.1, bf16[32,24,512]{2,1,0:T(8,128)(2,1)} %collective-permute-done.2), kind=kLoop, calls=%fused_computation | loop fusion | flops 4718592 | bytes 9437184 | tf_op jit(solution)/shard_map/concatenate | solution.py:133
  28.4 0.0 copy-done
  28.4 28.0 %shard_map.46 = f32[480,288]{1,0:T(8,128)S(1)} custom-call(s32[1536]{0:T(1024)S(1)} %fusion.6.wpos_ref, s32[256]{0:T(256)S(1)} %reshape.8.jloc_ref, bf16[192,24,512]{2,1,0:T(8,128)(2,1)} %pad_maximum_fusion.pb_ref, bf16[128,64,128]{2,1,0:T(8,128)(2,1)S(1)} %copy-done), custom_call_target="tpu_custom_call" | custom-call | flops 8556380160 | bytes 7368704 | tf_op jit(solution)/shard_map/pallas_call | solution.py:95
  56.4 0.2 copy.11
  56.7 3.1 %collective-permute-start.6 = (f32[3,24,480]{2,1,0:T(8,128)S(1)}, f32[3,24,480]{2,1,0:T(8,128)S(1)}, u32[]{:S(2)}, u32[]{:S(2)}) collective-permute-start(f32[3,24,480]{2,1,0:T(8,128)S(1)} %get-tuple-element.8), channel_id=1, source_target_pairs={{0,3},{1,0},{2,1},{3,2},{4,7},{5,4},{6,5},{7,6},{8,11},{9,8},{10,9... | collective-permute-start | bytes 414728 | tf_op jit(solution)/shard_map/ppermute | solution.py:20
  59.8 0.6 collective-permute-start.5
  60.4 1.0 %collective-permute-start.4 = (f32[3,24,480]{2,1,0:T(8,128)S(1)}, f32[3,24,480]{2,1,0:T(8,128)S(1)}, u32[]{:S(2)}, u32[]{:S(2)}) collective-permute-start(f32[3,24,480]{2,1,0:T(8,128)S(1)} %get-tuple-element.7), channel_id=1, source_target_pairs={{0,1},{1,2},{2,3},{3,0},{4,5},{5,6},{6,7},{7,4},{8,9},{9,10},{10,1... | collective-permute-start | bytes 414728 | tf_op jit(solution)/shard_map/ppermute | solution.py:20
  61.4 2.7 %collective-permute-done.6 = f32[3,24,480]{2,1,0:T(8,128)S(1)} collective-permute-done((f32[3,24,480]{2,1,0:T(8,128)S(1)}, f32[3,24,480]{2,1,0:T(8,128)S(1)}, u32[]{:S(2)}, u32[]{:S(2)}) %collective-permute-start.6) | collective-permute-done | bytes 138272 | tf_op jit(solution)/shard_map/ppermute | solution.py:20
  64.1 2.5 %collective-permute-done.5 = f32[3,24,480]{2,1,0:T(8,128)S(1)} collective-permute-done((f32[3,24,480]{2,1,0:T(8,128)S(1)}, f32[3,24,480]{2,1,0:T(8,128)S(1)}, u32[]{:S(2)}, u32[]{:S(2)}) %collective-permute-start.5) | collective-permute-done | bytes 138272 | tf_op jit(solution)/shard_map/ppermute | solution.py:20
  66.5 1.5 %collective-permute-done.4 = f32[3,24,480]{2,1,0:T(8,128)S(1)} collective-permute-done((f32[3,24,480]{2,1,0:T(8,128)S(1)}, f32[3,24,480]{2,1,0:T(8,128)S(1)}, u32[]{:S(2)}, u32[]{:S(2)}) %collective-permute-start.4) | collective-permute-done | bytes 138272 | tf_op jit(solution)/shard_map/ppermute | solution.py:20
  68.0 0.1 fusion.1
  68.1 0.4 collective-permute-start.8
  68.4 0.2 collective-permute-start.7
  68.7 1.5 %collective-permute-done.8 = f32[24,480]{1,0:T(8,128)S(1)} collective-permute-done((f32[24,480]{1,0:T(8,128)S(1)}, f32[24,480]{1,0:T(8,128)S(1)}, u32[]{:S(2)}, u32[]{:S(2)}) %collective-permute-start.8) | collective-permute-done | bytes 46112 | tf_op jit(solution)/shard_map/ppermute | solution.py:20
  70.2 5.1 %collective-permute-done.7 = f32[24,480]{1,0:T(8,128)S(1)} collective-permute-done((f32[24,480]{1,0:T(8,128)S(1)}, f32[24,480]{1,0:T(8,128)S(1)}, u32[]{:S(2)}, u32[]{:S(2)}) %collective-permute-start.7) | collective-permute-done | bytes 46112 | tf_op jit(solution)/shard_map/ppermute | solution.py:20
  75.3 0.7 add_bitcast_fusion
  (3 shorter events, 0.1 us)
Async XLA Ops:
  0.0 24.7 %copy-start.1 = (bf16[128,24,512]{2,1,0:T(8,128)(2,1)S(1)}, bf16[128,24,512]{2,1,0:T(8,128)(2,1)}, u32[]{:S(2)}) copy-start(bf16[128,24,512]{2,1,0:T(8,128)(2,1)} %param.6) | copy-start | bytes 9437188
  2.8 21.8 %collective-permute-start.3 = (bf16[32,24,512]{2,1,0:T(8,128)(2,1)}, bf16[32,24,512]{2,1,0:T(8,128)(2,1)}, u32[]{:S(2)}, u32[]{:S(2)}) collective-permute-start(bf16[32,24,512]{2,1,0:T(8,128)(2,1)} %get-tuple-element.6), channel_id=1, source_target_pairs={{0,252},{4,0},{8,4},{12,8},{16,12},{20,16},{24,20},{28,24},{32,28}... | collective-permute-start | bytes 2359304 | tf_op jit(solution)/shard_map/ppermute | solution.py:20
  8.6 16.1 %collective-permute-start.2 = (bf16[32,24,512]{2,1,0:T(8,128)(2,1)}, bf16[32,24,512]{2,1,0:T(8,128)(2,1)}, u32[]{:S(2)}, u32[]{:S(2)}) collective-permute-start(bf16[32,24,512]{2,1,0:T(8,128)(2,1)} %get-tuple-element.5), channel_id=1, source_target_pairs={{0,4},{4,8},{8,12},{12,16},{16,20},{20,24},{24,28},{28,32},{32,36}... | collective-permute-start | bytes 2359304 | tf_op jit(solution)/shard_map/ppermute | solution.py:20
  9.4 9.0 %collective-permute-start.1 = (s32[32,8]{0,1:T(8,128)S(1)}, s32[32,8]{0,1:T(8,128)S(1)}, u32[]{:S(2)}, u32[]{:S(2)}) collective-permute-start(s32[32,8]{0,1:T(8,128)S(1)} %get-tuple-element.14), channel_id=1, source_target_pairs={{0,252},{4,0},{8,4},{12,8},{16,12},{20,16},{24,20},{28,24},{32,28}... | collective-permute-start | bytes 3080 | tf_op jit(solution)/shard_map/ppermute | solution.py:20
  14.5 9.2 %collective-permute-start = (s32[32,8]{0,1:T(8,128)S(1)}, s32[32,8]{0,1:T(8,128)S(1)}, u32[]{:S(2)}, u32[]{:S(2)}) collective-permute-start(s32[32,8]{0,1:T(8,128)S(1)} %get-tuple-element.13), channel_id=1, source_target_pairs={{0,4},{4,8},{8,12},{12,16},{16,20},{20,24},{24,28},{28,32},{32,36}... | collective-permute-start | bytes 3080 | tf_op jit(solution)/shard_map/ppermute | solution.py:20
  24.6 3.8 %copy-start = (bf16[128,64,128]{2,1,0:T(8,128)(2,1)S(1)}, bf16[128,64,128]{2,1,0:T(8,128)(2,1)}, u32[]{:S(2)}) copy-start(bf16[128,64,128]{2,1,0:T(8,128)(2,1)} %tb_ref.1) | copy-start | bytes 6291460
  56.7 7.4 %collective-permute-start.6 = (f32[3,24,480]{2,1,0:T(8,128)S(1)}, f32[3,24,480]{2,1,0:T(8,128)S(1)}, u32[]{:S(2)}, u32[]{:S(2)}) collective-permute-start(f32[3,24,480]{2,1,0:T(8,128)S(1)} %get-tuple-element.8), channel_id=1, source_target_pairs={{0,3},{1,0},{2,1},{3,2},{4,7},{5,4},{6,5},{7,6},{8,11},{9,8},{10,9... | collective-permute-start | bytes 414728 | tf_op jit(solution)/shard_map/ppermute | solution.py:20
  59.8 6.8 %collective-permute-start.5 = (f32[3,24,480]{2,1,0:T(8,128)S(1)}, f32[3,24,480]{2,1,0:T(8,128)S(1)}, u32[]{:S(2)}, u32[]{:S(2)}) collective-permute-start(f32[3,24,480]{2,1,0:T(8,128)S(1)} %get-tuple-element.9), channel_id=1, source_target_pairs={{0,2},{1,3},{2,0},{3,1},{4,6},{5,7},{6,4},{7,5},{8,10},{9,11},{10,... | collective-permute-start | bytes 414728 | tf_op jit(solution)/shard_map/ppermute | solution.py:20
  60.4 7.6 %collective-permute-start.4 = (f32[3,24,480]{2,1,0:T(8,128)S(1)}, f32[3,24,480]{2,1,0:T(8,128)S(1)}, u32[]{:S(2)}, u32[]{:S(2)}) collective-permute-start(f32[3,24,480]{2,1,0:T(8,128)S(1)} %get-tuple-element.7), channel_id=1, source_target_pairs={{0,1},{1,2},{2,3},{3,0},{4,5},{5,6},{6,7},{7,4},{8,9},{9,10},{10,1... | collective-permute-start | bytes 414728 | tf_op jit(solution)/shard_map/ppermute | solution.py:20
  68.1 2.1 %collective-permute-start.8 = (f32[24,480]{1,0:T(8,128)S(1)}, f32[24,480]{1,0:T(8,128)S(1)}, u32[]{:S(2)}, u32[]{:S(2)}) collective-permute-start(f32[24,480]{1,0:T(8,128)S(1)} %get-tuple-element.11), channel_id=1, source_target_pairs={{0,252},{4,0},{8,4},{12,8},{16,12},{20,16},{24,20},{28,24},{32,28}... | collective-permute-start | bytes 138248 | tf_op jit(solution)/shard_map/ppermute | solution.py:20
  68.4 6.8 %collective-permute-start.7 = (f32[24,480]{1,0:T(8,128)S(1)}, f32[24,480]{1,0:T(8,128)S(1)}, u32[]{:S(2)}, u32[]{:S(2)}) collective-permute-start(f32[24,480]{1,0:T(8,128)S(1)} %get-tuple-element.12), channel_id=1, source_target_pairs={{0,4},{4,8},{8,12},{12,16},{16,20},{20,24},{24,28},{28,32},{32,36}... | collective-permute-start | bytes 138248 | tf_op jit(solution)/shard_map/ppermute | solution.py:20

commit v5 on v3

--- a/solution.py
+++ b/solution.py
@@ -33,26 +33,28 @@
     return upper24, upper64
 
 
-def place(src_ref, r, p, dst, slot, lane_group, upper, upper24):
+def place(src_ref, r, p, dst, slot, lane_group, upper, upper24, flag=None):
     src = src_ref[r, 0:CB, (p // 2) * 128:(p // 2) * 128 + 128].astype(jnp.float32)
     if (p % 2 == 1) != upper:
         src = pltpu.roll(src, B, 1)
     keep = upper24 if upper else jnp.logical_not(upper24)
+    if flag is not None:
+        keep = jnp.logical_and(keep, flag)
     rows = pl.ds(pl.multiple_of(slot * CB, 8), CB)
     lanes = slice(lane_group * 128, lane_group * 128 + 128)
-    dst[rows, lanes] = dst[rows, lanes] + jnp.where(keep, src, 0.0)
-
-
-def place_row_side(pb_ref, wpos_ref, wbase, i, xs_ref, m, upper24):
+    pltpu.store(dst.at[rows, lanes], src, mask=keep)
+
+
+def place_row_side(pb_ref, wpos_ref, wbase, i, xs_ref, m, upper24, flag=None):
     for p in range(KP):
         slot = jnp.clip(wpos_ref[wbase + p] - NCD, 0, 3 * NCD - 1)
-        place(pb_ref, i, p, xs_ref, slot, m // 2, m % 2 == 1, upper24)
-
-
-def place_window(src_ref, r, wpos_ref, wbase, s_ref, m, upper24):
+        place(pb_ref, i, p, xs_ref, slot, m // 2, m % 2 == 1, upper24, flag)
+
+
+def place_window(src_ref, r, wpos_ref, wbase, s_ref, m, upper24, flag=None):
     for p in range(KP):
         slot = jnp.clip(wpos_ref[wbase + p], 0, 5 * NCD - 1)
-        place(src_ref, r, p, s_ref, slot, m // 2, m % 2 == 1, upper24)
+        place(src_ref, r, p, s_ref, slot, m // 2, m % 2 == 1, upper24, flag)
 
 
 def chunk_product(s_ref, w_ref, c):
@@ -74,6 +76,7 @@
         for m in range(GROUP):
             place_row_side(pb_ref, wpos_ref, (base + m) * KP, base + m, xs_ref, m, upper24)
         xsb = xs_ref[...].astype(jnp.bfloat16)
+        stacked = []
         for k in range(local_k):
             s_ref[...] = jnp.zeros(s_ref.shape, f32)
             for m in range(GROUP):
@@ -81,9 +84,7 @@
                 inside = jnp.logical_and(r >= 0, r < row_count)
                 rr = jnp.clip(r, 0, row_count - 1)
 
-                @pl.when(inside)
-                def _():
-                    place_window(pb_ref, rr, wpos_ref, rr * KP, s_ref, m, upper24)
+                place_window(pb_ref, rr, wpos_ref, rr * KP, s_ref, m, upper24, inside)
 
             parts = []
             for c in range(GROUP // 4):
@@ -96,8 +97,14 @@
                         keep, t, 0.0
                     ).astype(jnp.bfloat16)
                 parts.append(chunk_product(s_ref, w_ref, c))
-            qt = jnp.concatenate(parts, axis=1)
-            gt_ref[...] += lax.dot_general(qt, xsb, NT, preferred_element_type=f32)
+            stacked.append(jnp.concatenate(parts, axis=1))
+        qt = jnp.concatenate(stacked, axis=0)
+        both = lax.dot_general(qt, xsb, NT, preferred_element_type=f32)
+        width = gt_ref.shape[0]
+        total = both[0:width]
+        for k in range(1, local_k):
+            total = total + both[k * width:(k + 1) * width]
+        gt_ref[...] += total
         return carry
 
     lax.fori_loop(0, row_count // GROUP, group, 0)
@@ -132,19 +139,13 @@
                     keep, t, 0.0
                 ).astype(jnp.bfloat16)
 
-                @pl.when(valid)
-                def _():
-                    place_row_side(pb_ref, wpos_ref, (i + halo_rows) * KP, i, xs_ref, m, upper24)
-
-                    @pl.when(r < halo_rows)
-                    def _():
-                        rl = jnp.clip(r, 0, halo_rows - 1)
-                        place_window(lo_ref, rl, wpos_ref, r * KP, s_ref, m, upper24)
-
-                    @pl.when(r >= halo_rows + row_count)
-                    def _():
-                        ru = jnp.clip(r - halo_rows - row_count, 0, halo_rows - 1)
-                        place_window(up_ref, ru, wpos_ref, r * KP, s_ref, m, upper24)
+                place_row_side(pb_ref, wpos_ref, (i + halo_rows) * KP, i, xs_ref, m, upper24, valid)
+                rl = jnp.clip(r, 0, halo_rows - 1)
+                from_lower = jnp.logical_and(valid, r < halo_rows)
+                place_window(lo_ref, rl, wpos_ref, r * KP, s_ref, m, upper24, from_lower)
+                ru = jnp.clip(r - halo_rows - row_count, 0, halo_rows - 1)
+                from_upper = jnp.logical_and(valid, r >= halo_rows + row_count)
+                place_window(up_ref, ru, wpos_ref, r * KP, s_ref, m, upper24, from_upper)
 
             parts.append(chunk_product(s_ref, w_ref, c))
         qt = jnp.concatenate(parts, axis=1)

time: 131 us -> 92.4 us (0.71)
  Pallas kernels: 69.2 us -> 37.2 us
  starting transfers between devices: 30.4 us -> 24.5 us
    pallas_call x1, Pallas kernels: 52.5 us -> 28 us  [own_terms(): pl.pallas_call(functools.partial(own_kernel, halo_rows, local_k), out_sha...]
    pallas_call x1, Pallas kernels: 16.7 us -> 9.16 us  [halo_terms(): pl.pallas_call(functools.partial(halo_kernel, halo_rows, local_k), out_sh...]
    ppermute x7, starting transfers between devices: 30.4 us -> 24.5 us  [shifted(): return lax.ppermute(value, axis, pairs)]
  transfers between devices with their start and end apart: 7 -> 7, of which waited for: 5 -> 5; matrix products, arithmetic and copies ran while one was open for 3% -> 5% of each run, Pallas kernels for 40% -> 31%
where the time goes in v5:
time: 92.4 us; the launch traced here: 91.7 us
  Pallas kernels  37.2 us (40%)
  starting transfers between devices  24.5 us (27%)
  waiting for transfers between devices  13.2 us (14%)
  local copies, waits for them, and re-layouts  10 us (11%)
  other arithmetic  5.78 us (6%)
  between operations  0.95 us (1%)
    pallas_call x1, Pallas kernels, own_terms(): pl.pallas_call(functools.partial(own_kernel, halo_rows, local_k), out_sha...  28 us
    ppermute x7, starting transfers between devices, shifted(): return lax.ppermute(value, axis, pairs)  24.5 us
    ppermute x7, waiting for transfers between devices, shifted(): return lax.ppermute(value, axis, pairs)  13.2 us
    pallas_call x1, Pallas kernels, halo_terms(): pl.pallas_call(functools.partial(halo_kernel, halo_rows, local_k), out_sh...  9.16 us
    unnamed x17, local copies, waits for them, and re-layouts  3.72 us
    ppermute x2, local copies, waits for them, and re-layouts, shifted(): return lax.ppermute(value, axis, pairs)  3.29 us
    concatenate x2, other arithmetic, with_columns(): return jnp.concatenate([blocks, columns], axis=1)  1.95 us
  transfers between devices with their start and end apart: 7, of which 5 were waited for; matrix products, arithmetic and copies ran while one was open for 5% of the time, Pallas kernels for 31%

profile of v5, /device:TPU:0, one launch (start us, length us, event | category | flops | bytes accessed | tf_op | source)
XLA Modules:
  0.0 91.7 jit_solution(12906730875691003203)
XLA Ops:
  0.0 0.8 copy.62
  0.8 1.5 %fusion.32 = (bf16[32,24,512]{2,1,0:T(8,128)(2,1)S(1)}, bf16[32,24,512]{2,1,0:T(8,128)(2,1)S(1)}) fusion(bf16[128,24,512]{2,1,0:T(8,128)(2,1)} %pb_ref.3), kind=kLoop, calls=%fused_computation.87 | loop fusion | bytes 3145728 | tf_op jit(solution)/shard_map/slice | solution.py:219
  2.3 0.0 copy-start.6
  2.3 0.0 copy-start.5
  2.3 0.0 copy-start
  2.3 0.2 copy.72
  2.6 1.0 %pad_maximum_fusion.1 = bf16[32,25,512]{2,0,1:T(8,128)(2,1)} fusion(bf16[32,1,512]{2,0,1:T(8,128)(2,1)S(1)} %pad_bitcast_fusion, bf16[32,24,512]{2,0,1:T(8,128)(2,1)S(1)} %copy.72), kind=kLoop, calls=%fused_computation.1 | loop fusion | flops 409600 | bytes 1638400 | tf_op jit(solution)/shard_map/concatenate | solution.py:222
  3.6 5.8 %collective-permute-start.1 = (bf16[32,25,512]{2,0,1:T(8,128)(2,1)}, bf16[32,25,512]{2,0,1:T(8,128)(2,1)}, u32[]{:S(2)}, u32[]{:S(2)}) collective-permute-start(bf16[32,25,512]{2,0,1:T(8,128)(2,1)} %pad_maximum_fusion.1), channel_id=1, source_target_pairs={{0,252},{4,0},{8,4},{12,8},{16,12},{20,16},{24,20},{28,24},{32,28}... | collective-permute-start | bytes 2457608 | tf_op jit(solution)/shard_map/ppermute | solution.py:20
  9.3 0.2 copy.71
  9.6 1.0 %pad_maximum_fusion = bf16[32,25,512]{2,0,1:T(8,128)(2,1)} fusion(bf16[32,1,512]{2,0,1:T(8,128)(2,1)S(1)} %pad_bitcast_fusion.1, bf16[32,24,512]{2,0,1:T(8,128)(2,1)S(1)} %copy.71), kind=kLoop, calls=%fused_computation | loop fusion | flops 409600 | bytes 1638400 | tf_op jit(solution)/shard_map/concatenate | solution.py:222
  10.5 0.0 collective-permute-start
  10.5 0.0 copy-done.6
  10.5 0.1 copy.60
  10.7 0.1 reshape.69
  10.8 0.3 reduce-window.9
  11.1 0.1 slice.36
  11.2 0.1 slice_reduce_fusion
  11.3 0.1 add_bitcast_fusion.1
  11.4 0.1 copy.59
  11.5 0.1 reshape.64.jloc_ref
  11.7 0.1 fusion.1
  11.8 0.1 select_reduce_fusion
  11.9 0.0 copy-done.5
  12.0 0.6 fusion.30
  13.3 0.1 copy.67
  13.4 0.1 reshape.67.wpos_ref
  13.6 0.0 copy-done
  13.6 0.0 copy-start.1
  13.6 1.6 %copy-done.1 = bf16[128,64,128]{2,1,0:T(8,128)(2,1)S(1)} copy-done((bf16[128,64,128]{2,1,0:T(8,128)(2,1)S(1)}, bf16[128,64,128]{2,1,0:T(8,128)(2,1)}, u32[]{:S(2)}) %copy-start.1) | copy-done | bytes 2097176
  15.2 28.0 %shard_map.46.ga_ref = f32[480,288]{1,0:T(8,128)S(1)} custom-call(s32[1024]{0:T(1024)S(1)} %reshape.67.wpos_ref, s32[256]{0:T(256)S(1)} %reshape.64.jloc_ref, bf16[128,24,512]{2,1,0:T(8,128)(2,1)S(1)} %copy-done, bf16[128,64,128]{2,1,0:T(8,128)(2,1)S(1)} %copy-done.1), custom_call_target="tpu_custom_call" | custom-call | flops 8556380160 | bytes 5795840 | tf_op jit(solution)/shard_map/pallas_call | solution.py:174
  43.2 0.0 copy-start.3
  43.2 0.9 copy-done.3
  44.1 0.0 copy-start.2
  44.1 0.0 collective-permute-done.1
  44.1 0.9 fusion.17
  45.0 0.1 copy.65
  45.0 0.0 collective-permute-done
  45.0 0.7 fusion.12
  45.8 0.1 copy.64
  45.8 0.1 pad_add_fusion
  45.9 0.1 copy.66
  46.0 0.1 reshape.66.wpos_ref
  46.1 0.0 copy-start.4
  46.2 1.7 %copy.68.lo_ref = bf16[32,25,512]{2,1,0:T(8,128)(2,1)S(1)} copy(bf16[32,25,512]{2,0,1:T(8,128)(2,1)} %collective-permute-done) | data formatting | bytes 1638400 | tf_op jit(solution)/shard_map/ppermute | solution.py:20
  47.8 1.6 %copy.69.up_ref = bf16[32,25,512]{2,1,0:T(8,128)(2,1)S(1)} copy(bf16[32,25,512]{2,0,1:T(8,128)(2,1)} %collective-permute-done.1) | data formatting | bytes 1638400 | tf_op jit(solution)/shard_map/ppermute | solution.py:20
  49.5 0.0 copy-done.2
  49.5 0.0 copy-done.4
  49.5 9.2 %shard_map.47 = f32[480,288]{1,0:T(8,128)S(1)} custom-call(s32[1]{0:T(128)} %bitcast.count_ref, s32[256]{0:T(256)S(1)} %broadcast_select_fusion.list_ref, s32[1536]{0:T(1024)S(1)} %reshape.66.wpos_ref, s32[256]{0:T(256)S(1)} %reshape.64.jloc_ref, bf16[128,24,512]{2,1,0:T(8,128)(2,1)} %pb_ref.3, bf16[32,25,512]{2,1,0:T(8,128)(2,1)S(1)} %copy.68.lo_ref, ...), custom_call_target="tpu_custom_call" | custom-call | flops 4278190080 | bytes 6348800 | tf_op jit(solution)/shard_map/pallas_call | solution.py:194
  58.6 0.2 copy.70
  58.9 11.7 %collective-permute-start.4 = (f32[3,24,480]{2,1,0:T(8,128)S(1)}, f32[3,24,480]{2,1,0:T(8,128)S(1)}, u32[]{:S(2)}, u32[]{:S(2)}) collective-permute-start(f32[3,24,480]{2,1,0:T(8,128)S(1)} %get-tuple-element.10), channel_id=1, source_target_pairs={{0,3},{1,0},{2,1},{3,2},{4,7},{5,4},{6,5},{7,6},{8,11},{9,8},{10,9... | collective-permute-start | bytes 414728 | tf_op jit(solution)/shard_map/ppermute | solution.py:20
  70.7 2.1 %collective-permute-start.3 = (f32[3,24,480]{2,1,0:T(8,128)S(1)}, f32[3,24,480]{2,1,0:T(8,128)S(1)}, u32[]{:S(2)}, u32[]{:S(2)}) collective-permute-start(f32[3,24,480]{2,1,0:T(8,128)S(1)} %get-tuple-element.11), channel_id=1, source_target_pairs={{0,2},{1,3},{2,0},{3,1},{4,6},{5,7},{6,4},{7,5},{8,10},{9,11},{10,... | collective-permute-start | bytes 414728 | tf_op jit(solution)/shard_map/ppermute | solution.py:20
  72.7 0.0 collective-permute-start.2
  72.7 2.2 %collective-permute-done.4 = f32[3,24,480]{2,1,0:T(8,128)S(1)} collective-permute-done((f32[3,24,480]{2,1,0:T(8,128)S(1)}, f32[3,24,480]{2,1,0:T(8,128)S(1)}, u32[]{:S(2)}, u32[]{:S(2)}) %collective-permute-start.4) | collective-permute-done | bytes 138272 | tf_op jit(solution)/shard_map/ppermute | solution.py:20
  74.9 2.4 %collective-permute-done.3 = f32[3,24,480]{2,1,0:T(8,128)S(1)} collective-permute-done((f32[3,24,480]{2,1,0:T(8,128)S(1)}, f32[3,24,480]{2,1,0:T(8,128)S(1)}, u32[]{:S(2)}, u32[]{:S(2)}) %collective-permute-start.3) | collective-permute-done | bytes 138272 | tf_op jit(solution)/shard_map/ppermute | solution.py:20
  77.3 1.8 %collective-permute-done.2 = f32[3,24,480]{2,1,0:T(8,128)S(1)} collective-permute-done((f32[3,24,480]{2,1,0:T(8,128)S(1)}, f32[3,24,480]{2,1,0:T(8,128)S(1)}, u32[]{:S(2)}, u32[]{:S(2)}) %collective-permute-start.2) | collective-permute-done | bytes 138272 | tf_op jit(solution)/shard_map/ppermute | solution.py:20
  79.1 4.9 %collective-permute-start.6 = (f32[24,480]{1,0:T(8,128)S(1)}, f32[24,480]{1,0:T(8,128)S(1)}, u32[]{:S(2)}, u32[]{:S(2)}) collective-permute-start(f32[24,480]{1,0:T(8,128)S(1)} %get-tuple-element.13), channel_id=1, source_target_pairs={{0,252},{4,0},{8,4},{12,8},{16,12},{20,16},{24,20},{28,24},{32,28}... | collective-permute-start | bytes 138248 | tf_op jit(solution)/shard_map/ppermute | solution.py:20
  84.1 0.0 collective-permute-start.5
  84.1 1.7 %collective-permute-done.6 = f32[24,480]{1,0:T(8,128)S(1)} collective-permute-done((f32[24,480]{1,0:T(8,128)S(1)}, f32[24,480]{1,0:T(8,128)S(1)}, u32[]{:S(2)}, u32[]{:S(2)}) %collective-permute-start.6) | collective-permute-done | bytes 46112 | tf_op jit(solution)/shard_map/ppermute | solution.py:20
  85.8 5.1 %collective-permute-done.5 = f32[24,480]{1,0:T(8,128)S(1)} collective-permute-done((f32[24,480]{1,0:T(8,128)S(1)}, f32[24,480]{1,0:T(8,128)S(1)}, u32[]{:S(2)}, u32[]{:S(2)}) %collective-permute-start.5) | collective-permute-done | bytes 46112 | tf_op jit(solution)/shard_map/ppermute | solution.py:20
  90.9 0.7 add_bitcast_fusion
  (12 shorter events, 0.2 us)
Async XLA Ops:
  2.3 8.2 %copy-start.6 = (s32[128,2]{0,1:T(2,128)S(1)}, s32[128,2]{0,1:T(2,128)}, u32[]{:S(2)}) copy-start(s32[128,2]{0,1:T(2,128)} %param.5) | copy-start | bytes 3076
  2.3 9.6 %copy-start.5 = (s32[128,8]{0,1:T(8,128)S(1)}, s32[128,8]{0,1:T(8,128)}, u32[]{:S(2)}) copy-start(s32[128,8]{0,1:T(8,128)} %param.7) | copy-start | bytes 12292
  2.3 11.2 %copy-start = (bf16[128,24,512]{2,1,0:T(8,128)(2,1)S(1)}, bf16[128,24,512]{2,1,0:T(8,128)(2,1)}, u32[]{:S(2)}) copy-start(bf16[128,24,512]{2,1,0:T(8,128)(2,1)} %pb_ref.3) | copy-start | bytes 9437188
  3.6 40.5 %collective-permute-start.1 = (bf16[32,25,512]{2,0,1:T(8,128)(2,1)}, bf16[32,25,512]{2,0,1:T(8,128)(2,1)}, u32[]{:S(2)}, u32[]{:S(2)}) collective-permute-start(bf16[32,25,512]{2,0,1:T(8,128)(2,1)} %pad_maximum_fusion.1), channel_id=1, source_target_pairs={{0,252},{4,0},{8,4},{12,8},{16,12},{20,16},{24,20},{28,24},{32,28}... | collective-permute-start | bytes 2457608 | tf_op jit(solution)/shard_map/ppermute | solution.py:20
  10.5 34.5 %collective-permute-start = (bf16[32,25,512]{2,0,1:T(8,128)(2,1)}, bf16[32,25,512]{2,0,1:T(8,128)(2,1)}, u32[]{:S(2)}, u32[]{:S(2)}) collective-permute-start(bf16[32,25,512]{2,0,1:T(8,128)(2,1)} %pad_maximum_fusion), channel_id=1, source_target_pairs={{0,4},{4,8},{8,12},{12,16},{16,20},{20,24},{24,28},{28,32},{32,36}... | collective-permute-start | bytes 2457608 | tf_op jit(solution)/shard_map/ppermute | solution.py:20
  13.6 1.6 %copy-start.1 = (bf16[128,64,128]{2,1,0:T(8,128)(2,1)S(1)}, bf16[128,64,128]{2,1,0:T(8,128)(2,1)}, u32[]{:S(2)}) copy-start(bf16[128,64,128]{2,1,0:T(8,128)(2,1)} %tb_ref.3) | copy-start | bytes 6291460
  43.2 0.9 copy-start.3
  44.1 5.4 %copy-start.2 = (bf16[128,64,128]{2,1,0:T(8,128)(2,1)S(1)}, bf16[128,64,128]{2,1,0:T(8,128)(2,1)}, u32[]{:S(2)}) copy-start(bf16[128,64,128]{2,1,0:T(8,128)(2,1)} %tb_ref.3) | copy-start | bytes 6291460
  46.1 3.3 %copy-start.4 = (f32[480,288]{1,0:T(8,128)S(1)}, f32[480,288]{1,0:T(8,128)}, u32[]{:S(2)}) copy-start(f32[480,288]{1,0:T(8,128)} %copy-done.3) | copy-start | bytes 1658884
  58.9 16.0 %collective-permute-start.4 = (f32[3,24,480]{2,1,0:T(8,128)S(1)}, f32[3,24,480]{2,1,0:T(8,128)S(1)}, u32[]{:S(2)}, u32[]{:S(2)}) collective-permute-start(f32[3,24,480]{2,1,0:T(8,128)S(1)} %get-tuple-element.10), channel_id=1, source_target_pairs={{0,3},{1,0},{2,1},{3,2},{4,7},{5,4},{6,5},{7,6},{8,11},{9,8},{10,9... | collective-permute-start | bytes 414728 | tf_op jit(solution)/shard_map/ppermute | solution.py:20
  70.7 6.6 %collective-permute-start.3 = (f32[3,24,480]{2,1,0:T(8,128)S(1)}, f32[3,24,480]{2,1,0:T(8,128)S(1)}, u32[]{:S(2)}, u32[]{:S(2)}) collective-permute-start(f32[3,24,480]{2,1,0:T(8,128)S(1)} %get-tuple-element.11), channel_id=1, source_target_pairs={{0,2},{1,3},{2,0},{3,1},{4,6},{5,7},{6,4},{7,5},{8,10},{9,11},{10,... | collective-permute-start | bytes 414728 | tf_op jit(solution)/shard_map/ppermute | solution.py:20
  72.7 6.4 %collective-permute-start.2 = (f32[3,24,480]{2,1,0:T(8,128)S(1)}, f32[3,24,480]{2,1,0:T(8,128)S(1)}, u32[]{:S(2)}, u32[]{:S(2)}) collective-permute-start(f32[3,24,480]{2,1,0:T(8,128)S(1)} %get-tuple-element.9), channel_id=1, source_target_pairs={{0,1},{1,2},{2,3},{3,0},{4,5},{5,6},{6,7},{7,4},{8,9},{9,10},{10,1... | collective-permute-start | bytes 414728 | tf_op jit(solution)/shard_map/ppermute | solution.py:20
  79.1 6.7 %collective-permute-start.6 = (f32[24,480]{1,0:T(8,128)S(1)}, f32[24,480]{1,0:T(8,128)S(1)}, u32[]{:S(2)}, u32[]{:S(2)}) collective-permute-start(f32[24,480]{1,0:T(8,128)S(1)} %get-tuple-element.13), channel_id=1, source_target_pairs={{0,252},{4,0},{8,4},{12,8},{16,12},{20,16},{24,20},{28,24},{32,28}... | collective-permute-start | bytes 138248 | tf_op jit(solution)/shard_map/ppermute | solution.py:20
  84.1 6.8 %collective-permute-start.5 = (f32[24,480]{1,0:T(8,128)S(1)}, f32[24,480]{1,0:T(8,128)S(1)}, u32[]{:S(2)}, u32[]{:S(2)}) collective-permute-start(f32[24,480]{1,0:T(8,128)S(1)} %get-tuple-element.14), channel_id=1, source_target_pairs={{0,4},{4,8},{8,12},{12,16},{16,20},{20,24},{24,28},{28,32},{32,36}... | collective-permute-start | bytes 138248 | tf_op jit(solution)/shard_map/ppermute | solution.py:20

commit v6 on v4

--- a/solution.py
+++ b/solution.py
@@ -24,8 +24,17 @@
     return jnp.pad(values, ((0, 0),) * (values.ndim - 1) + ((left_pad, right_pad),))
 
 
-def slab_kernel(halo_rows, row_count, local_k, wpos_ref, jloc_ref, pb_ref, tb_ref, gt_ref,
-                s_ref, xs_ref, w_ref):
+def slab_kernel(halo_rows, row_count, local_k, wpos_ref, jloc_ref, lower_ref, own_ref, upper_ref,
+                tb_ref, gt_ref, pb_ref, s_ref, xs_ref, w_ref, sems):
+    copies = [
+        pltpu.make_async_copy(lower_ref, pb_ref.at[0:halo_rows], sems.at[0]),
+        pltpu.make_async_copy(own_ref, pb_ref.at[halo_rows:halo_rows + row_count], sems.at[1]),
+        pltpu.make_async_copy(
+            upper_ref, pb_ref.at[halo_rows + row_count:2 * halo_rows + row_count], sems.at[2]
+        ),
+    ]
+    for copy in copies:
+        copy.start()
     window_slots = 5 * NCD
     row_slots = 3 * NCD
     f32 = jnp.float32
@@ -34,6 +43,8 @@
     upper64 = lax.broadcasted_iota(jnp.int32, (B, 128), 1) >= B
     gt_ref[...] = jnp.zeros(gt_ref.shape, f32)
     w_ref[...] = jnp.zeros(w_ref.shape, bf16)
+    for copy in copies:
+        copy.wait()
 
     def place(dst, slot, lane_group, upper, r, p):
         src = pb_ref[r, :, (p // 2) * 128:(p // 2) * 128 + 128].astype(f32)
@@ -86,7 +97,7 @@
     lax.fori_loop(0, row_count // GROUP, group, 0)
 
 
-def slab_terms_t(wpos, jloc, pb, tb, halo_rows, row_count):
+def slab_terms_t(wpos, jloc, lower, own, upper, tb, halo_rows, row_count):
     local_k = tb.shape[2] // B
     window_width = 5 * NCD * CB
     row_width = 3 * NCD * CB
@@ -98,22 +109,26 @@
         in_specs=[
             pl.BlockSpec(memory_space=pltpu.SMEM),
             pl.BlockSpec(memory_space=pltpu.SMEM),
-            pl.BlockSpec(memory_space=pltpu.VMEM),
+            pl.BlockSpec(memory_space=pl.ANY),
+            pl.BlockSpec(memory_space=pl.ANY),
+            pl.BlockSpec(memory_space=pl.ANY),
             pl.BlockSpec(memory_space=pltpu.VMEM),
         ],
         out_specs=pl.BlockSpec(memory_space=pltpu.VMEM),
         scratch_shapes=[
+            pltpu.VMEM((row_count + 2 * halo_rows,) + own.shape[1:], own.dtype),
             pltpu.VMEM((window_width, GROUP * B), jnp.float32),
             pltpu.VMEM((row_width, GROUP * B), jnp.float32),
             pltpu.VMEM((256, 256), jnp.bfloat16),
+            pltpu.SemaphoreType.DMA((3,)),
         ],
         compiler_params=pltpu.CompilerParams(vmem_limit_bytes=48 * 1024 * 1024),
         cost_estimate=pl.CostEstimate(
             flops=flops,
-            bytes_accessed=pb.size * 2 + tb.size * 2 + window_width * row_width * 4,
+            bytes_accessed=(lower.size + own.size + upper.size) * 2 + tb.size * 2 + window_width * row_width * 4,
             transcendentals=0,
         ),
-    )(wpos, jloc, pb, tb)
+    )(wpos, jloc, lower, own, upper, tb)
 
 
 def on_device(tangent_blocks, tangent_columns, prolong_blocks, prolong_columns):
@@ -130,14 +145,14 @@
     upper_blocks = shifted(prolong_blocks[:halo_rows], "blk", -1)
     lower_columns = shifted(prolong_columns[row_count - halo_rows:], "blk", 1)
     upper_columns = shifted(prolong_columns[:halo_rows], "blk", -1)
-    near_blocks = jnp.concatenate([lower_blocks, prolong_blocks, upper_blocks], axis=0)
     near_columns = jnp.concatenate([lower_columns, prolong_columns, upper_columns], axis=0)
     wpos = ((near_columns // NCD - slab_index + 2) % slab_count) * NCD + near_columns % NCD
     wpos = wpos.astype(jnp.int32).reshape(-1)
     jloc = (tangent_columns - slab_index * row_count + halo_rows) % fine_count
     jloc = jnp.clip(jloc, 0, row_count + 2 * halo_rows - 1).astype(jnp.int32).reshape(-1)
 
-    gt = slab_terms_t(wpos, jloc, near_blocks, tangent_blocks, halo_rows, row_count)
+    gt = slab_terms_t(wpos, jloc, lower_blocks, prolong_blocks, upper_blocks, tangent_blocks,
+                      halo_rows, row_count)
     terms = gt.T.reshape(3, NCD, CB, 5 * coarse_width)
 
     shares = lax.dynamic_index_in_dim(terms, lane_index, axis=1, keepdims=False)

time: 76.2 us -> 71.3 us (0.936)
  other arithmetic: 5.98 us -> 0.89 us
  waiting for transfers between devices: 21.4 us -> 22.4 us
  local copies, waits for them, and re-layouts: 4.4 us -> 3.63 us
    concatenate x1 -> x0, other arithmetic: 3.72 us -> none  [on_device(): jnp.concatenate([lower_blocks, prolong_blocks, upper_blocks], axis=0)]
    ppermute x9, waiting for transfers between devices: 21.4 us -> 22.4 us  [shifted(): return lax.ppermute(value, axis, pairs)]
  transfers between devices with their start and end apart: 9 -> 9, of which waited for: 7 -> 7; matrix products, arithmetic and copies ran while one was open for 4% -> 1% of each run, Pallas kernels for 0% -> 0%
where the time goes in v6:
time: 71.3 us
  Pallas kernels  28.1 us (39%)
  waiting for transfers between devices  22.4 us (31%)
  starting transfers between devices  16.1 us (23%)
  local copies, waits for them, and re-layouts  3.63 us (5%)
  other arithmetic  0.89 us (1%)
    pallas_call x1, Pallas kernels, slab_terms_t(): pl.pallas_call(kernel, out_shape=jax.ShapeDtypeStruct((window_width, row_...  28.1 us
    ppermute x9, waiting for transfers between devices, shifted(): return lax.ppermute(value, axis, pairs)  22.4 us
    ppermute x9, starting transfers between devices, shifted(): return lax.ppermute(value, axis, pairs)  16.1 us
    slice x1, local copies, waits for them, and re-layouts, on_device(): upper_blocks = shifted(prolong_blocks[:halo_rows], 'blk', -1)  2.79 us
  transfers between devices with their start and end apart: 9, of which 7 were waited for; matrix products, arithmetic and copies ran while one was open for 1% of the time, Pallas kernels for 0%

profile of v6, /device:TPU:0, one launch (start us, length us, event | category | flops | bytes accessed | tf_op | source)
XLA Modules:
  0.0 71.3 jit_solution(11699152482878806024)
XLA Ops:
  0.0 0.0 copy-start.1
  0.0 0.0 copy-start.2
  0.0 0.0 copy-start
  0.0 2.8 %fusion.10 = (bf16[32,24,512]{2,1,0:T(8,128)(2,1)}, bf16[32,24,512]{2,1,0:T(8,128)(2,1)}) fusion(bf16[128,24,512]{2,1,0:T(8,128)(2,1)} %own_ref.1), kind=kLoop, calls=%fused_computation.31 | loop fusion | bytes 3145728 | tf_op jit(solution)/shard_map/slice | solution.py:145
  2.8 0.0 collective-permute-start.2
  2.8 5.8 %collective-permute-start.3 = (bf16[32,24,512]{2,1,0:T(8,128)(2,1)}, bf16[32,24,512]{2,1,0:T(8,128)(2,1)}, u32[]{:S(2)}, u32[]{:S(2)}) collective-permute-start(bf16[32,24,512]{2,1,0:T(8,128)(2,1)} %get-tuple-element.5), channel_id=1, source_target_pairs={{0,252},{4,0},{8,4},{12,8},{16,12},{20,16},{24,20},{28,24},{32,28}... | collective-permute-start | bytes 2359304 | tf_op jit(solution)/shard_map/ppermute | solution.py:20
  8.6 0.0 copy-done.1
  8.6 0.1 fusion.11
  8.6 0.7 collective-permute-start.1
  9.3 0.0 collective-permute-start
  9.3 0.0 copy-done.2
  9.4 0.1 copy.10
  9.5 0.1 reshape.8.jloc_ref
  9.6 8.8 %collective-permute-done.1 = s32[32,8]{0,1:T(8,128)S(1)} collective-permute-done((s32[32,8]{0,1:T(8,128)S(1)}, s32[32,8]{0,1:T(8,128)S(1)}, u32[]{:S(2)}, u32[]{:S(2)}) %collective-permute-start.1) | collective-permute-done | bytes 1056 | tf_op jit(solution)/shard_map/ppermute | solution.py:20
  18.4 0.2 collective-permute-done
  18.5 0.1 pad_add_fusion
  18.6 0.1 copy.9
  18.7 0.1 concatenate.6
  18.9 0.0 collective-permute-done.2.lower_ref
  18.9 0.0 collective-permute-done.3.upper_ref
  18.9 0.0 copy-done
  18.9 28.1 %shard_map.46 = f32[480,288]{1,0:T(8,128)S(1)} custom-call(s32[1536]{0:T(1024)S(1)} %fusion.6.wpos_ref, s32[256]{0:T(256)S(1)} %reshape.8.jloc_ref, bf16[32,24,512]{2,1,0:T(8,128)(2,1)} %collective-permute-done.2.lower_ref, bf16[128,24,512]{2,1,0:T(8,128)(2,1)} %own_ref.1, bf16[32,24,512]{2,1,0:T(8,128)(2,1)} %collective-permute-done.3.upper_ref, ...), custom_call_target="tpu_custom_call" | custom-call | flops 8556380160 | bytes 7368704 | tf_op jit(solution)/shard_map/pallas_call | solution.py:106
  47.0 0.2 copy.11
  47.3 3.1 %collective-permute-start.6 = (f32[3,24,480]{2,1,0:T(8,128)S(1)}, f32[3,24,480]{2,1,0:T(8,128)S(1)}, u32[]{:S(2)}, u32[]{:S(2)}) collective-permute-start(f32[3,24,480]{2,1,0:T(8,128)S(1)} %get-tuple-element.8), channel_id=1, source_target_pairs={{0,3},{1,0},{2,1},{3,2},{4,7},{5,4},{6,5},{7,6},{8,11},{9,8},{10,9... | collective-permute-start | bytes 414728 | tf_op jit(solution)/shard_map/ppermute | solution.py:20
  50.4 0.6 collective-permute-start.5
  51.1 1.0 %collective-permute-start.4 = (f32[3,24,480]{2,1,0:T(8,128)S(1)}, f32[3,24,480]{2,1,0:T(8,128)S(1)}, u32[]{:S(2)}, u32[]{:S(2)}) collective-permute-start(f32[3,24,480]{2,1,0:T(8,128)S(1)} %get-tuple-element.7), channel_id=1, source_target_pairs={{0,1},{1,2},{2,3},{3,0},{4,5},{5,6},{6,7},{7,4},{8,9},{9,10},{10,1... | collective-permute-start | bytes 414728 | tf_op jit(solution)/shard_map/ppermute | solution.py:20
  52.0 2.7 %collective-permute-done.6 = f32[3,24,480]{2,1,0:T(8,128)S(1)} collective-permute-done((f32[3,24,480]{2,1,0:T(8,128)S(1)}, f32[3,24,480]{2,1,0:T(8,128)S(1)}, u32[]{:S(2)}, u32[]{:S(2)}) %collective-permute-start.6) | collective-permute-done | bytes 138272 | tf_op jit(solution)/shard_map/ppermute | solution.py:20
  54.7 2.5 %collective-permute-done.5 = f32[3,24,480]{2,1,0:T(8,128)S(1)} collective-permute-done((f32[3,24,480]{2,1,0:T(8,128)S(1)}, f32[3,24,480]{2,1,0:T(8,128)S(1)}, u32[]{:S(2)}, u32[]{:S(2)}) %collective-permute-start.5) | collective-permute-done | bytes 138272 | tf_op jit(solution)/shard_map/ppermute | solution.py:20
  57.2 1.5 %collective-permute-done.4 = f32[3,24,480]{2,1,0:T(8,128)S(1)} collective-permute-done((f32[3,24,480]{2,1,0:T(8,128)S(1)}, f32[3,24,480]{2,1,0:T(8,128)S(1)}, u32[]{:S(2)}, u32[]{:S(2)}) %collective-permute-start.4) | collective-permute-done | bytes 138272 | tf_op jit(solution)/shard_map/ppermute | solution.py:20
  58.7 5.0 %collective-permute-start.8 = (f32[24,480]{1,0:T(8,128)S(1)}, f32[24,480]{1,0:T(8,128)S(1)}, u32[]{:S(2)}, u32[]{:S(2)}) collective-permute-start(f32[24,480]{1,0:T(8,128)S(1)} %get-tuple-element.11), channel_id=1, source_target_pairs={{0,252},{4,0},{8,4},{12,8},{16,12},{20,16},{24,20},{28,24},{32,28}... | collective-permute-start | bytes 138248 | tf_op jit(solution)/shard_map/ppermute | solution.py:20
  63.7 0.0 collective-permute-start.7
  63.7 1.7 %collective-permute-done.8 = f32[24,480]{1,0:T(8,128)S(1)} collective-permute-done((f32[24,480]{1,0:T(8,128)S(1)}, f32[24,480]{1,0:T(8,128)S(1)}, u32[]{:S(2)}, u32[]{:S(2)}) %collective-permute-start.8) | collective-permute-done | bytes 46112 | tf_op jit(solution)/shard_map/ppermute | solution.py:20
  65.4 5.1 %collective-permute-done.7 = f32[24,480]{1,0:T(8,128)S(1)} collective-permute-done((f32[24,480]{1,0:T(8,128)S(1)}, f32[24,480]{1,0:T(8,128)S(1)}, u32[]{:S(2)}, u32[]{:S(2)}) %collective-permute-start.7) | collective-permute-done | bytes 46112 | tf_op jit(solution)/shard_map/ppermute | solution.py:20
  70.5 0.7 %add_bitcast_fusion = f32[1,24,672]{2,1,0:T(8,128)} fusion(f32[24,480]{1,0:T(8,128)S(1)} %collective-permute-done.8, f32[24,480]{1,0:T(8,128)S(1)} %collective-permute-done.7, f32[24,480]{1,0:T(8,128)S(1)} %get-tuple-element.10), kind=kLoop, calls=%fused_computation.6 | loop fusion | flops 32256 | bytes 202752 | tf_op jit(solution)/shard_map/broadcast_in_dim | solution.py:171
  (5 shorter events, 0.1 us)
Async XLA Ops:
  0.0 8.6 %copy-start.1 = (s32[128,8]{0,1:T(8,128)S(1)}, s32[128,8]{0,1:T(8,128)}, u32[]{:S(2)}) copy-start(s32[128,8]{0,1:T(8,128)} %param.7) | copy-start | bytes 12292
  0.0 9.3 %copy-start.2 = (s32[128,2]{0,1:T(2,128)S(1)}, s32[128,2]{0,1:T(2,128)}, u32[]{:S(2)}) copy-start(s32[128,2]{0,1:T(2,128)} %param.5) | copy-start | bytes 3076
  0.0 18.9 %copy-start = (bf16[128,64,128]{2,1,0:T(8,128)(2,1)S(1)}, bf16[128,64,128]{2,1,0:T(8,128)(2,1)}, u32[]{:S(2)}) copy-start(bf16[128,64,128]{2,1,0:T(8,128)(2,1)} %tb_ref.1) | copy-start | bytes 6291460
  2.8 16.1 %collective-permute-start.2 = (bf16[32,24,512]{2,1,0:T(8,128)(2,1)}, bf16[32,24,512]{2,1,0:T(8,128)(2,1)}, u32[]{:S(2)}, u32[]{:S(2)}) collective-permute-start(bf16[32,24,512]{2,1,0:T(8,128)(2,1)} %get-tuple-element.6), channel_id=1, source_target_pairs={{0,4},{4,8},{8,12},{12,16},{16,20},{20,24},{24,28},{28,32},{32,36}... | collective-permute-start | bytes 2359304 | tf_op jit(solution)/shard_map/ppermute | solution.py:20
  2.8 16.1 %collective-permute-start.3 = (bf16[32,24,512]{2,1,0:T(8,128)(2,1)}, bf16[32,24,512]{2,1,0:T(8,128)(2,1)}, u32[]{:S(2)}, u32[]{:S(2)}) collective-permute-start(bf16[32,24,512]{2,1,0:T(8,128)(2,1)} %get-tuple-element.5), channel_id=1, source_target_pairs={{0,252},{4,0},{8,4},{12,8},{16,12},{20,16},{24,20},{28,24},{32,28}... | collective-permute-start | bytes 2359304 | tf_op jit(solution)/shard_map/ppermute | solution.py:20
  8.6 9.7 %collective-permute-start.1 = (s32[32,8]{0,1:T(8,128)S(1)}, s32[32,8]{0,1:T(8,128)S(1)}, u32[]{:S(2)}, u32[]{:S(2)}) collective-permute-start(s32[32,8]{0,1:T(8,128)S(1)} %get-tuple-element.14), channel_id=1, source_target_pairs={{0,252},{4,0},{8,4},{12,8},{16,12},{20,16},{24,20},{28,24},{32,28}... | collective-permute-start | bytes 3080 | tf_op jit(solution)/shard_map/ppermute | solution.py:20
  9.3 9.2 %collective-permute-start = (s32[32,8]{0,1:T(8,128)S(1)}, s32[32,8]{0,1:T(8,128)S(1)}, u32[]{:S(2)}, u32[]{:S(2)}) collective-permute-start(s32[32,8]{0,1:T(8,128)S(1)} %get-tuple-element.13), channel_id=1, source_target_pairs={{0,4},{4,8},{8,12},{12,16},{16,20},{20,24},{24,28},{28,32},{32,36}... | collective-permute-start | bytes 3080 | tf_op jit(solution)/shard_map/ppermute | solution.py:20
  47.3 7.4 %collective-permute-start.6 = (f32[3,24,480]{2,1,0:T(8,128)S(1)}, f32[3,24,480]{2,1,0:T(8,128)S(1)}, u32[]{:S(2)}, u32[]{:S(2)}) collective-permute-start(f32[3,24,480]{2,1,0:T(8,128)S(1)} %get-tuple-element.8), channel_id=1, source_target_pairs={{0,3},{1,0},{2,1},{3,2},{4,7},{5,4},{6,5},{7,6},{8,11},{9,8},{10,9... | collective-permute-start | bytes 414728 | tf_op jit(solution)/shard_map/ppermute | solution.py:20
  50.4 6.8 %collective-permute-start.5 = (f32[3,24,480]{2,1,0:T(8,128)S(1)}, f32[3,24,480]{2,1,0:T(8,128)S(1)}, u32[]{:S(2)}, u32[]{:S(2)}) collective-permute-start(f32[3,24,480]{2,1,0:T(8,128)S(1)} %get-tuple-element.9), channel_id=1, source_target_pairs={{0,2},{1,3},{2,0},{3,1},{4,6},{5,7},{6,4},{7,5},{8,10},{9,11},{10,... | collective-permute-start | bytes 414728 | tf_op jit(solution)/shard_map/ppermute | solution.py:20
  51.1 7.6 %collective-permute-start.4 = (f32[3,24,480]{2,1,0:T(8,128)S(1)}, f32[3,24,480]{2,1,0:T(8,128)S(1)}, u32[]{:S(2)}, u32[]{:S(2)}) collective-permute-start(f32[3,24,480]{2,1,0:T(8,128)S(1)} %get-tuple-element.7), channel_id=1, source_target_pairs={{0,1},{1,2},{2,3},{3,0},{4,5},{5,6},{6,7},{7,4},{8,9},{9,10},{10,1... | collective-permute-start | bytes 414728 | tf_op jit(solution)/shard_map/ppermute | solution.py:20
  58.7 6.7 %collective-permute-start.8 = (f32[24,480]{1,0:T(8,128)S(1)}, f32[24,480]{1,0:T(8,128)S(1)}, u32[]{:S(2)}, u32[]{:S(2)}) collective-permute-start(f32[24,480]{1,0:T(8,128)S(1)} %get-tuple-element.11), channel_id=1, source_target_pairs={{0,252},{4,0},{8,4},{12,8},{16,12},{20,16},{24,20},{28,24},{32,28}... | collective-permute-start | bytes 138248 | tf_op jit(solution)/shard_map/ppermute | solution.py:20
  63.7 6.8 %collective-permute-start.7 = (f32[24,480]{1,0:T(8,128)S(1)}, f32[24,480]{1,0:T(8,128)S(1)}, u32[]{:S(2)}, u32[]{:S(2)}) collective-permute-start(f32[24,480]{1,0:T(8,128)S(1)} %get-tuple-element.12), channel_id=1, source_target_pairs={{0,4},{4,8},{8,12},{12,16},{16,20},{20,24},{24,28},{28,32},{32,36}... | collective-permute-start | bytes 138248 | tf_op jit(solution)/shard_map/ppermute | solution.py:20

commit v7 on v6

--- a/solution.py
+++ b/solution.py
@@ -24,8 +24,51 @@
     return jnp.pad(values, ((0, 0),) * (values.ndim - 1) + ((left_pad, right_pad),))
 
 
+def row_side_kernel(wpos_ref, own_ref, out_ref, xs_ref):
+    f32 = jnp.float32
+    upper24 = lax.broadcasted_iota(jnp.int32, (CB, 128), 1) >= B
+    row_slots = 3 * NCD
+
+    def group(g, carry):
+        base = g * GROUP
+        xs_ref[...] = jnp.zeros(xs_ref.shape, f32)
+        for m in range(GROUP):
+            upper = m % 2 == 1
+            for p in range(KP):
+                slot = jnp.clip(wpos_ref[(base + m) * KP + p] - NCD, 0, row_slots - 1)
+                src = own_ref[base + m, :, (p // 2) * 128:(p // 2) * 128 + 128].astype(f32)
+                if (p % 2 == 1) != upper:
+                    src = pltpu.roll(src, B, 1)
+                keep = upper24 if upper else jnp.logical_not(upper24)
+                rows = pl.ds(pl.multiple_of(slot * CB, 8), CB)
+                lanes = slice((m // 2) * 128, (m // 2) * 128 + 128)
+                pltpu.store(xs_ref.at[rows, lanes], src, mask=keep)
+        out_ref[g] = xs_ref[...].astype(jnp.bfloat16)
+        return carry
+
+    lax.fori_loop(0, out_ref.shape[0], group, 0)
+
+
+def row_side(wpos_own, own):
+    row_count = own.shape[0]
+    groups = row_count // GROUP
+    shape = (groups, 3 * NCD * CB, GROUP * B)
+    return pl.pallas_call(
+        row_side_kernel,
+        out_shape=jax.ShapeDtypeStruct(shape, jnp.bfloat16),
+        in_specs=[pl.BlockSpec(memory_space=pltpu.SMEM), pl.BlockSpec(memory_space=pltpu.VMEM)],
+        out_specs=pl.BlockSpec(memory_space=pltpu.VMEM),
+        scratch_shapes=[pltpu.VMEM(shape[1:], jnp.float32)],
+        compiler_params=pltpu.CompilerParams(vmem_limit_bytes=48 * 1024 * 1024),
+        cost_estimate=pl.CostEstimate(
+            flops=0, bytes_accessed=own.size * 2 + groups * shape[1] * shape[2] * 2,
+            transcendentals=0,
+        ),
+    )(wpos_own, own)
+
+
 def slab_kernel(halo_rows, row_count, local_k, wpos_ref, jloc_ref, lower_ref, own_ref, upper_ref,
-                tb_ref, gt_ref, pb_ref, s_ref, xs_ref, w_ref, sems):
+                tb_ref, xsall_ref, gt_ref, pb_ref, s_ref, w_ref, sems):
     copies = [
         pltpu.make_async_copy(lower_ref, pb_ref.at[0:halo_rows], sems.at[0]),
         pltpu.make_async_copy(own_ref, pb_ref.at[halo_rows:halo_rows + row_count], sems.at[1]),
@@ -57,14 +100,7 @@
 
     def group(g, carry):
         base = g * GROUP
-        xs_ref[...] = jnp.zeros(xs_ref.shape, f32)
-        for m in range(GROUP):
-            r = base + m + halo_rows
-            for p in range(KP):
-                w = wpos_ref[r * KP + p]
-                slot = jnp.clip(w - NCD, 0, row_slots - 1)
-                place(xs_ref, slot, m // 2, m % 2 == 1, r, p)
-        xsb = xs_ref[...].astype(bf16)
+        xsb = xsall_ref[g]
         for k in range(local_k):
             s_ref[...] = jnp.zeros(s_ref.shape, f32)
             for m in range(GROUP):
@@ -97,7 +133,7 @@
     lax.fori_loop(0, row_count // GROUP, group, 0)
 
 
-def slab_terms_t(wpos, jloc, lower, own, upper, tb, halo_rows, row_count):
+def slab_terms_t(wpos, jloc, lower, own, upper, tb, xs_all, halo_rows, row_count):
     local_k = tb.shape[2] // B
     window_width = 5 * NCD * CB
     row_width = 3 * NCD * CB
@@ -113,12 +149,12 @@
             pl.BlockSpec(memory_space=pl.ANY),
             pl.BlockSpec(memory_space=pl.ANY),
             pl.BlockSpec(memory_space=pltpu.VMEM),
+            pl.BlockSpec(memory_space=pltpu.VMEM),
         ],
         out_specs=pl.BlockSpec(memory_space=pltpu.VMEM),
         scratch_shapes=[
             pltpu.VMEM((row_count + 2 * halo_rows,) + own.shape[1:], own.dtype),
             pltpu.VMEM((window_width, GROUP * B), jnp.float32),
-            pltpu.VMEM((row_width, GROUP * B), jnp.float32),
             pltpu.VMEM((256, 256), jnp.bfloat16),
             pltpu.SemaphoreType.DMA((3,)),
         ],
@@ -128,7 +164,7 @@
             bytes_accessed=(lower.size + own.size + upper.size) * 2 + tb.size * 2 + window_width * row_width * 4,
             transcendentals=0,
         ),
-    )(wpos, jloc, lower, own, upper, tb)
+    )(wpos, jloc, lower, own, upper, tb, xs_all)
 
 
 def on_device(tangent_blocks, tangent_columns, prolong_blocks, prolong_columns):
@@ -151,8 +187,10 @@
     jloc = (tangent_columns - slab_index * row_count + halo_rows) % fine_count
     jloc = jnp.clip(jloc, 0, row_count + 2 * halo_rows - 1).astype(jnp.int32).reshape(-1)
 
+    own_slots = ((prolong_columns // NCD - slab_index + 2) % slab_count) * NCD + prolong_columns % NCD
+    xs_all = row_side(own_slots.astype(jnp.int32).reshape(-1), prolong_blocks)
     gt = slab_terms_t(wpos, jloc, lower_blocks, prolong_blocks, upper_blocks, tangent_blocks,
-                      halo_rows, row_count)
+                      xs_all, halo_rows, row_count)
     terms = gt.T.reshape(3, NCD, CB, 5 * coarse_width)
 
     shares = lax.dynamic_index_in_dim(terms, lane_index, axis=1, keepdims=False)

time: 71.3 us -> 75.7 us (1.062)
  waiting for transfers between devices: 22.4 us -> 15.7 us
  Pallas kernels: 28.1 us -> 33.5 us
  starting transfers between devices: 16.1 us -> 19.2 us
  local copies, waits for them, and re-layouts: 3.63 us -> 6.17 us
    pallas_call x0 -> x1, Pallas kernels: none -> 6.97 us  [row_side(): pl.pallas_call(row_side_kernel, out_shape=jax.ShapeDtypeStruct(shape, jnp...]
    ppermute x9, waiting for transfers between devices: 22.4 us -> 15.7 us  [shifted(): return lax.ppermute(value, axis, pairs)]
    ppermute x9, starting transfers between devices: 16.1 us -> 19.2 us  [shifted(): return lax.ppermute(value, axis, pairs)]
    pallas_call x1, Pallas kernels: 28.1 us -> 26.5 us  [slab_terms_t(): pl.pallas_call(kernel, out_shape=jax.ShapeDtypeStruct((window_width, row_...]
    unnamed x6 -> x8, local copies, waits for them, and re-layouts: 0.01 us -> 1.6 us
    slice x1, local copies, waits for them, and re-layouts: 0.07 us -> 0.94 us  [on_device(): lower_columns = shifted(prolong_columns[row_count - halo_rows:], 'blk', 1)]
  transfers between devices with their start and end apart: 9 -> 9, of which waited for: 7 -> 6; matrix products, arithmetic and copies ran while one was open for 1% -> 5% of each run, Pallas kernels for 0% -> 9%
where the time goes in v7:
time: 75.7 us; the launch traced here: 75.5 us
  Pallas kernels  33.5 us (44%)
  starting transfers between devices  19.2 us (25%)
  waiting for transfers between devices  15.7 us (21%)
  local copies, waits for them, and re-layouts  6.17 us (8%)
  other arithmetic  0.91 us (1%)
    pallas_call x1, Pallas kernels, slab_terms_t(): pl.pallas_call(kernel, out_shape=jax.ShapeDtypeStruct((window_width, row_...  26.5 us
    ppermute x9, starting transfers between devices, shifted(): return lax.ppermute(value, axis, pairs)  19.2 us
    ppermute x9, waiting for transfers between devices, shifted(): return lax.ppermute(value, axis, pairs)  15.7 us
    pallas_call x1, Pallas kernels, row_side(): pl.pallas_call(row_side_kernel, out_shape=jax.ShapeDtypeStruct(shape, jnp...  6.97 us
    slice x1, local copies, waits for them, and re-layouts, on_device(): upper_blocks = shifted(prolong_blocks[:halo_rows], 'blk', -1)  2.68 us
    unnamed x8, local copies, waits for them, and re-layouts  1.6 us
  transfers between devices with their start and end apart: 9, of which 6 were waited for; matrix products, arithmetic and copies ran while one was open for 5% of the time, Pallas kernels for 9%

profile of v7, /device:TPU:0, one launch (start us, length us, event | category | flops | bytes accessed | tf_op | source)
XLA Modules:
  0.0 75.5 jit_solution(16675892446303255531)
XLA Ops:
  0.0 0.0 copy-start.2
  0.0 0.0 copy-start
  0.0 0.0 copy-start.3
  0.0 0.9 %fusion.17 = (s32[32,8]{0,1:T(8,128)S(1)}, s32[32,8]{0,1:T(8,128)S(1)}) fusion(s32[128,8]{0,1:T(8,128)} %param.7), kind=kLoop, calls=%fused_computation.47 | loop fusion | bytes 4096 | tf_op jit(solution)/shard_map/slice | solution.py:182
  0.9 5.8 %collective-permute-start.1 = (s32[32,8]{0,1:T(8,128)S(1)}, s32[32,8]{0,1:T(8,128)S(1)}, u32[]{:S(2)}, u32[]{:S(2)}) collective-permute-start(s32[32,8]{0,1:T(8,128)S(1)} %get-tuple-element.14), channel_id=1, source_target_pairs={{0,252},{4,0},{8,4},{12,8},{16,12},{20,16},{24,20},{28,24},{32,28}... | collective-permute-start | bytes 3080 | tf_op jit(solution)/shard_map/ppermute | solution.py:20
  6.7 0.0 collective-permute-start
  6.7 2.7 %fusion.16 = (bf16[32,24,512]{2,1,0:T(8,128)(2,1)}, bf16[32,24,512]{2,1,0:T(8,128)(2,1)}) fusion(bf16[128,24,512]{2,1,0:T(8,128)(2,1)} %own_ref.3), kind=kLoop, calls=%fused_computation.46 | loop fusion | bytes 3145728 | tf_op jit(solution)/shard_map/slice | solution.py:181
  9.4 0.0 collective-permute-start.2
  9.4 5.1 %collective-permute-start.3 = (bf16[32,24,512]{2,1,0:T(8,128)(2,1)}, bf16[32,24,512]{2,1,0:T(8,128)(2,1)}, u32[]{:S(2)}, u32[]{:S(2)}) collective-permute-start(bf16[32,24,512]{2,1,0:T(8,128)(2,1)} %get-tuple-element.5), channel_id=1, source_target_pairs={{0,252},{4,0},{8,4},{12,8},{16,12},{20,16},{24,20},{28,24},{32,28}... | collective-permute-start | bytes 2359304 | tf_op jit(solution)/shard_map/ppermute | solution.py:20
  14.4 0.0 copy-done.3
  14.5 0.0 copy-done.2
  14.5 0.1 copy.10
  14.6 0.1 reshape.11.jloc_ref
  14.8 0.1 copy.11
  14.9 0.1 reshape.12.wpos_ref
  15.0 0.0 copy-done
  15.0 7.0 %shard_map.46.xsall_ref = bf16[16,288,512]{2,1,0:T(8,128)(2,1)} custom-call(s32[1024]{0:T(1024)S(1)} %reshape.12.wpos_ref, bf16[128,24,512]{2,1,0:T(8,128)(2,1)S(1)} %copy-done), custom_call_target="tpu_custom_call" | custom-call | bytes 7864320 | tf_op jit(solution)/shard_map/pallas_call | solution.py:56
  21.9 0.0 collective-permute-done.1
  21.9 0.0 collective-permute-done
  22.0 0.1 pad_add_fusion
  22.0 0.1 copy.9
  22.1 0.1 concatenate.6
  22.3 2.1 %collective-permute-done.2.lower_ref = bf16[32,24,512]{2,1,0:T(8,128)(2,1)} collective-permute-done((bf16[32,24,512]{2,1,0:T(8,128)(2,1)}, bf16[32,24,512]{2,1,0:T(8,128)(2,1)}, u32[]{:S(2)}, u32[]{:S(2)}) %collective-permute-start.2) | collective-permute-done | bytes 786464 | tf_op jit(solution)/shard_map/ppermute | solution.py:20
  24.4 0.0 collective-permute-done.3.upper_ref
  24.4 0.0 copy-start.1
  24.4 1.6 %copy-done.1 = bf16[128,64,128]{2,1,0:T(8,128)(2,1)S(1)} copy-done((bf16[128,64,128]{2,1,0:T(8,128)(2,1)S(1)}, bf16[128,64,128]{2,1,0:T(8,128)(2,1)}, u32[]{:S(2)}) %copy-start.1) | copy-done | bytes 2097176
  26.0 26.5 %shard_map.47 = f32[480,288]{1,0:T(8,128)S(1)} custom-call(s32[1536]{0:T(1024)S(1)} %fusion.6.wpos_ref, s32[256]{0:T(256)S(1)} %reshape.11.jloc_ref, bf16[32,24,512]{2,1,0:T(8,128)(2,1)} %collective-permute-done.2.lower_ref, bf16[128,24,512]{2,1,0:T(8,128)(2,1)} %own_ref.3, bf16[32,24,512]{2,1,0:T(8,128)(2,1)} %collective-permute-done.3.upper_ref, ...), custom_call_target="tpu_custom_call" | custom-call | flops 8556380160 | bytes 7368704 | tf_op jit(solution)/shard_map/pallas_call | solution.py:142
  52.5 0.2 copy.12
  52.8 3.2 %collective-permute-start.6 = (f32[3,24,480]{2,1,0:T(8,128)S(1)}, f32[3,24,480]{2,1,0:T(8,128)S(1)}, u32[]{:S(2)}, u32[]{:S(2)}) collective-permute-start(f32[3,24,480]{2,1,0:T(8,128)S(1)} %get-tuple-element.8), channel_id=1, source_target_pairs={{0,3},{1,0},{2,1},{3,2},{4,7},{5,4},{6,5},{7,6},{8,11},{9,8},{10,9... | collective-permute-start | bytes 414728 | tf_op jit(solution)/shard_map/ppermute | solution.py:20
  56.0 0.6 collective-permute-start.5
  56.6 0.9 %collective-permute-start.4 = (f32[3,24,480]{2,1,0:T(8,128)S(1)}, f32[3,24,480]{2,1,0:T(8,128)S(1)}, u32[]{:S(2)}, u32[]{:S(2)}) collective-permute-start(f32[3,24,480]{2,1,0:T(8,128)S(1)} %get-tuple-element.7), channel_id=1, source_target_pairs={{0,1},{1,2},{2,3},{3,0},{4,5},{5,6},{6,7},{7,4},{8,9},{9,10},{10,1... | collective-permute-start | bytes 414728 | tf_op jit(solution)/shard_map/ppermute | solution.py:20
  57.5 2.8 %collective-permute-done.6 = f32[3,24,480]{2,1,0:T(8,128)S(1)} collective-permute-done((f32[3,24,480]{2,1,0:T(8,128)S(1)}, f32[3,24,480]{2,1,0:T(8,128)S(1)}, u32[]{:S(2)}, u32[]{:S(2)}) %collective-permute-start.6) | collective-permute-done | bytes 138272 | tf_op jit(solution)/shard_map/ppermute | solution.py:20
  60.3 2.5 %collective-permute-done.5 = f32[3,24,480]{2,1,0:T(8,128)S(1)} collective-permute-done((f32[3,24,480]{2,1,0:T(8,128)S(1)}, f32[3,24,480]{2,1,0:T(8,128)S(1)}, u32[]{:S(2)}, u32[]{:S(2)}) %collective-permute-start.5) | collective-permute-done | bytes 138272 | tf_op jit(solution)/shard_map/ppermute | solution.py:20
  62.7 1.5 %collective-permute-done.4 = f32[3,24,480]{2,1,0:T(8,128)S(1)} collective-permute-done((f32[3,24,480]{2,1,0:T(8,128)S(1)}, f32[3,24,480]{2,1,0:T(8,128)S(1)}, u32[]{:S(2)}, u32[]{:S(2)}) %collective-permute-start.4) | collective-permute-done | bytes 138272 | tf_op jit(solution)/shard_map/ppermute | solution.py:20
  64.3 3.7 %collective-permute-start.8 = (f32[24,480]{1,0:T(8,128)S(1)}, f32[24,480]{1,0:T(8,128)S(1)}, u32[]{:S(2)}, u32[]{:S(2)}) collective-permute-start(f32[24,480]{1,0:T(8,128)S(1)} %get-tuple-element.11), channel_id=1, source_target_pairs={{0,252},{4,0},{8,4},{12,8},{16,12},{20,16},{24,20},{28,24},{32,28}... | collective-permute-start | bytes 138248 | tf_op jit(solution)/shard_map/ppermute | solution.py:20
  68.0 0.0 collective-permute-start.7
  68.0 1.7 %collective-permute-done.8 = f32[24,480]{1,0:T(8,128)S(1)} collective-permute-done((f32[24,480]{1,0:T(8,128)S(1)}, f32[24,480]{1,0:T(8,128)S(1)}, u32[]{:S(2)}, u32[]{:S(2)}) %collective-permute-start.8) | collective-permute-done | bytes 46112 | tf_op jit(solution)/shard_map/ppermute | solution.py:20
  69.7 5.1 %collective-permute-done.7 = f32[24,480]{1,0:T(8,128)S(1)} collective-permute-done((f32[24,480]{1,0:T(8,128)S(1)}, f32[24,480]{1,0:T(8,128)S(1)}, u32[]{:S(2)}, u32[]{:S(2)}) %collective-permute-start.7) | collective-permute-done | bytes 46112 | tf_op jit(solution)/shard_map/ppermute | solution.py:20
  74.8 0.7 add_bitcast_fusion
  (6 shorter events, 0.1 us)
Async XLA Ops:
  0.0 14.5 %copy-start.2 = (s32[128,8]{0,1:T(8,128)S(1)}, s32[128,8]{0,1:T(8,128)}, u32[]{:S(2)}) copy-start(s32[128,8]{0,1:T(8,128)} %param.7) | copy-start | bytes 12292
  0.0 15.0 %copy-start = (bf16[128,24,512]{2,1,0:T(8,128)(2,1)S(1)}, bf16[128,24,512]{2,1,0:T(8,128)(2,1)}, u32[]{:S(2)}) copy-start(bf16[128,24,512]{2,1,0:T(8,128)(2,1)} %own_ref.3) | copy-start | bytes 9437188
  0.0 14.4 %copy-start.3 = (s32[128,2]{0,1:T(2,128)S(1)}, s32[128,2]{0,1:T(2,128)}, u32[]{:S(2)}) copy-start(s32[128,2]{0,1:T(2,128)} %param.5) | copy-start | bytes 3076
  0.9 21.0 %collective-permute-start.1 = (s32[32,8]{0,1:T(8,128)S(1)}, s32[32,8]{0,1:T(8,128)S(1)}, u32[]{:S(2)}, u32[]{:S(2)}) collective-permute-start(s32[32,8]{0,1:T(8,128)S(1)} %get-tuple-element.14), channel_id=1, source_target_pairs={{0,252},{4,0},{8,4},{12,8},{16,12},{20,16},{24,20},{28,24},{32,28}... | collective-permute-start | bytes 3080 | tf_op jit(solution)/shard_map/ppermute | solution.py:20
  6.7 15.3 %collective-permute-start = (s32[32,8]{0,1:T(8,128)S(1)}, s32[32,8]{0,1:T(8,128)S(1)}, u32[]{:S(2)}, u32[]{:S(2)}) collective-permute-start(s32[32,8]{0,1:T(8,128)S(1)} %get-tuple-element.13), channel_id=1, source_target_pairs={{0,4},{4,8},{8,12},{12,16},{16,20},{20,24},{24,28},{28,32},{32,36}... | collective-permute-start | bytes 3080 | tf_op jit(solution)/shard_map/ppermute | solution.py:20
  9.4 15.1 %collective-permute-start.2 = (bf16[32,24,512]{2,1,0:T(8,128)(2,1)}, bf16[32,24,512]{2,1,0:T(8,128)(2,1)}, u32[]{:S(2)}, u32[]{:S(2)}) collective-permute-start(bf16[32,24,512]{2,1,0:T(8,128)(2,1)} %get-tuple-element.6), channel_id=1, source_target_pairs={{0,4},{4,8},{8,12},{12,16},{16,20},{20,24},{24,28},{28,32},{32,36}... | collective-permute-start | bytes 2359304 | tf_op jit(solution)/shard_map/ppermute | solution.py:20
  9.4 15.1 %collective-permute-start.3 = (bf16[32,24,512]{2,1,0:T(8,128)(2,1)}, bf16[32,24,512]{2,1,0:T(8,128)(2,1)}, u32[]{:S(2)}, u32[]{:S(2)}) collective-permute-start(bf16[32,24,512]{2,1,0:T(8,128)(2,1)} %get-tuple-element.5), channel_id=1, source_target_pairs={{0,252},{4,0},{8,4},{12,8},{16,12},{20,16},{24,20},{28,24},{32,28}... | collective-permute-start | bytes 2359304 | tf_op jit(solution)/shard_map/ppermute | solution.py:20
  24.4 1.6 %copy-start.1 = (bf16[128,64,128]{2,1,0:T(8,128)(2,1)S(1)}, bf16[128,64,128]{2,1,0:T(8,128)(2,1)}, u32[]{:S(2)}) copy-start(bf16[128,64,128]{2,1,0:T(8,128)(2,1)} %tb_ref.1) | copy-start | bytes 6291460
  52.8 7.4 %collective-permute-start.6 = (f32[3,24,480]{2,1,0:T(8,128)S(1)}, f32[3,24,480]{2,1,0:T(8,128)S(1)}, u32[]{:S(2)}, u32[]{:S(2)}) collective-permute-start(f32[3,24,480]{2,1,0:T(8,128)S(1)} %get-tuple-element.8), channel_id=1, source_target_pairs={{0,3},{1,0},{2,1},{3,2},{4,7},{5,4},{6,5},{7,6},{8,11},{9,8},{10,9... | collective-permute-start | bytes 414728 | tf_op jit(solution)/shard_map/ppermute | solution.py:20
  56.0 6.8 %collective-permute-start.5 = (f32[3,24,480]{2,1,0:T(8,128)S(1)}, f32[3,24,480]{2,1,0:T(8,128)S(1)}, u32[]{:S(2)}, u32[]{:S(2)}) collective-permute-start(f32[3,24,480]{2,1,0:T(8,128)S(1)} %get-tuple-element.9), channel_id=1, source_target_pairs={{0,2},{1,3},{2,0},{3,1},{4,6},{5,7},{6,4},{7,5},{8,10},{9,11},{10,... | collective-permute-start | bytes 414728 | tf_op jit(solution)/shard_map/ppermute | solution.py:20
  56.6 7.6 %collective-permute-start.4 = (f32[3,24,480]{2,1,0:T(8,128)S(1)}, f32[3,24,480]{2,1,0:T(8,128)S(1)}, u32[]{:S(2)}, u32[]{:S(2)}) collective-permute-start(f32[3,24,480]{2,1,0:T(8,128)S(1)} %get-tuple-element.7), channel_id=1, source_target_pairs={{0,1},{1,2},{2,3},{3,0},{4,5},{5,6},{6,7},{7,4},{8,9},{9,10},{10,1... | collective-permute-start | bytes 414728 | tf_op jit(solution)/shard_map/ppermute | solution.py:20
  64.3 5.4 %collective-permute-start.8 = (f32[24,480]{1,0:T(8,128)S(1)}, f32[24,480]{1,0:T(8,128)S(1)}, u32[]{:S(2)}, u32[]{:S(2)}) collective-permute-start(f32[24,480]{1,0:T(8,128)S(1)} %get-tuple-element.11), channel_id=1, source_target_pairs={{0,252},{4,0},{8,4},{12,8},{16,12},{20,16},{24,20},{28,24},{32,28}... | collective-permute-start | bytes 138248 | tf_op jit(solution)/shard_map/ppermute | solution.py:20
  68.0 6.8 %collective-permute-start.7 = (f32[24,480]{1,0:T(8,128)S(1)}, f32[24,480]{1,0:T(8,128)S(1)}, u32[]{:S(2)}, u32[]{:S(2)}) collective-permute-start(f32[24,480]{1,0:T(8,128)S(1)} %get-tuple-element.12), channel_id=1, source_target_pairs={{0,4},{4,8},{8,12},{12,16},{16,20},{20,24},{24,28},{28,32},{32,36}... | collective-permute-start | bytes 138248 | tf_op jit(solution)/shard_map/ppermute | solution.py:20

commit v8 on v6

--- a/solution.py
+++ b/solution.py
@@ -25,7 +25,7 @@
 
 
 def slab_kernel(halo_rows, row_count, local_k, wpos_ref, jloc_ref, lower_ref, own_ref, upper_ref,
-                tb_ref, gt_ref, pb_ref, s_ref, xs_ref, w_ref, sems):
+                tb_ref, gt_ref, pb_ref, s_ref, xs_ref, w_ref, qall_ref, xall_ref, sems):
     copies = [
         pltpu.make_async_copy(lower_ref, pb_ref.at[0:halo_rows], sems.at[0]),
         pltpu.make_async_copy(own_ref, pb_ref.at[halo_rows:halo_rows + row_count], sems.at[1]),
@@ -65,6 +65,8 @@
                 slot = jnp.clip(w - NCD, 0, row_slots - 1)
                 place(xs_ref, slot, m // 2, m % 2 == 1, r, p)
         xsb = xs_ref[...].astype(bf16)
+        span = pl.ds(pl.multiple_of(g * GROUP * B, GROUP * B), GROUP * B)
+        xall_ref[:, span] = xsb
         for k in range(local_k):
             s_ref[...] = jnp.zeros(s_ref.shape, f32)
             for m in range(GROUP):
@@ -88,13 +90,16 @@
                     window, w_ref[...], (((1,), (1,)), ((), ())), preferred_element_type=f32
                 )
                 parts.append(q.astype(bf16))
-            qt = jnp.concatenate(parts, axis=1)
-            gt_ref[...] += lax.dot_general(
-                qt, xsb, (((1,), (1,)), ((), ())), preferred_element_type=f32
-            )
+            qall_ref[k, :, span] = jnp.concatenate(parts, axis=1)
         return carry
 
     lax.fori_loop(0, row_count // GROUP, group, 0)
+    total = lax.dot_general(qall_ref[0], xall_ref[...], (((1,), (1,)), ((), ())),
+                            preferred_element_type=f32)
+    for k in range(1, local_k):
+        total = total + lax.dot_general(qall_ref[k], xall_ref[...], (((1,), (1,)), ((), ())),
+                                        preferred_element_type=f32)
+    gt_ref[...] = total
 
 
 def slab_terms_t(wpos, jloc, lower, own, upper, tb, halo_rows, row_count):
@@ -120,9 +125,11 @@
             pltpu.VMEM((window_width, GROUP * B), jnp.float32),
             pltpu.VMEM((row_width, GROUP * B), jnp.float32),
             pltpu.VMEM((256, 256), jnp.bfloat16),
+            pltpu.VMEM((local_k, window_width, row_count * B), jnp.bfloat16),
+            pltpu.VMEM((row_width, row_count * B), jnp.bfloat16),
             pltpu.SemaphoreType.DMA((3,)),
         ],
-        compiler_params=pltpu.CompilerParams(vmem_limit_bytes=48 * 1024 * 1024),
+        compiler_params=pltpu.CompilerParams(vmem_limit_bytes=60 * 1024 * 1024),
         cost_estimate=pl.CostEstimate(
             flops=flops,
             bytes_accessed=(lower.size + own.size + upper.size) * 2 + tb.size * 2 + window_width * row_width * 4,

time: 71.3 us -> 75.5 us (1.059)
  local copies, waits for them, and re-layouts: 3.63 us -> 5.84 us
  Pallas kernels: 28.1 us -> 30.2 us
  waiting for transfers between devices: 22.4 us -> 21.5 us
    pallas_call x1, Pallas kernels: 28.1 us -> 30.2 us  [slab_terms_t(): pl.pallas_call(kernel, out_shape=jax.ShapeDtypeStruct((window_width, row_...]
    unnamed x6 -> x8, local copies, waits for them, and re-layouts: 0.01 us -> 1.82 us
    slice x1, local copies, waits for them, and re-layouts: 2.79 us -> 1.5 us  [on_device(): upper_blocks = shifted(prolong_blocks[:halo_rows], 'blk', -1)]
    transpose x1, local copies, waits for them, and re-layouts: 0.24 us -> 1.35 us  [on_device(): terms = gt.T.reshape(3, NCD, CB, 5 * coarse_width)]
    ppermute x9, waiting for transfers between devices: 22.4 us -> 21.5 us  [shifted(): return lax.ppermute(value, axis, pairs)]
  transfers between devices with their start and end apart: 9 -> 9, of which waited for: 7 -> 7; matrix products, arithmetic and copies ran while one was open for 1% -> 2% of each run, Pallas kernels for 0% -> 0%
where the time goes in v8:
time: 75.5 us; the launch traced here: 75.3 us
  Pallas kernels  30.2 us (40%)
  waiting for transfers between devices  21.5 us (28%)
  starting transfers between devices  16.3 us (22%)
  local copies, waits for them, and re-layouts  5.84 us (8%)
  other arithmetic  1.49 us (2%)
    pallas_call x1, Pallas kernels, slab_terms_t(): pl.pallas_call(kernel, out_shape=jax.ShapeDtypeStruct((window_width, row_...  30.2 us
    ppermute x9, waiting for transfers between devices, shifted(): return lax.ppermute(value, axis, pairs)  21.5 us
    ppermute x9, starting transfers between devices, shifted(): return lax.ppermute(value, axis, pairs)  16.3 us
    unnamed x8, local copies, waits for them, and re-layouts  1.82 us
  transfers between devices with their start and end apart: 9, of which 7 were waited for; matrix products, arithmetic and copies ran while one was open for 2% of the time, Pallas kernels for 0%

profile of v8, /device:TPU:0, one launch (start us, length us, event | category | flops | bytes accessed | tf_op | source)
XLA Modules:
  0.0 75.3 jit_solution(16251321151120315011)
XLA Ops:
  0.0 0.0 copy-start
  0.0 0.0 copy-start.1
  0.0 1.5 %fusion.10 = (bf16[32,24,512]{2,1,0:T(8,128)(2,1)S(1)}, bf16[32,24,512]{2,1,0:T(8,128)(2,1)S(1)}) fusion(bf16[128,24,512]{2,1,0:T(8,128)(2,1)} %own_ref.1), kind=kLoop, calls=%fused_computation.31 | loop fusion | bytes 3145728 | tf_op jit(solution)/shard_map/slice | solution.py:152
  1.5 0.1 collective-permute-start.2
  1.6 5.8 %collective-permute-start.3 = (bf16[32,24,512]{2,1,0:T(8,128)(2,1)S(1)}, bf16[32,24,512]{2,1,0:T(8,128)(2,1)S(1)}, u32[]{:S(2)}, u32[]{:S(2)}) collective-permute-start(bf16[32,24,512]{2,1,0:T(8,128)(2,1)S(1)} %get-tuple-element.5), channel_id=1, source_target_pairs={{0,252},{4,0},{8,4},{12,8},{16,12},{20,16},{24,20},{28,24},{32,28}... | collective-permute-start | bytes 2359304 | tf_op jit(solution)/shard_map/ppermute | solution.py:20
  7.4 0.0 copy-done
  7.4 0.1 fusion.11
  7.5 0.7 collective-permute-start.1
  8.2 0.0 collective-permute-start
  8.2 0.0 copy-done.1
  8.2 0.1 copy.10
  8.3 0.7 reshape.8.jloc_ref
  9.1 7.9 %collective-permute-done.1 = s32[32,8]{0,1:T(8,128)S(1)} collective-permute-done((s32[32,8]{0,1:T(8,128)S(1)}, s32[32,8]{0,1:T(8,128)S(1)}, u32[]{:S(2)}, u32[]{:S(2)}) %collective-permute-start.1) | collective-permute-done | bytes 1056 | tf_op jit(solution)/shard_map/ppermute | solution.py:20
  17.0 0.1 collective-permute-done
  17.1 0.1 pad_add_fusion
  17.1 0.1 copy.9
  17.2 0.1 concatenate.6
  17.4 0.6 fusion.6.wpos_ref
  18.0 0.0 collective-permute-done.2.lower_ref
  18.0 0.0 copy-start.2
  18.0 0.0 collective-permute-done.3.upper_ref
  18.0 0.9 %copy-done.2 = bf16[32,24,512]{2,1,0:T(8,128)(2,1)} copy-done((bf16[32,24,512]{2,1,0:T(8,128)(2,1)}, bf16[32,24,512]{2,1,0:T(8,128)(2,1)S(1)}, u32[]{:S(2)}) %copy-start.2) | copy-done | bytes 786456
  18.9 0.0 copy-start.3
  18.9 0.9 %copy-done.3 = bf16[32,24,512]{2,1,0:T(8,128)(2,1)} copy-done((bf16[32,24,512]{2,1,0:T(8,128)(2,1)}, bf16[32,24,512]{2,1,0:T(8,128)(2,1)S(1)}, u32[]{:S(2)}) %copy-start.3) | copy-done | bytes 786456
  19.8 30.2 %shard_map.46 = f32[480,288]{1,0:T(8,128)} custom-call(s32[1536]{0:T(1024)} %fusion.6.wpos_ref, s32[256]{0:T(256)} %reshape.8.jloc_ref, bf16[32,24,512]{2,1,0:T(8,128)(2,1)} %copy-done.2, bf16[128,24,512]{2,1,0:T(8,128)(2,1)} %own_ref.1, bf16[32,24,512]{2,1,0:T(8,128)(2,1)} %copy-done.3, bf16[128,64,128]{2,1,0:T(8,128)(2,1)} %tb_ref.1), custom_call_target="tpu_custom_call" | custom-call | flops 8556380160 | bytes 7368704 | tf_op jit(solution)/shard_map/pallas_call | solution.py:111
  50.0 1.4 %copy.11 = f32[288,480]{1,0:T(8,128)S(1)} copy(f32[288,480]{0,1:T(8,128)} %bitcast.24) | data formatting | bytes 1105920 | tf_op jit(solution)/shard_map/transpose | solution.py:163
  51.4 3.1 %collective-permute-start.6 = (f32[3,24,480]{2,1,0:T(8,128)S(1)}, f32[3,24,480]{2,1,0:T(8,128)S(1)}, u32[]{:S(2)}, u32[]{:S(2)}) collective-permute-start(f32[3,24,480]{2,1,0:T(8,128)S(1)} %get-tuple-element.8), channel_id=1, source_target_pairs={{0,3},{1,0},{2,1},{3,2},{4,7},{5,4},{6,5},{7,6},{8,11},{9,8},{10,9... | collective-permute-start | bytes 414728 | tf_op jit(solution)/shard_map/ppermute | solution.py:20
  54.5 0.6 collective-permute-start.5
  55.1 1.0 %collective-permute-start.4 = (f32[3,24,480]{2,1,0:T(8,128)S(1)}, f32[3,24,480]{2,1,0:T(8,128)S(1)}, u32[]{:S(2)}, u32[]{:S(2)}) collective-permute-start(f32[3,24,480]{2,1,0:T(8,128)S(1)} %get-tuple-element.7), channel_id=1, source_target_pairs={{0,1},{1,2},{2,3},{3,0},{4,5},{5,6},{6,7},{7,4},{8,9},{9,10},{10,1... | collective-permute-start | bytes 414728 | tf_op jit(solution)/shard_map/ppermute | solution.py:20
  56.1 2.7 %collective-permute-done.6 = f32[3,24,480]{2,1,0:T(8,128)S(1)} collective-permute-done((f32[3,24,480]{2,1,0:T(8,128)S(1)}, f32[3,24,480]{2,1,0:T(8,128)S(1)}, u32[]{:S(2)}, u32[]{:S(2)}) %collective-permute-start.6) | collective-permute-done | bytes 138272 | tf_op jit(solution)/shard_map/ppermute | solution.py:20
  58.7 2.5 %collective-permute-done.5 = f32[3,24,480]{2,1,0:T(8,128)S(1)} collective-permute-done((f32[3,24,480]{2,1,0:T(8,128)S(1)}, f32[3,24,480]{2,1,0:T(8,128)S(1)}, u32[]{:S(2)}, u32[]{:S(2)}) %collective-permute-start.5) | collective-permute-done | bytes 138272 | tf_op jit(solution)/shard_map/ppermute | solution.py:20
  61.2 1.5 %collective-permute-done.4 = f32[3,24,480]{2,1,0:T(8,128)S(1)} collective-permute-done((f32[3,24,480]{2,1,0:T(8,128)S(1)}, f32[3,24,480]{2,1,0:T(8,128)S(1)}, u32[]{:S(2)}, u32[]{:S(2)}) %collective-permute-start.4) | collective-permute-done | bytes 138272 | tf_op jit(solution)/shard_map/ppermute | solution.py:20
  62.8 5.0 %collective-permute-start.8 = (f32[24,480]{1,0:T(8,128)S(1)}, f32[24,480]{1,0:T(8,128)S(1)}, u32[]{:S(2)}, u32[]{:S(2)}) collective-permute-start(f32[24,480]{1,0:T(8,128)S(1)} %get-tuple-element.11), channel_id=1, source_target_pairs={{0,252},{4,0},{8,4},{12,8},{16,12},{20,16},{24,20},{28,24},{32,28}... | collective-permute-start | bytes 138248 | tf_op jit(solution)/shard_map/ppermute | solution.py:20
  67.7 0.0 collective-permute-start.7
  67.7 1.7 %collective-permute-done.8 = f32[24,480]{1,0:T(8,128)S(1)} collective-permute-done((f32[24,480]{1,0:T(8,128)S(1)}, f32[24,480]{1,0:T(8,128)S(1)}, u32[]{:S(2)}, u32[]{:S(2)}) %collective-permute-start.8) | collective-permute-done | bytes 46112 | tf_op jit(solution)/shard_map/ppermute | solution.py:20
  69.5 5.1 %collective-permute-done.7 = f32[24,480]{1,0:T(8,128)S(1)} collective-permute-done((f32[24,480]{1,0:T(8,128)S(1)}, f32[24,480]{1,0:T(8,128)S(1)}, u32[]{:S(2)}, u32[]{:S(2)}) %collective-permute-start.7) | collective-permute-done | bytes 46112 | tf_op jit(solution)/shard_map/ppermute | solution.py:20
  74.6 0.7 add_bitcast_fusion
  (4 shorter events, 0.1 us)
Async XLA Ops:
  0.0 7.4 %copy-start = (s32[128,8]{0,1:T(8,128)S(1)}, s32[128,8]{0,1:T(8,128)}, u32[]{:S(2)}) copy-start(s32[128,8]{0,1:T(8,128)} %param.7) | copy-start | bytes 12292
  0.0 8.2 %copy-start.1 = (s32[128,2]{0,1:T(2,128)S(1)}, s32[128,2]{0,1:T(2,128)}, u32[]{:S(2)}) copy-start(s32[128,2]{0,1:T(2,128)} %param.5) | copy-start | bytes 3076
  1.5 16.5 %collective-permute-start.2 = (bf16[32,24,512]{2,1,0:T(8,128)(2,1)S(1)}, bf16[32,24,512]{2,1,0:T(8,128)(2,1)S(1)}, u32[]{:S(2)}, u32[]{:S(2)}) collective-permute-start(bf16[32,24,512]{2,1,0:T(8,128)(2,1)S(1)} %get-tuple-element.6), channel_id=1, source_target_pairs={{0,4},{4,8},{8,12},{12,16},{16,20},{20,24},{24,28},{28,32},{32,36}... | collective-permute-start | bytes 2359304 | tf_op jit(solution)/shard_map/ppermute | solution.py:20
  1.6 16.4 %collective-permute-start.3 = (bf16[32,24,512]{2,1,0:T(8,128)(2,1)S(1)}, bf16[32,24,512]{2,1,0:T(8,128)(2,1)S(1)}, u32[]{:S(2)}, u32[]{:S(2)}) collective-permute-start(bf16[32,24,512]{2,1,0:T(8,128)(2,1)S(1)} %get-tuple-element.5), channel_id=1, source_target_pairs={{0,252},{4,0},{8,4},{12,8},{16,12},{20,16},{24,20},{28,24},{32,28}... | collective-permute-start | bytes 2359304 | tf_op jit(solution)/shard_map/ppermute | solution.py:20
  7.5 9.5 %collective-permute-start.1 = (s32[32,8]{0,1:T(8,128)S(1)}, s32[32,8]{0,1:T(8,128)S(1)}, u32[]{:S(2)}, u32[]{:S(2)}) collective-permute-start(s32[32,8]{0,1:T(8,128)S(1)} %get-tuple-element.14), channel_id=1, source_target_pairs={{0,252},{4,0},{8,4},{12,8},{16,12},{20,16},{24,20},{28,24},{32,28}... | collective-permute-start | bytes 3080 | tf_op jit(solution)/shard_map/ppermute | solution.py:20
  8.2 8.9 %collective-permute-start = (s32[32,8]{0,1:T(8,128)S(1)}, s32[32,8]{0,1:T(8,128)S(1)}, u32[]{:S(2)}, u32[]{:S(2)}) collective-permute-start(s32[32,8]{0,1:T(8,128)S(1)} %get-tuple-element.13), channel_id=1, source_target_pairs={{0,4},{4,8},{8,12},{12,16},{16,20},{20,24},{24,28},{28,32},{32,36}... | collective-permute-start | bytes 3080 | tf_op jit(solution)/shard_map/ppermute | solution.py:20
  18.0 0.9 %copy-start.2 = (bf16[32,24,512]{2,1,0:T(8,128)(2,1)}, bf16[32,24,512]{2,1,0:T(8,128)(2,1)S(1)}, u32[]{:S(2)}) copy-start(bf16[32,24,512]{2,1,0:T(8,128)(2,1)S(1)} %collective-permute-done.2.lower_ref) | copy-start | bytes 2359300
  18.9 0.9 %copy-start.3 = (bf16[32,24,512]{2,1,0:T(8,128)(2,1)}, bf16[32,24,512]{2,1,0:T(8,128)(2,1)S(1)}, u32[]{:S(2)}) copy-start(bf16[32,24,512]{2,1,0:T(8,128)(2,1)S(1)} %collective-permute-done.3.upper_ref) | copy-start | bytes 2359300
  51.4 7.4 %collective-permute-start.6 = (f32[3,24,480]{2,1,0:T(8,128)S(1)}, f32[3,24,480]{2,1,0:T(8,128)S(1)}, u32[]{:S(2)}, u32[]{:S(2)}) collective-permute-start(f32[3,24,480]{2,1,0:T(8,128)S(1)} %get-tuple-element.8), channel_id=1, source_target_pairs={{0,3},{1,0},{2,1},{3,2},{4,7},{5,4},{6,5},{7,6},{8,11},{9,8},{10,9... | collective-permute-start | bytes 414728 | tf_op jit(solution)/shard_map/ppermute | solution.py:20
  54.5 6.8 %collective-permute-start.5 = (f32[3,24,480]{2,1,0:T(8,128)S(1)}, f32[3,24,480]{2,1,0:T(8,128)S(1)}, u32[]{:S(2)}, u32[]{:S(2)}) collective-permute-start(f32[3,24,480]{2,1,0:T(8,128)S(1)} %get-tuple-element.9), channel_id=1, source_target_pairs={{0,2},{1,3},{2,0},{3,1},{4,6},{5,7},{6,4},{7,5},{8,10},{9,11},{10,... | collective-permute-start | bytes 414728 | tf_op jit(solution)/shard_map/ppermute | solution.py:20
  55.1 7.6 %collective-permute-start.4 = (f32[3,24,480]{2,1,0:T(8,128)S(1)}, f32[3,24,480]{2,1,0:T(8,128)S(1)}, u32[]{:S(2)}, u32[]{:S(2)}) collective-permute-start(f32[3,24,480]{2,1,0:T(8,128)S(1)} %get-tuple-element.7), channel_id=1, source_target_pairs={{0,1},{1,2},{2,3},{3,0},{4,5},{5,6},{6,7},{7,4},{8,9},{9,10},{10,1... | collective-permute-start | bytes 414728 | tf_op jit(solution)/shard_map/ppermute | solution.py:20
  62.8 6.7 %collective-permute-start.8 = (f32[24,480]{1,0:T(8,128)S(1)}, f32[24,480]{1,0:T(8,128)S(1)}, u32[]{:S(2)}, u32[]{:S(2)}) collective-permute-start(f32[24,480]{1,0:T(8,128)S(1)} %get-tuple-element.11), channel_id=1, source_target_pairs={{0,252},{4,0},{8,4},{12,8},{16,12},{20,16},{24,20},{28,24},{32,28}... | collective-permute-start | bytes 138248 | tf_op jit(solution)/shard_map/ppermute | solution.py:20
  67.7 6.8 %collective-permute-start.7 = (f32[24,480]{1,0:T(8,128)S(1)}, f32[24,480]{1,0:T(8,128)S(1)}, u32[]{:S(2)}, u32[]{:S(2)}) collective-permute-start(f32[24,480]{1,0:T(8,128)S(1)} %get-tuple-element.12), channel_id=1, source_target_pairs={{0,4},{4,8},{8,12},{12,16},{16,20},{20,24},{24,28},{28,32},{32,36}... | collective-permute-start | bytes 138248 | tf_op jit(solution)/shard_map/ppermute | solution.py:20

commit v9 on v6

--- a/solution.py
+++ b/solution.py
@@ -22,6 +22,32 @@
 
 def widen(values, left_pad, right_pad):
     return jnp.pad(values, ((0, 0),) * (values.ndim - 1) + ((left_pad, right_pad),))
+
+
+def send_rows_kernel(halo_rows, src_ref, tail_ref, head_ref, sems):
+    row_count = src_ref.shape[0]
+    copies = [
+        pltpu.make_async_copy(src_ref.at[row_count - halo_rows:row_count], tail_ref, sems.at[0]),
+        pltpu.make_async_copy(src_ref.at[0:halo_rows], head_ref, sems.at[1]),
+    ]
+    for copy in copies:
+        copy.start()
+    for copy in copies:
+        copy.wait()
+
+
+def send_rows(blocks, halo_rows):
+    piece = jax.ShapeDtypeStruct((halo_rows,) + blocks.shape[1:], blocks.dtype)
+    return pl.pallas_call(
+        functools.partial(send_rows_kernel, halo_rows),
+        out_shape=(piece, piece),
+        in_specs=[pl.BlockSpec(memory_space=pl.ANY)],
+        out_specs=(pl.BlockSpec(memory_space=pl.ANY), pl.BlockSpec(memory_space=pl.ANY)),
+        scratch_shapes=[pltpu.SemaphoreType.DMA((2,))],
+        cost_estimate=pl.CostEstimate(
+            flops=0, bytes_accessed=4 * halo_rows * blocks[0].size * 2, transcendentals=0
+        ),
+    )(blocks)
 
 
 def slab_kernel(halo_rows, row_count, local_k, wpos_ref, jloc_ref, lower_ref, own_ref, upper_ref,
@@ -141,8 +167,9 @@
     coarse_width = NCD * CB
     fine_count = row_count * slab_count
 
-    lower_blocks = shifted(prolong_blocks[row_count - halo_rows:], "blk", 1)
-    upper_blocks = shifted(prolong_blocks[:halo_rows], "blk", -1)
+    tail_rows, head_rows = send_rows(prolong_blocks, halo_rows)
+    lower_blocks = shifted(tail_rows, "blk", 1)
+    upper_blocks = shifted(head_rows, "blk", -1)
     lower_columns = shifted(prolong_columns[row_count - halo_rows:], "blk", 1)
     upper_columns = shifted(prolong_columns[:halo_rows], "blk", -1)
     near_columns = jnp.concatenate([lower_columns, prolong_columns, upper_columns], axis=0)

time: 71.3 us -> 118 us (1.65)
  Pallas kernels: 28.1 us -> 77.3 us
  local copies, waits for them, and re-layouts: 3.63 us -> 0.83 us
    pallas_call x0 -> x1, Pallas kernels: none -> 48.8 us  [send_rows(): pl.pallas_call(functools.partial(send_rows_kernel, halo_rows), out_shape=...]
    slice x1 -> x0, local copies, waits for them, and re-layouts: 2.79 us -> none  [on_device(): upper_blocks = shifted(prolong_blocks[:halo_rows], 'blk', -1)]
where the time goes in v9:
time: 118 us
  Pallas kernels  77.3 us (66%)
  waiting for transfers between devices  22.3 us (19%)
  starting transfers between devices  16.2 us (14%)
    pallas_call x1, Pallas kernels, send_rows(): pl.pallas_call(functools.partial(send_rows_kernel, halo_rows), out_shape=...  48.8 us
    pallas_call x1, Pallas kernels, slab_terms_t(): pl.pallas_call(kernel, out_shape=jax.ShapeDtypeStruct((window_width, row_...  28.5 us
    ppermute x9, waiting for transfers between devices, shifted(): return lax.ppermute(value, axis, pairs)  22.3 us
    ppermute x9, starting transfers between devices, shifted(): return lax.ppermute(value, axis, pairs)  16.2 us
  transfers between devices with their start and end apart: 9, of which 7 were waited for; matrix products, arithmetic and copies ran while one was open for 1% of the time, Pallas kernels for 0%

profile of v9, /device:TPU:0, one launch (start us, length us, event | category | flops | bytes accessed | tf_op | source)
XLA Modules:
  0.0 117.7 jit_solution(3867835470018154502)
XLA Ops:
  0.0 0.0 copy-start.1
  0.0 0.0 copy-start.2
  0.0 0.0 copy-start
  0.0 48.8 %shard_map.46 = (bf16[32,24,512]{2,1,0:T(8,128)(2,1)}, bf16[32,24,512]{2,1,0:T(8,128)(2,1)}) custom-call(bf16[128,24,512]{2,1,0:T(8,128)(2,1)} %own_ref.1), custom_call_target="tpu_custom_call" | custom-call | bytes 3145728 | tf_op jit(solution)/shard_map/pallas_call | solution.py:41
  48.8 0.1 collective-permute-start.2
  48.9 5.8 %collective-permute-start.3 = (bf16[32,24,512]{2,1,0:T(8,128)(2,1)}, bf16[32,24,512]{2,1,0:T(8,128)(2,1)}, u32[]{:S(2)}, u32[]{:S(2)}) collective-permute-start(bf16[32,24,512]{2,1,0:T(8,128)(2,1)} %get-tuple-element.8), channel_id=1, source_target_pairs={{0,252},{4,0},{8,4},{12,8},{16,12},{20,16},{24,20},{28,24},{32,28}... | collective-permute-start | bytes 2359304 | tf_op jit(solution)/shard_map/ppermute | solution.py:20
  54.7 0.0 copy-done.1
  54.7 0.1 fusion.10
  54.8 0.7 collective-permute-start.1
  55.5 0.0 collective-permute-start
  55.5 0.0 copy-done.2
  55.5 0.1 copy.10
  55.6 0.1 reshape.8.jloc_ref
  55.8 8.8 %collective-permute-done.1 = s32[32,8]{0,1:T(8,128)S(1)} collective-permute-done((s32[32,8]{0,1:T(8,128)S(1)}, s32[32,8]{0,1:T(8,128)S(1)}, u32[]{:S(2)}, u32[]{:S(2)}) %collective-permute-start.1) | collective-permute-done | bytes 1056 | tf_op jit(solution)/shard_map/ppermute | solution.py:20
  64.5 0.1 collective-permute-done
  64.6 0.1 pad_add_fusion
  64.7 0.1 copy.9
  64.8 0.1 concatenate.6
  64.9 0.0 collective-permute-done.2.lower_ref
  65.0 0.0 collective-permute-done.3.upper_ref
  65.0 0.0 copy-done
  65.0 28.5 %shard_map.47 = f32[480,288]{1,0:T(8,128)S(1)} custom-call(s32[1536]{0:T(1024)S(1)} %fusion.6.wpos_ref, s32[256]{0:T(256)S(1)} %reshape.8.jloc_ref, bf16[32,24,512]{2,1,0:T(8,128)(2,1)} %collective-permute-done.2.lower_ref, bf16[128,24,512]{2,1,0:T(8,128)(2,1)} %own_ref.1, bf16[32,24,512]{2,1,0:T(8,128)(2,1)} %collective-permute-done.3.upper_ref, ...), custom_call_target="tpu_custom_call" | custom-call | flops 8556380160 | bytes 7368704 | tf_op jit(solution)/shard_map/pallas_call | solution.py:132
  93.5 0.2 copy.11
  93.8 3.1 %collective-permute-start.6 = (f32[3,24,480]{2,1,0:T(8,128)S(1)}, f32[3,24,480]{2,1,0:T(8,128)S(1)}, u32[]{:S(2)}, u32[]{:S(2)}) collective-permute-start(f32[3,24,480]{2,1,0:T(8,128)S(1)} %get-tuple-element.10), channel_id=1, source_target_pairs={{0,3},{1,0},{2,1},{3,2},{4,7},{5,4},{6,5},{7,6},{8,11},{9,8},{10,9... | collective-permute-start | bytes 414728 | tf_op jit(solution)/shard_map/ppermute | solution.py:20
  96.9 0.6 collective-permute-start.5
  97.5 1.0 collective-permute-start.4
  98.5 2.7 %collective-permute-done.6 = f32[3,24,480]{2,1,0:T(8,128)S(1)} collective-permute-done((f32[3,24,480]{2,1,0:T(8,128)S(1)}, f32[3,24,480]{2,1,0:T(8,128)S(1)}, u32[]{:S(2)}, u32[]{:S(2)}) %collective-permute-start.6) | collective-permute-done | bytes 138272 | tf_op jit(solution)/shard_map/ppermute | solution.py:20
  101.2 2.5 %collective-permute-done.5 = f32[3,24,480]{2,1,0:T(8,128)S(1)} collective-permute-done((f32[3,24,480]{2,1,0:T(8,128)S(1)}, f32[3,24,480]{2,1,0:T(8,128)S(1)}, u32[]{:S(2)}, u32[]{:S(2)}) %collective-permute-start.5) | collective-permute-done | bytes 138272 | tf_op jit(solution)/shard_map/ppermute | solution.py:20
  103.6 1.5 %collective-permute-done.4 = f32[3,24,480]{2,1,0:T(8,128)S(1)} collective-permute-done((f32[3,24,480]{2,1,0:T(8,128)S(1)}, f32[3,24,480]{2,1,0:T(8,128)S(1)}, u32[]{:S(2)}, u32[]{:S(2)}) %collective-permute-start.4) | collective-permute-done | bytes 138272 | tf_op jit(solution)/shard_map/ppermute | solution.py:20
  105.2 5.0 %collective-permute-start.8 = (f32[24,480]{1,0:T(8,128)S(1)}, f32[24,480]{1,0:T(8,128)S(1)}, u32[]{:S(2)}, u32[]{:S(2)}) collective-permute-start(f32[24,480]{1,0:T(8,128)S(1)} %get-tuple-element.13), channel_id=1, source_target_pairs={{0,252},{4,0},{8,4},{12,8},{16,12},{20,16},{24,20},{28,24},{32,28}... | collective-permute-start | bytes 138248 | tf_op jit(solution)/shard_map/ppermute | solution.py:20
  110.1 0.0 collective-permute-start.7
  110.1 1.7 %collective-permute-done.8 = f32[24,480]{1,0:T(8,128)S(1)} collective-permute-done((f32[24,480]{1,0:T(8,128)S(1)}, f32[24,480]{1,0:T(8,128)S(1)}, u32[]{:S(2)}, u32[]{:S(2)}) %collective-permute-start.8) | collective-permute-done | bytes 46112 | tf_op jit(solution)/shard_map/ppermute | solution.py:20
  111.9 5.1 %collective-permute-done.7 = f32[24,480]{1,0:T(8,128)S(1)} collective-permute-done((f32[24,480]{1,0:T(8,128)S(1)}, f32[24,480]{1,0:T(8,128)S(1)}, u32[]{:S(2)}, u32[]{:S(2)}) %collective-permute-start.7) | collective-permute-done | bytes 46112 | tf_op jit(solution)/shard_map/ppermute | solution.py:20
  117.0 0.7 add_bitcast_fusion
  (5 shorter events, 0.1 us)
Async XLA Ops:
  0.0 54.7 %copy-start.1 = (s32[128,8]{0,1:T(8,128)S(1)}, s32[128,8]{0,1:T(8,128)}, u32[]{:S(2)}) copy-start(s32[128,8]{0,1:T(8,128)} %param.7) | copy-start | bytes 12292
  0.0 55.5 %copy-start.2 = (s32[128,2]{0,1:T(2,128)S(1)}, s32[128,2]{0,1:T(2,128)}, u32[]{:S(2)}) copy-start(s32[128,2]{0,1:T(2,128)} %param.5) | copy-start | bytes 3076
  0.0 65.0 %copy-start = (bf16[128,64,128]{2,1,0:T(8,128)(2,1)S(1)}, bf16[128,64,128]{2,1,0:T(8,128)(2,1)}, u32[]{:S(2)}) copy-start(bf16[128,64,128]{2,1,0:T(8,128)(2,1)} %tb_ref.1) | copy-start | bytes 6291460
  48.8 16.2 %collective-permute-start.2 = (bf16[32,24,512]{2,1,0:T(8,128)(2,1)}, bf16[32,24,512]{2,1,0:T(8,128)(2,1)}, u32[]{:S(2)}, u32[]{:S(2)}) collective-permute-start(bf16[32,24,512]{2,1,0:T(8,128)(2,1)} %get-tuple-element.7), channel_id=1, source_target_pairs={{0,4},{4,8},{8,12},{12,16},{16,20},{20,24},{24,28},{28,32},{32,36}... | collective-permute-start | bytes 2359304 | tf_op jit(solution)/shard_map/ppermute | solution.py:20
  48.9 16.1 %collective-permute-start.3 = (bf16[32,24,512]{2,1,0:T(8,128)(2,1)}, bf16[32,24,512]{2,1,0:T(8,128)(2,1)}, u32[]{:S(2)}, u32[]{:S(2)}) collective-permute-start(bf16[32,24,512]{2,1,0:T(8,128)(2,1)} %get-tuple-element.8), channel_id=1, source_target_pairs={{0,252},{4,0},{8,4},{12,8},{16,12},{20,16},{24,20},{28,24},{32,28}... | collective-permute-start | bytes 2359304 | tf_op jit(solution)/shard_map/ppermute | solution.py:20
  54.8 9.7 %collective-permute-start.1 = (s32[32,8]{0,1:T(8,128)S(1)}, s32[32,8]{0,1:T(8,128)S(1)}, u32[]{:S(2)}, u32[]{:S(2)}) collective-permute-start(s32[32,8]{0,1:T(8,128)S(1)} %get-tuple-element.16), channel_id=1, source_target_pairs={{0,252},{4,0},{8,4},{12,8},{16,12},{20,16},{24,20},{28,24},{32,28}... | collective-permute-start | bytes 3080 | tf_op jit(solution)/shard_map/ppermute | solution.py:20
  55.5 9.1 %collective-permute-start = (s32[32,8]{0,1:T(8,128)S(1)}, s32[32,8]{0,1:T(8,128)S(1)}, u32[]{:S(2)}, u32[]{:S(2)}) collective-permute-start(s32[32,8]{0,1:T(8,128)S(1)} %get-tuple-element.15), channel_id=1, source_target_pairs={{0,4},{4,8},{8,12},{12,16},{16,20},{20,24},{24,28},{28,32},{32,36}... | collective-permute-start | bytes 3080 | tf_op jit(solution)/shard_map/ppermute | solution.py:20
  93.8 7.4 %collective-permute-start.6 = (f32[3,24,480]{2,1,0:T(8,128)S(1)}, f32[3,24,480]{2,1,0:T(8,128)S(1)}, u32[]{:S(2)}, u32[]{:S(2)}) collective-permute-start(f32[3,24,480]{2,1,0:T(8,128)S(1)} %get-tuple-element.10), channel_id=1, source_target_pairs={{0,3},{1,0},{2,1},{3,2},{4,7},{5,4},{6,5},{7,6},{8,11},{9,8},{10,9... | collective-permute-start | bytes 414728 | tf_op jit(solution)/shard_map/ppermute | solution.py:20
  96.9 6.8 %collective-permute-start.5 = (f32[3,24,480]{2,1,0:T(8,128)S(1)}, f32[3,24,480]{2,1,0:T(8,128)S(1)}, u32[]{:S(2)}, u32[]{:S(2)}) collective-permute-start(f32[3,24,480]{2,1,0:T(8,128)S(1)} %get-tuple-element.11), channel_id=1, source_target_pairs={{0,2},{1,3},{2,0},{3,1},{4,6},{5,7},{6,4},{7,5},{8,10},{9,11},{10,... | collective-permute-start | bytes 414728 | tf_op jit(solution)/shard_map/ppermute | solution.py:20
  97.5 7.6 %collective-permute-start.4 = (f32[3,24,480]{2,1,0:T(8,128)S(1)}, f32[3,24,480]{2,1,0:T(8,128)S(1)}, u32[]{:S(2)}, u32[]{:S(2)}) collective-permute-start(f32[3,24,480]{2,1,0:T(8,128)S(1)} %get-tuple-element.9), channel_id=1, source_target_pairs={{0,1},{1,2},{2,3},{3,0},{4,5},{5,6},{6,7},{7,4},{8,9},{9,10},{10,1... | collective-permute-start | bytes 414728 | tf_op jit(solution)/shard_map/ppermute | solution.py:20
  105.2 6.7 %collective-permute-start.8 = (f32[24,480]{1,0:T(8,128)S(1)}, f32[24,480]{1,0:T(8,128)S(1)}, u32[]{:S(2)}, u32[]{:S(2)}) collective-permute-start(f32[24,480]{1,0:T(8,128)S(1)} %get-tuple-element.13), channel_id=1, source_target_pairs={{0,252},{4,0},{8,4},{12,8},{16,12},{20,16},{24,20},{28,24},{32,28}... | collective-permute-start | bytes 138248 | tf_op jit(solution)/shard_map/ppermute | solution.py:20
  110.1 6.8 %collective-permute-start.7 = (f32[24,480]{1,0:T(8,128)S(1)}, f32[24,480]{1,0:T(8,128)S(1)}, u32[]{:S(2)}, u32[]{:S(2)}) collective-permute-start(f32[24,480]{1,0:T(8,128)S(1)} %get-tuple-element.14), channel_id=1, source_target_pairs={{0,4},{4,8},{8,12},{12,16},{16,20},{20,24},{24,28},{28,32},{32,36}... | collective-permute-start | bytes 138248 | tf_op jit(solution)/shard_map/ppermute | solution.py:20

commit v10 on v6

--- a/solution.py
+++ b/solution.py
@@ -27,10 +27,11 @@
 def slab_kernel(halo_rows, row_count, local_k, wpos_ref, jloc_ref, lower_ref, own_ref, upper_ref,
                 tb_ref, gt_ref, pb_ref, s_ref, xs_ref, w_ref, sems):
     copies = [
-        pltpu.make_async_copy(lower_ref, pb_ref.at[0:halo_rows], sems.at[0]),
+        pltpu.make_async_copy(lower_ref.at[:, 0:CB], pb_ref.at[0:halo_rows], sems.at[0]),
         pltpu.make_async_copy(own_ref, pb_ref.at[halo_rows:halo_rows + row_count], sems.at[1]),
         pltpu.make_async_copy(
-            upper_ref, pb_ref.at[halo_rows + row_count:2 * halo_rows + row_count], sems.at[2]
+            upper_ref.at[:, 0:CB], pb_ref.at[halo_rows + row_count:2 * halo_rows + row_count],
+            sems.at[2],
         ),
     ]
     for copy in copies:
@@ -141,10 +142,17 @@
     coarse_width = NCD * CB
     fine_count = row_count * slab_count
 
-    lower_blocks = shifted(prolong_blocks[row_count - halo_rows:], "blk", 1)
-    upper_blocks = shifted(prolong_blocks[:halo_rows], "blk", -1)
-    lower_columns = shifted(prolong_columns[row_count - halo_rows:], "blk", 1)
-    upper_columns = shifted(prolong_columns[:halo_rows], "blk", -1)
+    def with_columns(rows):
+        blocks = prolong_blocks[rows]
+        columns = prolong_columns[rows].astype(jnp.bfloat16)
+        columns = jnp.pad(columns, ((0, 0), (0, blocks.shape[2] - KP)))[:, None, :]
+        spare = jnp.zeros((blocks.shape[0], 32 - CB - 1, blocks.shape[2]), blocks.dtype)
+        return jnp.concatenate([blocks, columns, spare], axis=1)
+
+    lower_blocks = shifted(with_columns(slice(row_count - halo_rows, row_count)), "blk", 1)
+    upper_blocks = shifted(with_columns(slice(0, halo_rows)), "blk", -1)
+    lower_columns = lower_blocks[:, CB, :KP].astype(jnp.int32)
+    upper_columns = upper_blocks[:, CB, :KP].astype(jnp.int32)
     near_columns = jnp.concatenate([lower_columns, prolong_columns, upper_columns], axis=0)
     wpos = ((near_columns // NCD - slab_index + 2) % slab_count) * NCD + near_columns % NCD
     wpos = wpos.astype(jnp.int32).reshape(-1)

time: 71.3 us -> 77.6 us (1.088)
  waiting for transfers between devices: 22.4 us -> 30.5 us
  starting transfers between devices: 16.1 us -> 11 us
  other arithmetic: 0.89 us -> 2.98 us
  local copies, waits for them, and re-layouts: 3.63 us -> 4.95 us
    ppermute x9 -> x7, waiting for transfers between devices: 22.4 us -> 30.5 us  [shifted(): return lax.ppermute(value, axis, pairs)]
    ppermute x9 -> x7, starting transfers between devices: 16.1 us -> 11 us  [shifted(): return lax.ppermute(value, axis, pairs)]
    unnamed x6 -> x7, local copies, waits for them, and re-layouts: 0.01 us -> 2.39 us
    concatenate x0 -> x1, other arithmetic: none -> 2.04 us  [with_columns(): return jnp.concatenate([blocks, columns, spare], axis=1)]
    slice x2, local copies, waits for them, and re-layouts: 2.87 us -> 1.48 us  [the longest x1 1.48 us: with_columns(): blocks = prolong_blocks[rows]]
  transfers between devices with their start and end apart: 9 -> 7, of which waited for: 7 -> 7; matrix products, arithmetic and copies ran while one was open for 1% -> 0% of each run, Pallas kernels for 0% -> 0%
where the time goes in v10:
time: 77.6 us; the launch traced here: 77.4 us
  waiting for transfers between devices  30.5 us (39%)
  Pallas kernels  27.8 us (36%)
  starting transfers between devices  11 us (14%)
  local copies, waits for them, and re-layouts  4.95 us (6%)
  other arithmetic  2.98 us (4%)
    ppermute x7, waiting for transfers between devices, shifted(): return lax.ppermute(value, axis, pairs)  30.5 us
    pallas_call x1, Pallas kernels, slab_terms_t(): pl.pallas_call(kernel, out_shape=jax.ShapeDtypeStruct((window_width, row_...  27.8 us
    ppermute x7, starting transfers between devices, shifted(): return lax.ppermute(value, axis, pairs)  11 us
    unnamed x7, local copies, waits for them, and re-layouts  2.39 us
    concatenate x1, other arithmetic, with_columns(): return jnp.concatenate([blocks, columns, spare], axis=1)  2.04 us
  transfers between devices with their start and end apart: 7, of which 7 were waited for; matrix products, arithmetic and copies ran while one was open for 0% of the time, Pallas kernels for 0%

profile of v10, /device:TPU:0, one launch (start us, length us, event | category | flops | bytes accessed | tf_op | source)
XLA Modules:
  0.0 77.4 jit_solution(18252093656551093675)
XLA Ops:
  0.0 0.8 %copy.20 = s32[128,8]{1,0:T(8,128)S(1)} copy(s32[128,8]{0,1:T(8,128)} %param.7) | data formatting | bytes 8192 | tf_op args[3]
  0.8 0.1 copy.21
  0.9 1.5 %fusion.10 = (bf16[32,24,512]{2,1,0:T(8,128)(2,1)S(1)}, bf16[32,24,512]{2,1,0:T(8,128)(2,1)S(1)}) fusion(bf16[128,24,512]{2,1,0:T(8,128)(2,1)} %own_ref.1), kind=kLoop, calls=%fused_computation.37 | loop fusion | bytes 3145728 | tf_op jit(solution)/shard_map/slice | solution.py:146
  2.4 0.0 copy-start.2
  2.4 0.1 copy.22
  2.4 0.0 copy-start.1
  2.5 0.1 pad.32.clone
  2.5 2.0 %maximum_maximum_fusion = (bf16[32,32,512]{2,1,0:T(8,128)(2,1)}, bf16[32,32,512]{2,1,0:T(8,128)(2,1)}) fusion(bf16[32,1,512]{2,1,0:T(2,128)(2,1)S(1)} %copy.21, bf16[32,24,512]{2,1,0:T(8,128)(2,1)S(1)} %get-tuple-element.5, bf16[32]{0:T(256)(128)(2,1)S(1)} %pad.32.clone, bf16[32,1,512]{2,1,0:T(2,128)(2,1)S(1)} %copy.22, ...), kind=kLoop, calls=%fused_computation | loop fusion | flops 5767168 | bytes 3735616 | tf_op jit(solution)/shard_map/concatenate | solution.py:150
  4.6 5.8 %collective-permute-start.1 = (bf16[32,32,512]{2,1,0:T(8,128)(2,1)}, bf16[32,32,512]{2,1,0:T(8,128)(2,1)S(1)}, u32[]{:S(2)}, u32[]{:S(2)}) collective-permute-start(bf16[32,32,512]{2,1,0:T(8,128)(2,1)} %get-tuple-element.16), channel_id=1, source_target_pairs={{0,252},{4,0},{8,4},{12,8},{16,12},{20,16},{24,20},{28,24},{32,28}... | collective-permute-start | bytes 3145736 | tf_op jit(solution)/shard_map/ppermute | solution.py:20
  10.3 0.0 collective-permute-start
  10.3 0.0 copy-done.2
  10.4 0.1 copy.26
  10.5 0.1 reshape.12.jloc_ref
  10.6 12.3 %collective-permute-done.1.upper_ref = bf16[32,32,512]{2,1,0:T(8,128)(2,1)S(1)} collective-permute-done((bf16[32,32,512]{2,1,0:T(8,128)(2,1)}, bf16[32,32,512]{2,1,0:T(8,128)(2,1)S(1)}, u32[]{:S(2)}, u32[]{:S(2)}) %collective-permute-start.1) | collective-permute-done | bytes 1048608 | tf_op jit(solution)/shard_map/ppermute | solution.py:20
  23.0 0.1 copy.24
  23.1 5.0 %collective-permute-done.lower_ref = bf16[32,32,512]{2,1,0:T(8,128)(2,1)S(1)} collective-permute-done((bf16[32,32,512]{2,1,0:T(8,128)(2,1)}, bf16[32,32,512]{2,1,0:T(8,128)(2,1)S(1)}, u32[]{:S(2)}, u32[]{:S(2)}) %collective-permute-start) | collective-permute-done | bytes 1048608 | tf_op jit(solution)/shard_map/ppermute | solution.py:20
  28.1 0.1 copy.23
  28.2 0.0 copy-done.1
  28.2 0.1 pad_add_fusion
  28.3 0.1 copy.25
  28.4 0.1 concatenate.14
  28.5 0.0 copy-start
  28.5 1.6 %copy-done = bf16[128,64,128]{2,1,0:T(8,128)(2,1)S(1)} copy-done((bf16[128,64,128]{2,1,0:T(8,128)(2,1)S(1)}, bf16[128,64,128]{2,1,0:T(8,128)(2,1)}, u32[]{:S(2)}) %copy-start) | copy-done | bytes 2097176
  30.1 27.8 %shard_map.46 = f32[480,288]{1,0:T(8,128)S(1)} custom-call(s32[1536]{0:T(1024)S(1)} %fusion.6.wpos_ref, s32[256]{0:T(256)S(1)} %reshape.12.jloc_ref, bf16[32,32,512]{2,1,0:T(8,128)(2,1)S(1)} %collective-permute-done.lower_ref, bf16[128,24,512]{2,1,0:T(8,128)(2,1)} %own_ref.1, bf16[32,32,512]{2,1,0:T(8,128)(2,1)S(1)} %collective-permute-done.1.upper_ref, ...), custom_call_target="tpu_custom_call" | custom-call | flops 8556380160 | bytes 7892992 | tf_op jit(solution)/shard_map/pallas_call | solution.py:107
  58.0 0.2 copy.27
  58.2 3.1 %collective-permute-start.4 = (f32[3,24,480]{2,1,0:T(8,128)S(1)}, f32[3,24,480]{2,1,0:T(8,128)S(1)}, u32[]{:S(2)}, u32[]{:S(2)}) collective-permute-start(f32[3,24,480]{2,1,0:T(8,128)S(1)} %get-tuple-element.8), channel_id=1, source_target_pairs={{0,3},{1,0},{2,1},{3,2},{4,7},{5,4},{6,5},{7,6},{8,11},{9,8},{10,9... | collective-permute-start | bytes 414728 | tf_op jit(solution)/shard_map/ppermute | solution.py:20
  61.3 0.6 collective-permute-start.3
  62.0 1.0 %collective-permute-start.2 = (f32[3,24,480]{2,1,0:T(8,128)S(1)}, f32[3,24,480]{2,1,0:T(8,128)S(1)}, u32[]{:S(2)}, u32[]{:S(2)}) collective-permute-start(f32[3,24,480]{2,1,0:T(8,128)S(1)} %get-tuple-element.7), channel_id=1, source_target_pairs={{0,1},{1,2},{2,3},{3,0},{4,5},{5,6},{6,7},{7,4},{8,9},{9,10},{10,1... | collective-permute-start | bytes 414728 | tf_op jit(solution)/shard_map/ppermute | solution.py:20
  62.9 2.7 %collective-permute-done.4 = f32[3,24,480]{2,1,0:T(8,128)S(1)} collective-permute-done((f32[3,24,480]{2,1,0:T(8,128)S(1)}, f32[3,24,480]{2,1,0:T(8,128)S(1)}, u32[]{:S(2)}, u32[]{:S(2)}) %collective-permute-start.4) | collective-permute-done | bytes 138272 | tf_op jit(solution)/shard_map/ppermute | solution.py:20
  65.6 2.5 %collective-permute-done.3 = f32[3,24,480]{2,1,0:T(8,128)S(1)} collective-permute-done((f32[3,24,480]{2,1,0:T(8,128)S(1)}, f32[3,24,480]{2,1,0:T(8,128)S(1)}, u32[]{:S(2)}, u32[]{:S(2)}) %collective-permute-start.3) | collective-permute-done | bytes 138272 | tf_op jit(solution)/shard_map/ppermute | solution.py:20
  68.1 1.5 %collective-permute-done.2 = f32[3,24,480]{2,1,0:T(8,128)S(1)} collective-permute-done((f32[3,24,480]{2,1,0:T(8,128)S(1)}, f32[3,24,480]{2,1,0:T(8,128)S(1)}, u32[]{:S(2)}, u32[]{:S(2)}) %collective-permute-start.2) | collective-permute-done | bytes 138272 | tf_op jit(solution)/shard_map/ppermute | solution.py:20
  69.6 0.3 collective-permute-start.6
  69.9 0.3 collective-permute-start.5
  70.2 1.4 %collective-permute-done.6 = f32[24,480]{1,0:T(8,128)S(1)} collective-permute-done((f32[24,480]{1,0:T(8,128)S(1)}, f32[24,480]{1,0:T(8,128)S(1)}, u32[]{:S(2)}, u32[]{:S(2)}) %collective-permute-start.6) | collective-permute-done | bytes 46112 | tf_op jit(solution)/shard_map/ppermute | solution.py:20
  71.6 5.1 %collective-permute-done.5 = f32[24,480]{1,0:T(8,128)S(1)} collective-permute-done((f32[24,480]{1,0:T(8,128)S(1)}, f32[24,480]{1,0:T(8,128)S(1)}, u32[]{:S(2)}, u32[]{:S(2)}) %collective-permute-start.5) | collective-permute-done | bytes 46112 | tf_op jit(solution)/shard_map/ppermute | solution.py:20
  76.7 0.7 add_bitcast_fusion
  (11 shorter events, 0.2 us)
Async XLA Ops:
  2.4 8.0 %copy-start.2 = (s32[128,2]{0,1:T(2,128)S(1)}, s32[128,2]{0,1:T(2,128)}, u32[]{:S(2)}) copy-start(s32[128,2]{0,1:T(2,128)} %param.5) | copy-start | bytes 3076
  2.4 25.7 %copy-start.1 = (s32[128,8]{0,1:T(8,128)S(1)}, s32[128,8]{0,1:T(8,128)}, u32[]{:S(2)}) copy-start(s32[128,8]{0,1:T(8,128)} %param.7) | copy-start | bytes 12292
  4.6 18.4 %collective-permute-start.1 = (bf16[32,32,512]{2,1,0:T(8,128)(2,1)}, bf16[32,32,512]{2,1,0:T(8,128)(2,1)S(1)}, u32[]{:S(2)}, u32[]{:S(2)}) collective-permute-start(bf16[32,32,512]{2,1,0:T(8,128)(2,1)} %get-tuple-element.16), channel_id=1, source_target_pairs={{0,252},{4,0},{8,4},{12,8},{16,12},{20,16},{24,20},{28,24},{32,28}... | collective-permute-start | bytes 3145736 | tf_op jit(solution)/shard_map/ppermute | solution.py:20
  10.3 17.8 %collective-permute-start = (bf16[32,32,512]{2,1,0:T(8,128)(2,1)}, bf16[32,32,512]{2,1,0:T(8,128)(2,1)S(1)}, u32[]{:S(2)}, u32[]{:S(2)}) collective-permute-start(bf16[32,32,512]{2,1,0:T(8,128)(2,1)} %get-tuple-element.15), channel_id=1, source_target_pairs={{0,4},{4,8},{8,12},{12,16},{16,20},{20,24},{24,28},{28,32},{32,36}... | collective-permute-start | bytes 3145736 | tf_op jit(solution)/shard_map/ppermute | solution.py:20
  28.5 1.6 %copy-start = (bf16[128,64,128]{2,1,0:T(8,128)(2,1)S(1)}, bf16[128,64,128]{2,1,0:T(8,128)(2,1)}, u32[]{:S(2)}) copy-start(bf16[128,64,128]{2,1,0:T(8,128)(2,1)} %tb_ref.1) | copy-start | bytes 6291460
  58.2 7.4 %collective-permute-start.4 = (f32[3,24,480]{2,1,0:T(8,128)S(1)}, f32[3,24,480]{2,1,0:T(8,128)S(1)}, u32[]{:S(2)}, u32[]{:S(2)}) collective-permute-start(f32[3,24,480]{2,1,0:T(8,128)S(1)} %get-tuple-element.8), channel_id=1, source_target_pairs={{0,3},{1,0},{2,1},{3,2},{4,7},{5,4},{6,5},{7,6},{8,11},{9,8},{10,9... | collective-permute-start | bytes 414728 | tf_op jit(solution)/shard_map/ppermute | solution.py:20
  61.3 6.8 %collective-permute-start.3 = (f32[3,24,480]{2,1,0:T(8,128)S(1)}, f32[3,24,480]{2,1,0:T(8,128)S(1)}, u32[]{:S(2)}, u32[]{:S(2)}) collective-permute-start(f32[3,24,480]{2,1,0:T(8,128)S(1)} %get-tuple-element.9), channel_id=1, source_target_pairs={{0,2},{1,3},{2,0},{3,1},{4,6},{5,7},{6,4},{7,5},{8,10},{9,11},{10,... | collective-permute-start | bytes 414728 | tf_op jit(solution)/shard_map/ppermute | solution.py:20
  62.0 7.6 %collective-permute-start.2 = (f32[3,24,480]{2,1,0:T(8,128)S(1)}, f32[3,24,480]{2,1,0:T(8,128)S(1)}, u32[]{:S(2)}, u32[]{:S(2)}) collective-permute-start(f32[3,24,480]{2,1,0:T(8,128)S(1)} %get-tuple-element.7), channel_id=1, source_target_pairs={{0,1},{1,2},{2,3},{3,0},{4,5},{5,6},{6,7},{7,4},{8,9},{9,10},{10,1... | collective-permute-start | bytes 414728 | tf_op jit(solution)/shard_map/ppermute | solution.py:20
  69.6 2.0 %collective-permute-start.6 = (f32[24,480]{1,0:T(8,128)S(1)}, f32[24,480]{1,0:T(8,128)S(1)}, u32[]{:S(2)}, u32[]{:S(2)}) collective-permute-start(f32[24,480]{1,0:T(8,128)S(1)} %get-tuple-element.11), channel_id=1, source_target_pairs={{0,252},{4,0},{8,4},{12,8},{16,12},{20,16},{24,20},{28,24},{32,28}... | collective-permute-start | bytes 138248 | tf_op jit(solution)/shard_map/ppermute | solution.py:20
  69.9 6.8 %collective-permute-start.5 = (f32[24,480]{1,0:T(8,128)S(1)}, f32[24,480]{1,0:T(8,128)S(1)}, u32[]{:S(2)}, u32[]{:S(2)}) collective-permute-start(f32[24,480]{1,0:T(8,128)S(1)} %get-tuple-element.12), channel_id=1, source_target_pairs={{0,4},{4,8},{8,12},{12,16},{16,20},{20,24},{24,28},{28,32},{32,36}... | collective-permute-start | bytes 138248 | tf_op jit(solution)/shard_map/ppermute | solution.py:20

commit v11 on v6

--- a/solution.py
+++ b/solution.py
@@ -90,7 +90,7 @@
                 parts.append(q.astype(bf16))
             qt = jnp.concatenate(parts, axis=1)
             gt_ref[...] += lax.dot_general(
-                qt, xsb, (((1,), (1,)), ((), ())), preferred_element_type=f32
+                xsb, qt, (((1,), (1,)), ((), ())), preferred_element_type=f32
             )
         return carry
 
@@ -105,7 +105,7 @@
     flops = 2 * row_count * local_k * (window_width * 256 * B + window_width * row_width * B)
     return pl.pallas_call(
         kernel,
-        out_shape=jax.ShapeDtypeStruct((window_width, row_width), jnp.float32),
+        out_shape=jax.ShapeDtypeStruct((row_width, window_width), jnp.float32),
         in_specs=[
             pl.BlockSpec(memory_space=pltpu.SMEM),
             pl.BlockSpec(memory_space=pltpu.SMEM),
@@ -153,7 +153,7 @@
 
     gt = slab_terms_t(wpos, jloc, lower_blocks, prolong_blocks, upper_blocks, tangent_blocks,
                       halo_rows, row_count)
-    terms = gt.T.reshape(3, NCD, CB, 5 * coarse_width)
+    terms = gt.reshape(3, NCD, CB, 5 * coarse_width)
 
     shares = lax.dynamic_index_in_dim(terms, lane_index, axis=1, keepdims=False)
     for step in range(1, lane_count):

time: 71.3 us -> 70.3 us (0.986)
  no operation moved by 1% of the time
where the time goes in v11:
time: 70.3 us; the launch traced here: 70.2 us
  Pallas kernels  27.4 us (39%)
  waiting for transfers between devices  22.3 us (32%)
  starting transfers between devices  16.1 us (23%)
  local copies, waits for them, and re-layouts  3.39 us (5%)
  other arithmetic  0.89 us (1%)
    pallas_call x1, Pallas kernels, slab_terms_t(): pl.pallas_call(kernel, out_shape=jax.ShapeDtypeStruct((row_width, window_...  27.4 us
    ppermute x9, waiting for transfers between devices, shifted(): return lax.ppermute(value, axis, pairs)  22.3 us
    ppermute x9, starting transfers between devices, shifted(): return lax.ppermute(value, axis, pairs)  16.1 us
    slice x1, local copies, waits for them, and re-layouts, on_device(): upper_blocks = shifted(prolong_blocks[:halo_rows], 'blk', -1)  2.79 us
  transfers between devices with their start and end apart: 9, of which 7 were waited for; matrix products, arithmetic and copies ran while one was open for 1% of the time, Pallas kernels for 0%

profile of v11, /device:TPU:0, one launch (start us, length us, event | category | flops | bytes accessed | tf_op | source)
XLA Modules:
  0.0 70.2 jit_solution(10064338745255944946)
XLA Ops:
  0.0 0.0 copy-start.1
  0.0 0.0 copy-start.2
  0.0 0.0 copy-start
  0.0 2.8 %fusion.10 = (bf16[32,24,512]{2,1,0:T(8,128)(2,1)}, bf16[32,24,512]{2,1,0:T(8,128)(2,1)}) fusion(bf16[128,24,512]{2,1,0:T(8,128)(2,1)} %own_ref.1), kind=kLoop, calls=%fused_computation.31 | loop fusion | bytes 3145728 | tf_op jit(solution)/shard_map/slice | solution.py:145
  2.8 0.0 collective-permute-start.2
  2.8 5.8 %collective-permute-start.3 = (bf16[32,24,512]{2,1,0:T(8,128)(2,1)}, bf16[32,24,512]{2,1,0:T(8,128)(2,1)}, u32[]{:S(2)}, u32[]{:S(2)}) collective-permute-start(bf16[32,24,512]{2,1,0:T(8,128)(2,1)} %get-tuple-element.5), channel_id=1, source_target_pairs={{0,252},{4,0},{8,4},{12,8},{16,12},{20,16},{24,20},{28,24},{32,28}... | collective-permute-start | bytes 2359304 | tf_op jit(solution)/shard_map/ppermute | solution.py:20
  8.6 0.0 copy-done.1
  8.6 0.1 fusion.11
  8.6 0.7 collective-permute-start.1
  9.3 0.0 collective-permute-start
  9.3 0.0 copy-done.2
  9.4 0.1 copy.6
  9.5 0.1 reshape.8.jloc_ref
  9.6 8.8 %collective-permute-done.1 = s32[32,8]{0,1:T(8,128)S(1)} collective-permute-done((s32[32,8]{0,1:T(8,128)S(1)}, s32[32,8]{0,1:T(8,128)S(1)}, u32[]{:S(2)}, u32[]{:S(2)}) %collective-permute-start.1) | collective-permute-done | bytes 1056 | tf_op jit(solution)/shard_map/ppermute | solution.py:20
  18.4 0.1 collective-permute-done
  18.5 0.1 pad_add_fusion
  18.6 0.1 copy.5
  18.7 0.1 concatenate.6
  18.8 0.0 collective-permute-done.2.lower_ref
  18.8 0.0 collective-permute-done.3.upper_ref
  18.8 0.0 copy-done
  18.9 27.4 %shard_map.46 = f32[288,480]{1,0:T(8,128)S(1)} custom-call(s32[1536]{0:T(1024)S(1)} %fusion.6.wpos_ref, s32[256]{0:T(256)S(1)} %reshape.8.jloc_ref, bf16[32,24,512]{2,1,0:T(8,128)(2,1)S(1)} %collective-permute-done.2.lower_ref, bf16[128,24,512]{2,1,0:T(8,128)(2,1)} %own_ref.1, bf16[32,24,512]{2,1,0:T(8,128)(2,1)} %collective-permute-done.3.upper_ref, ...), custom_call_target="tpu_custom_call" | custom-call | flops 8556380160 | bytes 7368704 | tf_op jit(solution)/shard_map/pallas_call | solution.py:106
  46.3 3.1 %collective-permute-start.6 = (f32[3,24,480]{2,1,0:T(8,128)S(1)}, f32[3,24,480]{2,1,0:T(8,128)S(1)}, u32[]{:S(2)}, u32[]{:S(2)}) collective-permute-start(f32[3,24,480]{2,1,0:T(8,128)S(1)} %get-tuple-element.8), channel_id=1, source_target_pairs={{0,3},{1,0},{2,1},{3,2},{4,7},{5,4},{6,5},{7,6},{8,11},{9,8},{10,9... | collective-permute-start | bytes 414728 | tf_op jit(solution)/shard_map/ppermute | solution.py:20
  49.4 0.6 collective-permute-start.5
  50.0 1.0 %collective-permute-start.4 = (f32[3,24,480]{2,1,0:T(8,128)S(1)}, f32[3,24,480]{2,1,0:T(8,128)S(1)}, u32[]{:S(2)}, u32[]{:S(2)}) collective-permute-start(f32[3,24,480]{2,1,0:T(8,128)S(1)} %get-tuple-element.7), channel_id=1, source_target_pairs={{0,1},{1,2},{2,3},{3,0},{4,5},{5,6},{6,7},{7,4},{8,9},{9,10},{10,1... | collective-permute-start | bytes 414728 | tf_op jit(solution)/shard_map/ppermute | solution.py:20
  51.0 2.7 %collective-permute-done.6 = f32[3,24,480]{2,1,0:T(8,128)S(1)} collective-permute-done((f32[3,24,480]{2,1,0:T(8,128)S(1)}, f32[3,24,480]{2,1,0:T(8,128)S(1)}, u32[]{:S(2)}, u32[]{:S(2)}) %collective-permute-start.6) | collective-permute-done | bytes 138272 | tf_op jit(solution)/shard_map/ppermute | solution.py:20
  53.7 2.5 %collective-permute-done.5 = f32[3,24,480]{2,1,0:T(8,128)S(1)} collective-permute-done((f32[3,24,480]{2,1,0:T(8,128)S(1)}, f32[3,24,480]{2,1,0:T(8,128)S(1)}, u32[]{:S(2)}, u32[]{:S(2)}) %collective-permute-start.5) | collective-permute-done | bytes 138272 | tf_op jit(solution)/shard_map/ppermute | solution.py:20
  56.2 1.5 %collective-permute-done.4 = f32[3,24,480]{2,1,0:T(8,128)S(1)} collective-permute-done((f32[3,24,480]{2,1,0:T(8,128)S(1)}, f32[3,24,480]{2,1,0:T(8,128)S(1)}, u32[]{:S(2)}, u32[]{:S(2)}) %collective-permute-start.4) | collective-permute-done | bytes 138272 | tf_op jit(solution)/shard_map/ppermute | solution.py:20
  57.7 5.0 %collective-permute-start.8 = (f32[24,480]{1,0:T(8,128)S(1)}, f32[24,480]{1,0:T(8,128)S(1)}, u32[]{:S(2)}, u32[]{:S(2)}) collective-permute-start(f32[24,480]{1,0:T(8,128)S(1)} %get-tuple-element.11), channel_id=1, source_target_pairs={{0,252},{4,0},{8,4},{12,8},{16,12},{20,16},{24,20},{28,24},{32,28}... | collective-permute-start | bytes 138248 | tf_op jit(solution)/shard_map/ppermute | solution.py:20
  62.7 0.0 collective-permute-start.7
  62.7 1.7 %collective-permute-done.8 = f32[24,480]{1,0:T(8,128)S(1)} collective-permute-done((f32[24,480]{1,0:T(8,128)S(1)}, f32[24,480]{1,0:T(8,128)S(1)}, u32[]{:S(2)}, u32[]{:S(2)}) %collective-permute-start.8) | collective-permute-done | bytes 46112 | tf_op jit(solution)/shard_map/ppermute | solution.py:20
  64.4 5.1 %collective-permute-done.7 = f32[24,480]{1,0:T(8,128)S(1)} collective-permute-done((f32[24,480]{1,0:T(8,128)S(1)}, f32[24,480]{1,0:T(8,128)S(1)}, u32[]{:S(2)}, u32[]{:S(2)}) %collective-permute-start.7) | collective-permute-done | bytes 46112 | tf_op jit(solution)/shard_map/ppermute | solution.py:20
  69.5 0.7 %add_bitcast_fusion = f32[1,24,672]{2,1,0:T(8,128)} fusion(f32[24,480]{1,0:T(8,128)S(1)} %collective-permute-done.8, f32[24,480]{1,0:T(8,128)S(1)} %collective-permute-done.7, f32[24,480]{1,0:T(8,128)S(1)} %get-tuple-element.10), kind=kLoop, calls=%fused_computation.6 | loop fusion | flops 32256 | bytes 202752 | tf_op jit(solution)/shard_map/broadcast_in_dim | solution.py:171
  (5 shorter events, 0.1 us)
Async XLA Ops:
  0.0 8.6 %copy-start.1 = (s32[128,8]{0,1:T(8,128)S(1)}, s32[128,8]{0,1:T(8,128)}, u32[]{:S(2)}) copy-start(s32[128,8]{0,1:T(8,128)} %param.7) | copy-start | bytes 12292
  0.0 9.3 %copy-start.2 = (s32[128,2]{0,1:T(2,128)S(1)}, s32[128,2]{0,1:T(2,128)}, u32[]{:S(2)}) copy-start(s32[128,2]{0,1:T(2,128)} %param.5) | copy-start | bytes 3076
  0.0 18.8 %copy-start = (bf16[128,64,128]{2,1,0:T(8,128)(2,1)S(1)}, bf16[128,64,128]{2,1,0:T(8,128)(2,1)}, u32[]{:S(2)}) copy-start(bf16[128,64,128]{2,1,0:T(8,128)(2,1)} %tb_ref.1) | copy-start | bytes 6291460
  2.8 16.0 %collective-permute-start.2 = (bf16[32,24,512]{2,1,0:T(8,128)(2,1)}, bf16[32,24,512]{2,1,0:T(8,128)(2,1)S(1)}, u32[]{:S(2)}, u32[]{:S(2)}) collective-permute-start(bf16[32,24,512]{2,1,0:T(8,128)(2,1)} %get-tuple-element.6), channel_id=1, source_target_pairs={{0,4},{4,8},{8,12},{12,16},{16,20},{20,24},{24,28},{28,32},{32,36}... | collective-permute-start | bytes 2359304 | tf_op jit(solution)/shard_map/ppermute | solution.py:20
  2.8 16.0 %collective-permute-start.3 = (bf16[32,24,512]{2,1,0:T(8,128)(2,1)}, bf16[32,24,512]{2,1,0:T(8,128)(2,1)}, u32[]{:S(2)}, u32[]{:S(2)}) collective-permute-start(bf16[32,24,512]{2,1,0:T(8,128)(2,1)} %get-tuple-element.5), channel_id=1, source_target_pairs={{0,252},{4,0},{8,4},{12,8},{16,12},{20,16},{24,20},{28,24},{32,28}... | collective-permute-start | bytes 2359304 | tf_op jit(solution)/shard_map/ppermute | solution.py:20
  8.6 9.7 %collective-permute-start.1 = (s32[32,8]{0,1:T(8,128)S(1)}, s32[32,8]{0,1:T(8,128)S(1)}, u32[]{:S(2)}, u32[]{:S(2)}) collective-permute-start(s32[32,8]{0,1:T(8,128)S(1)} %get-tuple-element.14), channel_id=1, source_target_pairs={{0,252},{4,0},{8,4},{12,8},{16,12},{20,16},{24,20},{28,24},{32,28}... | collective-permute-start | bytes 3080 | tf_op jit(solution)/shard_map/ppermute | solution.py:20
  9.3 9.2 %collective-permute-start = (s32[32,8]{0,1:T(8,128)S(1)}, s32[32,8]{0,1:T(8,128)S(1)}, u32[]{:S(2)}, u32[]{:S(2)}) collective-permute-start(s32[32,8]{0,1:T(8,128)S(1)} %get-tuple-element.13), channel_id=1, source_target_pairs={{0,4},{4,8},{8,12},{12,16},{16,20},{20,24},{24,28},{28,32},{32,36}... | collective-permute-start | bytes 3080 | tf_op jit(solution)/shard_map/ppermute | solution.py:20
  46.3 7.4 %collective-permute-start.6 = (f32[3,24,480]{2,1,0:T(8,128)S(1)}, f32[3,24,480]{2,1,0:T(8,128)S(1)}, u32[]{:S(2)}, u32[]{:S(2)}) collective-permute-start(f32[3,24,480]{2,1,0:T(8,128)S(1)} %get-tuple-element.8), channel_id=1, source_target_pairs={{0,3},{1,0},{2,1},{3,2},{4,7},{5,4},{6,5},{7,6},{8,11},{9,8},{10,9... | collective-permute-start | bytes 414728 | tf_op jit(solution)/shard_map/ppermute | solution.py:20
  49.4 6.8 %collective-permute-start.5 = (f32[3,24,480]{2,1,0:T(8,128)S(1)}, f32[3,24,480]{2,1,0:T(8,128)S(1)}, u32[]{:S(2)}, u32[]{:S(2)}) collective-permute-start(f32[3,24,480]{2,1,0:T(8,128)S(1)} %get-tuple-element.9), channel_id=1, source_target_pairs={{0,2},{1,3},{2,0},{3,1},{4,6},{5,7},{6,4},{7,5},{8,10},{9,11},{10,... | collective-permute-start | bytes 414728 | tf_op jit(solution)/shard_map/ppermute | solution.py:20
  50.0 7.6 %collective-permute-start.4 = (f32[3,24,480]{2,1,0:T(8,128)S(1)}, f32[3,24,480]{2,1,0:T(8,128)S(1)}, u32[]{:S(2)}, u32[]{:S(2)}) collective-permute-start(f32[3,24,480]{2,1,0:T(8,128)S(1)} %get-tuple-element.7), channel_id=1, source_target_pairs={{0,1},{1,2},{2,3},{3,0},{4,5},{5,6},{6,7},{7,4},{8,9},{9,10},{10,1... | collective-permute-start | bytes 414728 | tf_op jit(solution)/shard_map/ppermute | solution.py:20
  57.7 6.7 %collective-permute-start.8 = (f32[24,480]{1,0:T(8,128)S(1)}, f32[24,480]{1,0:T(8,128)S(1)}, u32[]{:S(2)}, u32[]{:S(2)}) collective-permute-start(f32[24,480]{1,0:T(8,128)S(1)} %get-tuple-element.11), channel_id=1, source_target_pairs={{0,252},{4,0},{8,4},{12,8},{16,12},{20,16},{24,20},{28,24},{32,28}... | collective-permute-start | bytes 138248 | tf_op jit(solution)/shard_map/ppermute | solution.py:20
  62.7 6.8 %collective-permute-start.7 = (f32[24,480]{1,0:T(8,128)S(1)}, f32[24,480]{1,0:T(8,128)S(1)}, u32[]{:S(2)}, u32[]{:S(2)}) collective-permute-start(f32[24,480]{1,0:T(8,128)S(1)} %get-tuple-element.12), channel_id=1, source_target_pairs={{0,4},{4,8},{8,12},{12,16},{16,20},{20,24},{24,28},{28,32},{32,36}... | collective-permute-start | bytes 138248 | tf_op jit(solution)/shard_map/ppermute | solution.py:20

commit v12 on v11

--- a/solution.py
+++ b/solution.py
@@ -11,7 +11,7 @@
 CB = 24
 KP = 8
 NCD = 4
-GROUP = 8
+GROUP = 16
 
 
 def shifted(value, axis, steps):

time: 70.3 us -> 66.6 us (0.947)
  Pallas kernels: 27.4 us -> 23.7 us
    pallas_call x1, Pallas kernels: 27.4 us -> 23.7 us  [slab_terms_t(): pl.pallas_call(kernel, out_shape=jax.ShapeDtypeStruct((row_width, window_...]
where the time goes in v12:
time: 66.6 us; the launch traced here: 66.5 us
  Pallas kernels  23.7 us (36%)
  waiting for transfers between devices  22.3 us (33%)
  starting transfers between devices  16.1 us (24%)
  local copies, waits for them, and re-layouts  3.39 us (5%)
  other arithmetic  0.89 us (1%)
    pallas_call x1, Pallas kernels, slab_terms_t(): pl.pallas_call(kernel, out_shape=jax.ShapeDtypeStruct((row_width, window_...  23.7 us
    ppermute x9, waiting for transfers between devices, shifted(): return lax.ppermute(value, axis, pairs)  22.3 us
    ppermute x9, starting transfers between devices, shifted(): return lax.ppermute(value, axis, pairs)  16.1 us
    slice x1, local copies, waits for them, and re-layouts, on_device(): upper_blocks = shifted(prolong_blocks[:halo_rows], 'blk', -1)  2.79 us
  transfers between devices with their start and end apart: 9, of which 7 were waited for; matrix products, arithmetic and copies ran while one was open for 1% of the time, Pallas kernels for 0%

profile of v12, /device:TPU:0, one launch (start us, length us, event | category | flops | bytes accessed | tf_op | source)
XLA Modules:
  0.0 66.5 jit_solution(5450878850811499884)
XLA Ops:
  0.0 0.0 copy-start.1
  0.0 0.0 copy-start.2
  0.0 0.0 copy-start
  0.0 2.8 %fusion.10 = (bf16[32,24,512]{2,1,0:T(8,128)(2,1)}, bf16[32,24,512]{2,1,0:T(8,128)(2,1)}) fusion(bf16[128,24,512]{2,1,0:T(8,128)(2,1)} %own_ref.1), kind=kLoop, calls=%fused_computation.31 | loop fusion | bytes 3145728 | tf_op jit(solution)/shard_map/slice | solution.py:145
  2.8 0.0 collective-permute-start.2
  2.8 5.8 %collective-permute-start.3 = (bf16[32,24,512]{2,1,0:T(8,128)(2,1)}, bf16[32,24,512]{2,1,0:T(8,128)(2,1)}, u32[]{:S(2)}, u32[]{:S(2)}) collective-permute-start(bf16[32,24,512]{2,1,0:T(8,128)(2,1)} %get-tuple-element.5), channel_id=1, source_target_pairs={{0,252},{4,0},{8,4},{12,8},{16,12},{20,16},{24,20},{28,24},{32,28}... | collective-permute-start | bytes 2359304 | tf_op jit(solution)/shard_map/ppermute | solution.py:20
  8.6 0.0 copy-done.1
  8.6 0.1 fusion.11
  8.6 0.7 %collective-permute-start.1 = (s32[32,8]{0,1:T(8,128)S(1)}, s32[32,8]{0,1:T(8,128)S(1)}, u32[]{:S(2)}, u32[]{:S(2)}) collective-permute-start(s32[32,8]{0,1:T(8,128)S(1)} %get-tuple-element.14), channel_id=1, source_target_pairs={{0,252},{4,0},{8,4},{12,8},{16,12},{20,16},{24,20},{28,24},{32,28}... | collective-permute-start | bytes 3080 | tf_op jit(solution)/shard_map/ppermute | solution.py:20
  9.3 0.0 collective-permute-start
  9.3 0.0 copy-done.2
  9.4 0.1 copy.6
  9.5 0.1 reshape.8.jloc_ref
  9.6 8.8 %collective-permute-done.1 = s32[32,8]{0,1:T(8,128)S(1)} collective-permute-done((s32[32,8]{0,1:T(8,128)S(1)}, s32[32,8]{0,1:T(8,128)S(1)}, u32[]{:S(2)}, u32[]{:S(2)}) %collective-permute-start.1) | collective-permute-done | bytes 1056 | tf_op jit(solution)/shard_map/ppermute | solution.py:20
  18.4 0.1 collective-permute-done
  18.5 0.1 pad_add_fusion
  18.6 0.1 copy.5
  18.7 0.1 concatenate.6
  18.8 0.0 collective-permute-done.2.lower_ref
  18.8 0.0 collective-permute-done.3.upper_ref
  18.8 0.0 copy-done
  18.9 23.7 %shard_map.46 = f32[288,480]{1,0:T(8,128)S(1)} custom-call(s32[1536]{0:T(1024)S(1)} %fusion.6.wpos_ref, s32[256]{0:T(256)S(1)} %reshape.8.jloc_ref, bf16[32,24,512]{2,1,0:T(8,128)(2,1)S(1)} %collective-permute-done.2.lower_ref, bf16[128,24,512]{2,1,0:T(8,128)(2,1)} %own_ref.1, bf16[32,24,512]{2,1,0:T(8,128)(2,1)} %collective-permute-done.3.upper_ref, ...), custom_call_target="tpu_custom_call" | custom-call | flops 8556380160 | bytes 7368704 | tf_op jit(solution)/shard_map/pallas_call | solution.py:106
  42.6 3.1 %collective-permute-start.6 = (f32[3,24,480]{2,1,0:T(8,128)S(1)}, f32[3,24,480]{2,1,0:T(8,128)S(1)}, u32[]{:S(2)}, u32[]{:S(2)}) collective-permute-start(f32[3,24,480]{2,1,0:T(8,128)S(1)} %get-tuple-element.8), channel_id=1, source_target_pairs={{0,3},{1,0},{2,1},{3,2},{4,7},{5,4},{6,5},{7,6},{8,11},{9,8},{10,9... | collective-permute-start | bytes 414728 | tf_op jit(solution)/shard_map/ppermute | solution.py:20
  45.7 0.6 collective-permute-start.5
  46.3 1.0 %collective-permute-start.4 = (f32[3,24,480]{2,1,0:T(8,128)S(1)}, f32[3,24,480]{2,1,0:T(8,128)S(1)}, u32[]{:S(2)}, u32[]{:S(2)}) collective-permute-start(f32[3,24,480]{2,1,0:T(8,128)S(1)} %get-tuple-element.7), channel_id=1, source_target_pairs={{0,1},{1,2},{2,3},{3,0},{4,5},{5,6},{6,7},{7,4},{8,9},{9,10},{10,1... | collective-permute-start | bytes 414728 | tf_op jit(solution)/shard_map/ppermute | solution.py:20
  47.3 2.7 %collective-permute-done.6 = f32[3,24,480]{2,1,0:T(8,128)S(1)} collective-permute-done((f32[3,24,480]{2,1,0:T(8,128)S(1)}, f32[3,24,480]{2,1,0:T(8,128)S(1)}, u32[]{:S(2)}, u32[]{:S(2)}) %collective-permute-start.6) | collective-permute-done | bytes 138272 | tf_op jit(solution)/shard_map/ppermute | solution.py:20
  50.0 2.5 %collective-permute-done.5 = f32[3,24,480]{2,1,0:T(8,128)S(1)} collective-permute-done((f32[3,24,480]{2,1,0:T(8,128)S(1)}, f32[3,24,480]{2,1,0:T(8,128)S(1)}, u32[]{:S(2)}, u32[]{:S(2)}) %collective-permute-start.5) | collective-permute-done | bytes 138272 | tf_op jit(solution)/shard_map/ppermute | solution.py:20
  52.4 1.5 %collective-permute-done.4 = f32[3,24,480]{2,1,0:T(8,128)S(1)} collective-permute-done((f32[3,24,480]{2,1,0:T(8,128)S(1)}, f32[3,24,480]{2,1,0:T(8,128)S(1)}, u32[]{:S(2)}, u32[]{:S(2)}) %collective-permute-start.4) | collective-permute-done | bytes 138272 | tf_op jit(solution)/shard_map/ppermute | solution.py:20
  54.0 5.0 %collective-permute-start.8 = (f32[24,480]{1,0:T(8,128)S(1)}, f32[24,480]{1,0:T(8,128)S(1)}, u32[]{:S(2)}, u32[]{:S(2)}) collective-permute-start(f32[24,480]{1,0:T(8,128)S(1)} %get-tuple-element.11), channel_id=1, source_target_pairs={{0,252},{4,0},{8,4},{12,8},{16,12},{20,16},{24,20},{28,24},{32,28}... | collective-permute-start | bytes 138248 | tf_op jit(solution)/shard_map/ppermute | solution.py:20
  59.0 0.0 collective-permute-start.7
  59.0 1.7 %collective-permute-done.8 = f32[24,480]{1,0:T(8,128)S(1)} collective-permute-done((f32[24,480]{1,0:T(8,128)S(1)}, f32[24,480]{1,0:T(8,128)S(1)}, u32[]{:S(2)}, u32[]{:S(2)}) %collective-permute-start.8) | collective-permute-done | bytes 46112 | tf_op jit(solution)/shard_map/ppermute | solution.py:20
  60.7 5.1 %collective-permute-done.7 = f32[24,480]{1,0:T(8,128)S(1)} collective-permute-done((f32[24,480]{1,0:T(8,128)S(1)}, f32[24,480]{1,0:T(8,128)S(1)}, u32[]{:S(2)}, u32[]{:S(2)}) %collective-permute-start.7) | collective-permute-done | bytes 46112 | tf_op jit(solution)/shard_map/ppermute | solution.py:20
  65.8 0.7 %add_bitcast_fusion = f32[1,24,672]{2,1,0:T(8,128)} fusion(f32[24,480]{1,0:T(8,128)S(1)} %collective-permute-done.8, f32[24,480]{1,0:T(8,128)S(1)} %collective-permute-done.7, f32[24,480]{1,0:T(8,128)S(1)} %get-tuple-element.10), kind=kLoop, calls=%fused_computation.6 | loop fusion | flops 32256 | bytes 202752 | tf_op jit(solution)/shard_map/broadcast_in_dim | solution.py:171
  (5 shorter events, 0.1 us)
Async XLA Ops:
  0.0 8.6 %copy-start.1 = (s32[128,8]{0,1:T(8,128)S(1)}, s32[128,8]{0,1:T(8,128)}, u32[]{:S(2)}) copy-start(s32[128,8]{0,1:T(8,128)} %param.7) | copy-start | bytes 12292
  0.0 9.3 %copy-start.2 = (s32[128,2]{0,1:T(2,128)S(1)}, s32[128,2]{0,1:T(2,128)}, u32[]{:S(2)}) copy-start(s32[128,2]{0,1:T(2,128)} %param.5) | copy-start | bytes 3076
  0.0 18.8 %copy-start = (bf16[128,64,128]{2,1,0:T(8,128)(2,1)S(1)}, bf16[128,64,128]{2,1,0:T(8,128)(2,1)}, u32[]{:S(2)}) copy-start(bf16[128,64,128]{2,1,0:T(8,128)(2,1)} %tb_ref.1) | copy-start | bytes 6291460
  2.8 16.0 %collective-permute-start.2 = (bf16[32,24,512]{2,1,0:T(8,128)(2,1)}, bf16[32,24,512]{2,1,0:T(8,128)(2,1)S(1)}, u32[]{:S(2)}, u32[]{:S(2)}) collective-permute-start(bf16[32,24,512]{2,1,0:T(8,128)(2,1)} %get-tuple-element.6), channel_id=1, source_target_pairs={{0,4},{4,8},{8,12},{12,16},{16,20},{20,24},{24,28},{28,32},{32,36}... | collective-permute-start | bytes 2359304 | tf_op jit(solution)/shard_map/ppermute | solution.py:20
  2.8 16.0 %collective-permute-start.3 = (bf16[32,24,512]{2,1,0:T(8,128)(2,1)}, bf16[32,24,512]{2,1,0:T(8,128)(2,1)}, u32[]{:S(2)}, u32[]{:S(2)}) collective-permute-start(bf16[32,24,512]{2,1,0:T(8,128)(2,1)} %get-tuple-element.5), channel_id=1, source_target_pairs={{0,252},{4,0},{8,4},{12,8},{16,12},{20,16},{24,20},{28,24},{32,28}... | collective-permute-start | bytes 2359304 | tf_op jit(solution)/shard_map/ppermute | solution.py:20
  8.6 9.7 %collective-permute-start.1 = (s32[32,8]{0,1:T(8,128)S(1)}, s32[32,8]{0,1:T(8,128)S(1)}, u32[]{:S(2)}, u32[]{:S(2)}) collective-permute-start(s32[32,8]{0,1:T(8,128)S(1)} %get-tuple-element.14), channel_id=1, source_target_pairs={{0,252},{4,0},{8,4},{12,8},{16,12},{20,16},{24,20},{28,24},{32,28}... | collective-permute-start | bytes 3080 | tf_op jit(solution)/shard_map/ppermute | solution.py:20
  9.3 9.2 %collective-permute-start = (s32[32,8]{0,1:T(8,128)S(1)}, s32[32,8]{0,1:T(8,128)S(1)}, u32[]{:S(2)}, u32[]{:S(2)}) collective-permute-start(s32[32,8]{0,1:T(8,128)S(1)} %get-tuple-element.13), channel_id=1, source_target_pairs={{0,4},{4,8},{8,12},{12,16},{16,20},{20,24},{24,28},{28,32},{32,36}... | collective-permute-start | bytes 3080 | tf_op jit(solution)/shard_map/ppermute | solution.py:20
  42.6 7.3 %collective-permute-start.6 = (f32[3,24,480]{2,1,0:T(8,128)S(1)}, f32[3,24,480]{2,1,0:T(8,128)S(1)}, u32[]{:S(2)}, u32[]{:S(2)}) collective-permute-start(f32[3,24,480]{2,1,0:T(8,128)S(1)} %get-tuple-element.8), channel_id=1, source_target_pairs={{0,3},{1,0},{2,1},{3,2},{4,7},{5,4},{6,5},{7,6},{8,11},{9,8},{10,9... | collective-permute-start | bytes 414728 | tf_op jit(solution)/shard_map/ppermute | solution.py:20
  45.7 6.8 %collective-permute-start.5 = (f32[3,24,480]{2,1,0:T(8,128)S(1)}, f32[3,24,480]{2,1,0:T(8,128)S(1)}, u32[]{:S(2)}, u32[]{:S(2)}) collective-permute-start(f32[3,24,480]{2,1,0:T(8,128)S(1)} %get-tuple-element.9), channel_id=1, source_target_pairs={{0,2},{1,3},{2,0},{3,1},{4,6},{5,7},{6,4},{7,5},{8,10},{9,11},{10,... | collective-permute-start | bytes 414728 | tf_op jit(solution)/shard_map/ppermute | solution.py:20
  46.3 7.6 %collective-permute-start.4 = (f32[3,24,480]{2,1,0:T(8,128)S(1)}, f32[3,24,480]{2,1,0:T(8,128)S(1)}, u32[]{:S(2)}, u32[]{:S(2)}) collective-permute-start(f32[3,24,480]{2,1,0:T(8,128)S(1)} %get-tuple-element.7), channel_id=1, source_target_pairs={{0,1},{1,2},{2,3},{3,0},{4,5},{5,6},{6,7},{7,4},{8,9},{9,10},{10,1... | collective-permute-start | bytes 414728 | tf_op jit(solution)/shard_map/ppermute | solution.py:20
  54.0 6.7 %collective-permute-start.8 = (f32[24,480]{1,0:T(8,128)S(1)}, f32[24,480]{1,0:T(8,128)S(1)}, u32[]{:S(2)}, u32[]{:S(2)}) collective-permute-start(f32[24,480]{1,0:T(8,128)S(1)} %get-tuple-element.11), channel_id=1, source_target_pairs={{0,252},{4,0},{8,4},{12,8},{16,12},{20,16},{24,20},{28,24},{32,28}... | collective-permute-start | bytes 138248 | tf_op jit(solution)/shard_map/ppermute | solution.py:20
  59.0 6.8 %collective-permute-start.7 = (f32[24,480]{1,0:T(8,128)S(1)}, f32[24,480]{1,0:T(8,128)S(1)}, u32[]{:S(2)}, u32[]{:S(2)}) collective-permute-start(f32[24,480]{1,0:T(8,128)S(1)} %get-tuple-element.12), channel_id=1, source_target_pairs={{0,4},{4,8},{8,12},{12,16},{16,20},{20,24},{24,28},{28,32},{32,36}... | collective-permute-start | bytes 138248 | tf_op jit(solution)/shard_map/ppermute | solution.py:20

commit v13 on v12

--- a/solution.py
+++ b/solution.py
@@ -156,7 +156,7 @@
     terms = gt.reshape(3, NCD, CB, 5 * coarse_width)
 
     shares = lax.dynamic_index_in_dim(terms, lane_index, axis=1, keepdims=False)
-    for step in range(1, lane_count):
+    for step in sorted(range(1, lane_count), key=lambda s: min(s, lane_count - s)):
         piece = lax.dynamic_index_in_dim(
             terms, (lane_index + step) % lane_count, axis=1, keepdims=False
         )

time: 66.6 us -> 65.9 us (0.989); the launches traced: 66.5 us -> 65 us
  waiting for transfers between devices: 22.3 us -> 21.1 us
    ppermute x9, waiting for transfers between devices: 22.3 us -> 21.1 us  [shifted(): return lax.ppermute(value, axis, pairs)]
where the time goes in v13:
time: 65.9 us; the launch traced here: 65 us
  Pallas kernels  23.7 us (36%)
  waiting for transfers between devices  21.1 us (32%)
  starting transfers between devices  15.8 us (24%)
  local copies, waits for them, and re-layouts  3.39 us (5%)
  other arithmetic  0.89 us (1%)
    pallas_call x1, Pallas kernels, slab_terms_t(): pl.pallas_call(kernel, out_shape=jax.ShapeDtypeStruct((row_width, window_...  23.7 us
    ppermute x9, waiting for transfers between devices, shifted(): return lax.ppermute(value, axis, pairs)  21.1 us
    ppermute x9, starting transfers between devices, shifted(): return lax.ppermute(value, axis, pairs)  15.8 us
    slice x1, local copies, waits for them, and re-layouts, on_device(): upper_blocks = shifted(prolong_blocks[:halo_rows], 'blk', -1)  2.79 us
  transfers between devices with their start and end apart: 9, of which 7 were waited for; matrix products, arithmetic and copies ran while one was open for 1% of the time, Pallas kernels for 0%

profile of v13, /device:TPU:0, one launch (start us, length us, event | category | flops | bytes accessed | tf_op | source)
XLA Modules:
  0.0 65.0 jit_solution(10878365253291261620)
XLA Ops:
  0.0 0.0 copy-start.1
  0.0 0.0 copy-start.2
  0.0 0.0 copy-start
  0.0 2.8 %fusion.10 = (bf16[32,24,512]{2,1,0:T(8,128)(2,1)}, bf16[32,24,512]{2,1,0:T(8,128)(2,1)}) fusion(bf16[128,24,512]{2,1,0:T(8,128)(2,1)} %own_ref.1), kind=kLoop, calls=%fused_computation.31 | loop fusion | bytes 3145728 | tf_op jit(solution)/shard_map/slice | solution.py:145
  2.8 0.0 collective-permute-start.2
  2.8 5.8 %collective-permute-start.3 = (bf16[32,24,512]{2,1,0:T(8,128)(2,1)}, bf16[32,24,512]{2,1,0:T(8,128)(2,1)}, u32[]{:S(2)}, u32[]{:S(2)}) collective-permute-start(bf16[32,24,512]{2,1,0:T(8,128)(2,1)} %get-tuple-element.5), channel_id=1, source_target_pairs={{0,252},{4,0},{8,4},{12,8},{16,12},{20,16},{24,20},{28,24},{32,28}... | collective-permute-start | bytes 2359304 | tf_op jit(solution)/shard_map/ppermute | solution.py:20
  8.6 0.0 copy-done.1
  8.6 0.1 fusion.11
  8.6 0.7 %collective-permute-start.1 = (s32[32,8]{0,1:T(8,128)S(1)}, s32[32,8]{0,1:T(8,128)S(1)}, u32[]{:S(2)}, u32[]{:S(2)}) collective-permute-start(s32[32,8]{0,1:T(8,128)S(1)} %get-tuple-element.14), channel_id=1, source_target_pairs={{0,252},{4,0},{8,4},{12,8},{16,12},{20,16},{24,20},{28,24},{32,28}... | collective-permute-start | bytes 3080 | tf_op jit(solution)/shard_map/ppermute | solution.py:20
  9.3 0.0 collective-permute-start
  9.3 0.0 copy-done.2
  9.4 0.1 copy.6
  9.5 0.1 reshape.8.jloc_ref
  9.6 8.8 %collective-permute-done.1 = s32[32,8]{0,1:T(8,128)S(1)} collective-permute-done((s32[32,8]{0,1:T(8,128)S(1)}, s32[32,8]{0,1:T(8,128)S(1)}, u32[]{:S(2)}, u32[]{:S(2)}) %collective-permute-start.1) | collective-permute-done | bytes 1056 | tf_op jit(solution)/shard_map/ppermute | solution.py:20
  18.4 0.1 collective-permute-done
  18.5 0.1 pad_add_fusion
  18.6 0.1 copy.5
  18.7 0.1 concatenate.6
  18.8 0.0 collective-permute-done.2.lower_ref
  18.8 0.0 collective-permute-done.3.upper_ref
  18.8 0.0 copy-done
  18.9 23.7 %shard_map.46 = f32[288,480]{1,0:T(8,128)S(1)} custom-call(s32[1536]{0:T(1024)S(1)} %fusion.6.wpos_ref, s32[256]{0:T(256)S(1)} %reshape.8.jloc_ref, bf16[32,24,512]{2,1,0:T(8,128)(2,1)S(1)} %collective-permute-done.2.lower_ref, bf16[128,24,512]{2,1,0:T(8,128)(2,1)} %own_ref.1, bf16[32,24,512]{2,1,0:T(8,128)(2,1)} %collective-permute-done.3.upper_ref, ...), custom_call_target="tpu_custom_call" | custom-call | flops 8556380160 | bytes 7368704 | tf_op jit(solution)/shard_map/pallas_call | solution.py:106
  42.6 3.3 %collective-permute-start.6 = (f32[3,24,480]{2,1,0:T(8,128)S(1)}, f32[3,24,480]{2,1,0:T(8,128)S(1)}, u32[]{:S(2)}, u32[]{:S(2)}) collective-permute-start(f32[3,24,480]{2,1,0:T(8,128)S(1)} %get-tuple-element.8), channel_id=1, source_target_pairs={{0,2},{1,3},{2,0},{3,1},{4,6},{5,7},{6,4},{7,5},{8,10},{9,11},{10,... | collective-permute-start | bytes 414728 | tf_op jit(solution)/shard_map/ppermute | solution.py:20
  45.9 1.1 %collective-permute-start.5 = (f32[3,24,480]{2,1,0:T(8,128)S(1)}, f32[3,24,480]{2,1,0:T(8,128)S(1)}, u32[]{:S(2)}, u32[]{:S(2)}) collective-permute-start(f32[3,24,480]{2,1,0:T(8,128)S(1)} %get-tuple-element.9), channel_id=1, source_target_pairs={{0,3},{1,0},{2,1},{3,2},{4,7},{5,4},{6,5},{7,6},{8,11},{9,8},{10,9... | collective-permute-start | bytes 414728 | tf_op jit(solution)/shard_map/ppermute | solution.py:20
  46.9 1.0 %collective-permute-start.4 = (f32[3,24,480]{2,1,0:T(8,128)S(1)}, f32[3,24,480]{2,1,0:T(8,128)S(1)}, u32[]{:S(2)}, u32[]{:S(2)}) collective-permute-start(f32[3,24,480]{2,1,0:T(8,128)S(1)} %get-tuple-element.7), channel_id=1, source_target_pairs={{0,1},{1,2},{2,3},{3,0},{4,5},{5,6},{6,7},{7,4},{8,9},{9,10},{10,1... | collective-permute-start | bytes 414728 | tf_op jit(solution)/shard_map/ppermute | solution.py:20
  47.9 1.5 %collective-permute-done.6 = f32[3,24,480]{2,1,0:T(8,128)S(1)} collective-permute-done((f32[3,24,480]{2,1,0:T(8,128)S(1)}, f32[3,24,480]{2,1,0:T(8,128)S(1)}, u32[]{:S(2)}, u32[]{:S(2)}) %collective-permute-start.6) | collective-permute-done | bytes 138272 | tf_op jit(solution)/shard_map/ppermute | solution.py:20
  49.5 1.8 %collective-permute-done.5 = f32[3,24,480]{2,1,0:T(8,128)S(1)} collective-permute-done((f32[3,24,480]{2,1,0:T(8,128)S(1)}, f32[3,24,480]{2,1,0:T(8,128)S(1)}, u32[]{:S(2)}, u32[]{:S(2)}) %collective-permute-start.5) | collective-permute-done | bytes 138272 | tf_op jit(solution)/shard_map/ppermute | solution.py:20
  51.2 2.1 %collective-permute-done.4 = f32[3,24,480]{2,1,0:T(8,128)S(1)} collective-permute-done((f32[3,24,480]{2,1,0:T(8,128)S(1)}, f32[3,24,480]{2,1,0:T(8,128)S(1)}, u32[]{:S(2)}, u32[]{:S(2)}) %collective-permute-start.4) | collective-permute-done | bytes 138272 | tf_op jit(solution)/shard_map/ppermute | solution.py:20
  53.4 4.1 %collective-permute-start.8 = (f32[24,480]{1,0:T(8,128)S(1)}, f32[24,480]{1,0:T(8,128)S(1)}, u32[]{:S(2)}, u32[]{:S(2)}) collective-permute-start(f32[24,480]{1,0:T(8,128)S(1)} %get-tuple-element.11), channel_id=1, source_target_pairs={{0,252},{4,0},{8,4},{12,8},{16,12},{20,16},{24,20},{28,24},{32,28}... | collective-permute-start | bytes 138248 | tf_op jit(solution)/shard_map/ppermute | solution.py:20
  57.4 0.0 collective-permute-start.7
  57.4 1.7 %collective-permute-done.8 = f32[24,480]{1,0:T(8,128)S(1)} collective-permute-done((f32[24,480]{1,0:T(8,128)S(1)}, f32[24,480]{1,0:T(8,128)S(1)}, u32[]{:S(2)}, u32[]{:S(2)}) %collective-permute-start.8) | collective-permute-done | bytes 46112 | tf_op jit(solution)/shard_map/ppermute | solution.py:20
  59.2 5.1 %collective-permute-done.7 = f32[24,480]{1,0:T(8,128)S(1)} collective-permute-done((f32[24,480]{1,0:T(8,128)S(1)}, f32[24,480]{1,0:T(8,128)S(1)}, u32[]{:S(2)}, u32[]{:S(2)}) %collective-permute-start.7) | collective-permute-done | bytes 46112 | tf_op jit(solution)/shard_map/ppermute | solution.py:20
  64.2 0.7 %add_bitcast_fusion = f32[1,24,672]{2,1,0:T(8,128)} fusion(f32[24,480]{1,0:T(8,128)S(1)} %collective-permute-done.8, f32[24,480]{1,0:T(8,128)S(1)} %collective-permute-done.7, f32[24,480]{1,0:T(8,128)S(1)} %get-tuple-element.10), kind=kLoop, calls=%fused_computation.6 | loop fusion | flops 32256 | bytes 202752 | tf_op jit(solution)/shard_map/broadcast_in_dim | solution.py:171
  (5 shorter events, 0.1 us)
Async XLA Ops:
  0.0 8.6 %copy-start.1 = (s32[128,8]{0,1:T(8,128)S(1)}, s32[128,8]{0,1:T(8,128)}, u32[]{:S(2)}) copy-start(s32[128,8]{0,1:T(8,128)} %param.7) | copy-start | bytes 12292
  0.0 9.3 %copy-start.2 = (s32[128,2]{0,1:T(2,128)S(1)}, s32[128,2]{0,1:T(2,128)}, u32[]{:S(2)}) copy-start(s32[128,2]{0,1:T(2,128)} %param.5) | copy-start | bytes 3076
  0.0 18.8 %copy-start = (bf16[128,64,128]{2,1,0:T(8,128)(2,1)S(1)}, bf16[128,64,128]{2,1,0:T(8,128)(2,1)}, u32[]{:S(2)}) copy-start(bf16[128,64,128]{2,1,0:T(8,128)(2,1)} %tb_ref.1) | copy-start | bytes 6291460
  2.8 16.0 %collective-permute-start.2 = (bf16[32,24,512]{2,1,0:T(8,128)(2,1)}, bf16[32,24,512]{2,1,0:T(8,128)(2,1)S(1)}, u32[]{:S(2)}, u32[]{:S(2)}) collective-permute-start(bf16[32,24,512]{2,1,0:T(8,128)(2,1)} %get-tuple-element.6), channel_id=1, source_target_pairs={{0,4},{4,8},{8,12},{12,16},{16,20},{20,24},{24,28},{28,32},{32,36}... | collective-permute-start | bytes 2359304 | tf_op jit(solution)/shard_map/ppermute | solution.py:20
  2.8 16.0 %collective-permute-start.3 = (bf16[32,24,512]{2,1,0:T(8,128)(2,1)}, bf16[32,24,512]{2,1,0:T(8,128)(2,1)}, u32[]{:S(2)}, u32[]{:S(2)}) collective-permute-start(bf16[32,24,512]{2,1,0:T(8,128)(2,1)} %get-tuple-element.5), channel_id=1, source_target_pairs={{0,252},{4,0},{8,4},{12,8},{16,12},{20,16},{24,20},{28,24},{32,28}... | collective-permute-start | bytes 2359304 | tf_op jit(solution)/shard_map/ppermute | solution.py:20
  8.6 9.7 %collective-permute-start.1 = (s32[32,8]{0,1:T(8,128)S(1)}, s32[32,8]{0,1:T(8,128)S(1)}, u32[]{:S(2)}, u32[]{:S(2)}) collective-permute-start(s32[32,8]{0,1:T(8,128)S(1)} %get-tuple-element.14), channel_id=1, source_target_pairs={{0,252},{4,0},{8,4},{12,8},{16,12},{20,16},{24,20},{28,24},{32,28}... | collective-permute-start | bytes 3080 | tf_op jit(solution)/shard_map/ppermute | solution.py:20
  9.3 9.2 %collective-permute-start = (s32[32,8]{0,1:T(8,128)S(1)}, s32[32,8]{0,1:T(8,128)S(1)}, u32[]{:S(2)}, u32[]{:S(2)}) collective-permute-start(s32[32,8]{0,1:T(8,128)S(1)} %get-tuple-element.13), channel_id=1, source_target_pairs={{0,4},{4,8},{8,12},{12,16},{16,20},{20,24},{24,28},{28,32},{32,36}... | collective-permute-start | bytes 3080 | tf_op jit(solution)/shard_map/ppermute | solution.py:20
  42.6 6.8 %collective-permute-start.6 = (f32[3,24,480]{2,1,0:T(8,128)S(1)}, f32[3,24,480]{2,1,0:T(8,128)S(1)}, u32[]{:S(2)}, u32[]{:S(2)}) collective-permute-start(f32[3,24,480]{2,1,0:T(8,128)S(1)} %get-tuple-element.8), channel_id=1, source_target_pairs={{0,2},{1,3},{2,0},{3,1},{4,6},{5,7},{6,4},{7,5},{8,10},{9,11},{10,... | collective-permute-start | bytes 414728 | tf_op jit(solution)/shard_map/ppermute | solution.py:20
  45.9 5.3 %collective-permute-start.5 = (f32[3,24,480]{2,1,0:T(8,128)S(1)}, f32[3,24,480]{2,1,0:T(8,128)S(1)}, u32[]{:S(2)}, u32[]{:S(2)}) collective-permute-start(f32[3,24,480]{2,1,0:T(8,128)S(1)} %get-tuple-element.9), channel_id=1, source_target_pairs={{0,3},{1,0},{2,1},{3,2},{4,7},{5,4},{6,5},{7,6},{8,11},{9,8},{10,9... | collective-permute-start | bytes 414728 | tf_op jit(solution)/shard_map/ppermute | solution.py:20
  46.9 6.4 %collective-permute-start.4 = (f32[3,24,480]{2,1,0:T(8,128)S(1)}, f32[3,24,480]{2,1,0:T(8,128)S(1)}, u32[]{:S(2)}, u32[]{:S(2)}) collective-permute-start(f32[3,24,480]{2,1,0:T(8,128)S(1)} %get-tuple-element.7), channel_id=1, source_target_pairs={{0,1},{1,2},{2,3},{3,0},{4,5},{5,6},{6,7},{7,4},{8,9},{9,10},{10,1... | collective-permute-start | bytes 414728 | tf_op jit(solution)/shard_map/ppermute | solution.py:20
  53.4 5.8 %collective-permute-start.8 = (f32[24,480]{1,0:T(8,128)S(1)}, f32[24,480]{1,0:T(8,128)S(1)}, u32[]{:S(2)}, u32[]{:S(2)}) collective-permute-start(f32[24,480]{1,0:T(8,128)S(1)} %get-tuple-element.11), channel_id=1, source_target_pairs={{0,252},{4,0},{8,4},{12,8},{16,12},{20,16},{24,20},{28,24},{32,28}... | collective-permute-start | bytes 138248 | tf_op jit(solution)/shard_map/ppermute | solution.py:20
  57.4 6.8 %collective-permute-start.7 = (f32[24,480]{1,0:T(8,128)S(1)}, f32[24,480]{1,0:T(8,128)S(1)}, u32[]{:S(2)}, u32[]{:S(2)}) collective-permute-start(f32[24,480]{1,0:T(8,128)S(1)} %get-tuple-element.12), channel_id=1, source_target_pairs={{0,4},{4,8},{8,12},{12,16},{16,20},{20,24},{24,28},{28,32},{32,36}... | collective-permute-start | bytes 138248 | tf_op jit(solution)/shard_map/ppermute | solution.py:20
